TPU v7x, 1024 devices: a whole 4x8x16 slice. The times are simulated.
1024 devices in a mesh: seq: 32 (over z, core), enc: 8 (over y), head: 4 (over x).
Axes of the slice: x: 4, y: 8, z: 16, core: 2. Of those that a mesh axis runs over, the one named last changes fastest.
Arguments:
- mel_frames: bfloat16 [65536, 128], P(('seq', 'enc')), may hold values from -6 to 6
- conv_weight: bfloat16 [384, 1280], replicated, may hold values from -0.3125 to 0.3125
- conv_bias: float32 [1280], replicated, may hold values from -3 to 3
- projector: bfloat16 [1280, 8, 1024], P(None, None, 'head'), may hold values from -0.15625 to 0.15625
- seg_offsets: int32 [64], replicated, may hold values from 0 to 65535, as said below
- seg_lengths: int32 [64], replicated, may hold values from 1 to 1535, as said below
- text_embed: bfloat16 [65536, 8192], P('seq', ('enc', 'head')), may hold values from -6 to 6
- mix_taps: float32 [4, 8192], P(None, ('enc', 'head')), may hold values from -3 to 3
- input_map: bfloat16 [65536, 1024], P('seq', 'enc'), may hold values from -1.796875 to 1.796875
- output_map: bfloat16 [65536, 1024], P('seq', 'enc'), may hold values from -1.796875 to 1.796875
- step_size: float32 [128, 65536], P(('enc', 'head'), 'seq'), may hold values from 0 to 2, as said below
- decay_log: float32 [128], P(('enc', 'head')), may hold values from -6 to -2
- skip_gain: float32 [128], P(('enc', 'head')), may hold values from 0.5 to 1.5
Outputs:
- mixer_out: bfloat16 [65536, 8192], P('seq', ('enc', 'head'))
Inputs may be any that keep to these rules, and one draw needn't show every extreme that they name: `seg_offsets`: offsets rise; owner k's two segments lie within positions k * 2048 to (k+1) * 2048 - 1 without intersection. Owner k's audio tokens are those of track indices within 256 of k * 1024 to (k+1) * 1024 - 1; in every draw some owner takes 256 tokens from each neighbour's share. `seg_lengths`: the lengths sum to 32768; an owner's two segments together hold between 512 and 1536 tokens. `step_size`: Positive.
All inputs are finite; a program needn't handle non-finite values.
Results may differ from a plain program's by a relative error of at most 0.006.
Values may be sent and summed in bfloat16 or wider, within the bound.
No kernel may reach another device: no remote copies, remote signals or barrier semaphores. Data moves between devices by JAX's collectives and lax.ppermute only.
A program may use at most 64 MiB of HBM per device.

v0:
```python
import jax
import jax.numpy as jnp
from jax import lax
from jax.sharding import PartitionSpec as P

HDIM = 64
SPAN = 128
DRIFT = 256


highest = lax.Precision.HIGHEST
high_mode = lax.Precision.HIGH


def from_behind(value, axis, by):
    count = lax.axis_size(axis)
    pairs = [(i, i + by) for i in range(count) if 0 <= i + by < count]
    return lax.ppermute(value, axis, pairs)


def padded_2(block, sides, width):
    for axis, dim in sides:
        count = lax.axis_size(axis)
        forward = [(i, i + 1) for i in range(count - 1)]
        backward = [(target, source) for source, target in forward]
        low = lax.ppermute(
            lax.slice_in_dim(block, block.shape[dim] - width, None, axis=dim), axis, forward
        )
        high = lax.ppermute(lax.slice_in_dim(block, 0, width, axis=dim), axis, backward)
        block = jnp.concatenate([low, block, high], axis=dim)
    return block


def entering(value, axis, join, neutral):
    place = lax.axis_index(axis)
    gathered = jax.tree.map(
        lambda a, kind: lax.all_gather(a.astype(kind), axis), value, (jnp.bfloat16, jnp.bfloat16)
    )
    state = jax.tree.map(lambda a, e: jnp.zeros_like(a) + jnp.asarray(e, a.dtype), value, neutral)

    def one(hop, state):
        return join(
            state,
            jax.tree.map(
                lambda a, own: lax.dynamic_index_in_dim(a, hop, 0, False).astype(own.dtype),
                gathered,
                value,
            ),
        )

    return lax.fori_loop(0, place, one, state)


def shards(
    mel_frames,
    conv_weight,
    conv_bias,
    projector,
    seg_offsets,
    seg_lengths,
    text_embed,
    mix_taps,
    input_map,
    output_map,
    step_size,
    decay_log,
    skip_gain,
):
    tiles = mel_frames.shape[0] // 2
    channels = mel_frames.shape[1]
    enc_count = lax.axis_size("enc")
    tile_first = (lax.axis_index("seq") * enc_count + lax.axis_index("enc")) * tiles
    seg_start = jnp.cumsum(seg_lengths) - seg_lengths
    frame_pairs = mel_frames.reshape(tiles, 2 * channels)
    edge_frame = from_behind(frame_pairs[-1:, channels:], ("seq", "enc"), 1)
    tokens = tile_first + jnp.arange(tiles, dtype=jnp.int32)
    opening = jnp.any(tokens[:, None] == seg_start[None, :], axis=1)
    left_frames = jnp.concatenate([edge_frame, frame_pairs[:-1, channels:]], axis=0)
    left_frames = jnp.where(opening[:, None], jnp.zeros_like(left_frames), left_frames)
    stacked = jnp.concatenate([left_frames, frame_pairs], axis=1)
    summed = jnp.dot(stacked, conv_weight, preferred_element_type=jnp.float32) + conv_bias
    features = jax.nn.gelu(summed, approximate=False).astype(jnp.bfloat16)
    column_width = projector.shape[2]
    projected = jnp.dot(
        features, projector.reshape(projector.shape[0], -1), preferred_element_type=jnp.float32
    )
    projected = projected.astype(jnp.bfloat16).reshape(tiles, enc_count, column_width)
    audio_rows = lax.all_to_all(projected, "enc", split_axis=1, concat_axis=0, tiled=True).reshape(
        tiles * enc_count, column_width
    )
    shard_audio = audio_rows.shape[0]
    widened = padded_2(audio_rows, (("seq", 0),), DRIFT)
    row_count = text_embed.shape[0]
    owner_index = lax.axis_index("seq")
    places = owner_index * row_count + jnp.arange(row_count, dtype=jnp.int32)
    segment = jnp.sum((places[:, None] >= seg_offsets[None, :]).astype(jnp.int32), axis=1) - 1
    chosen = jnp.arange(seg_offsets.shape[0], dtype=jnp.int32)[None, :] == segment[:, None]
    offset_here = jnp.sum(jnp.where(chosen, seg_offsets[None, :], 0), axis=1)
    length_here = jnp.sum(jnp.where(chosen, seg_lengths[None, :], 0), axis=1)
    start_here = jnp.sum(jnp.where(chosen, seg_start[None, :], 0), axis=1)
    within = places - offset_here
    is_audio = (segment >= 0) & (within < length_here)
    local_row = jnp.where(is_audio, start_here + within - owner_index * shard_audio + DRIFT, 0)
    x_raw = jnp.where(is_audio[:, None], jnp.take(widened, local_row, axis=0), text_embed)
    previous = from_behind(x_raw[-3:], "seq", 1)
    padded = jnp.concatenate([previous, x_raw], axis=0)
    summed_mix = jnp.zeros(x_raw.shape, jnp.float32)
    for offset in range(4):
        summed_mix = (
            summed_mix + padded[offset : offset + row_count].astype(jnp.float32) * mix_taps[offset]
        )
    mixed_in = jax.nn.silu(summed_mix).astype(jnp.bfloat16)
    head_count = step_size.shape[0]
    blocks = row_count // SPAN
    plain = mixed_in.reshape(blocks, SPAN, head_count, HDIM)
    values = plain.astype(jnp.float32)
    b_rows = input_map.reshape(blocks, SPAN, -1)
    c_rows = output_map.reshape(blocks, SPAN, -1)
    b_all = b_rows.astype(jnp.float32)
    c_all = c_rows.astype(jnp.float32)
    step_sizes = step_size.T.reshape(blocks, SPAN, head_count)
    log_decay = -step_sizes * jnp.exp(decay_log)[None, None, :]
    running = jnp.cumsum(log_decay, axis=1)
    lower_mask = (jnp.arange(SPAN)[:, None] >= jnp.arange(SPAN)[None, :])[None, :, :, None]
    gap_logs = running[:, :, None, :] - running[:, None, :, :]
    decay_table = jnp.where(lower_mask, jnp.exp(jnp.where(lower_mask, gap_logs, 0.0)), 0.0)
    intersection = jnp.einsum("cin,cjn->cij", c_rows, b_rows, preferred_element_type=jnp.float32)
    weight = (decay_table * intersection[..., None] * step_sizes[:, None, :, :]).astype(
        jnp.bfloat16
    )
    inner_part = jnp.einsum("cijh,cjhp->cihp", weight, plain, preferred_element_type=jnp.float32)
    inputs = values * step_sizes[..., None]
    tail_decay = jnp.exp(running[:, -1:, :] - running)
    block_states = jnp.einsum(
        "cjhp,cjn->chpn", inputs * tail_decay[..., None], b_all, precision=high_mode
    )
    totals = running[:, -1, :]
    through = jnp.cumsum(totals, axis=0)
    before_block = through - totals
    block_order = jnp.arange(blocks)
    earlier = (block_order[None, :] < block_order[:, None])[:, :, None]
    weights = jnp.where(
        earlier,
        jnp.exp(jnp.where(earlier, before_block[:, None, :] - through[None, :, :], 0.0)),
        0.0,
    )
    local_starts = jnp.einsum("cdh,dhpn->chpn", weights, block_states, precision=highest)
    device_total = through[-1]
    device_state = jnp.einsum(
        "dh,dhpn->hpn", jnp.exp(device_total[None, :] - through), block_states, precision=highest
    )

    def combine(earlier_part, later_part):
        return (
            earlier_part[0] + later_part[0],
            earlier_part[1] * jnp.exp(later_part[0])[:, None, None] + later_part[1],
        )

    identity = (jnp.zeros_like(device_total), jnp.zeros_like(device_state))
    passed_total, incoming = entering((device_total, device_state), "seq", combine, identity)
    block_in = local_starts + jnp.exp(before_block)[:, :, None, None] * incoming[None]
    carried = (
        jnp.einsum("cin,chpn->cihp", c_all, block_in, precision=high_mode)
        * jnp.exp(running)[..., None]
    )
    output = inner_part + carried + skip_gain[None, None, :, None] * values
    return output.reshape(row_count, head_count * HDIM).astype(jnp.bfloat16)


def solution(mesh):
    return jax.shard_map(
        shards,
        mesh=mesh,
        in_specs=(
            P(("seq", "enc"), None),
            P(),
            P(),
            P(None, None, "head"),
            P(),
            P(),
            P("seq", ("enc", "head")),
            P(None, ("enc", "head")),
            P("seq", "enc"),
            P("seq", "enc"),
            P(("enc", "head"), "seq"),
            P(("enc", "head")),
            P(("enc", "head")),
        ),
        out_specs=P("seq", ("enc", "head")),
        check_vma=False,
    )
```

profile of v0, /device:TPU:961, one launch (start us, length us, event | category | flops | bytes accessed | tf_op | source)
XLA Modules:
  0.0 208.1 jit_solution(15659310659934404497)
XLA Ops:
  7.5 3.2 %collective-permute-start = (bf16[1,128]{1,0:T(2,128)(2,1)S(1)}, bf16[1,128]{1,0:T(2,128)(2,1)S(1)}, u32[]{:S(2)}, u32[]{:S(2)}) collective-permute-start(bf16[1,128]{1,0:T(2,128)(2,1)S(1)} %slice.67), channel_id=1, source_target_pairs={{0,4},{4,8},{8,12},{12,16},{16,20},{20,24},{24,28},{28,32},{32,36}... | collective-permute-start | bytes 776 | tf_op jit(solution)/shard_map/ppermute | solution.py:18
  16.0 7.1 %copy.151 = bf16[160,8,8,256]{3,1,2,0:T(8,128)(2,1)} copy(bf16[160,8,8,256]{3,2,1,0:T(8,128)(2,1)} %bitcast.91) | data formatting | bytes 10485760
  23.2 4.9 %convolution_convert_fusion = bf16[128,2048]{1,0:T(8,128)(2,1)S(1)} fusion(bf16[1280,2048]{1,0:T(8,128)(2,1)} %bitcast.92, bf16[384,1280]{1,0:T(8,128)(2,1)S(1)} %copy-done, f32[1280]{0:T(1024)S(1)} %copy-done.11, bf16[128,256]{1,0:T(8,128)(2,1)S(1)} %reshape.210, bf16[128,128]{1,0:T(8,128)(2,1)S(1)} %maximum_select_fusion), kind=kOutput, calls=%fused_computation.7 | convolution fusion | flops 808189952 | bytes 6853632 | tf_op jit(solution)/shard_map/dot_general | solution.py:84
  28.9 5.9 %all-to-all-start = ((bf16[128,8,256]{2,0,1:T(8,128)(2,1)}), bf16[128,8,256]{2,0,1:T(8,128)(2,1)}, u32[]{:S(2)}, u32[]{:S(2)}) async-start(bf16[128,8,256]{2,0,1:T(8,128)(2,1)} %bitcast.85), calls=%async_computation | async-start | bytes 1048576 | tf_op jit(solution)/shard_map/all_to_all | solution.py:88
  36.2 15.8 %all-to-all-done = bf16[128,8,256]{2,0,1:T(8,128)(2,1)} async-done(((bf16[128,8,256]{2,0,1:T(8,128)(2,1)}), bf16[128,8,256]{2,0,1:T(8,128)(2,1)}, u32[]{:S(2)}, u32[]{:S(2)}) %all-to-all-start) | async-done | bytes 524320 | tf_op jit(solution)/shard_map/all_to_all | solution.py:88
  54.3 3.9 %collective-permute-start.2 = (bf16[256,256]{1,0:T(8,128)(2,1)S(1)}, bf16[256,256]{1,0:T(8,128)(2,1)S(1)}, u32[]{:S(2)}, u32[]{:S(2)}) collective-permute-start(bf16[256,256]{1,0:T(8,128)(2,1)S(1)} %bitcast.103), channel_id=1, source_target_pairs={{32,0},{64,32},{96,64},{128,96},{160,128},{192,160},{224,192},{256... | collective-permute-start | bytes 393224 | tf_op jit(solution)/shard_map/ppermute | solution.py:29
  60.3 9.1 %gather_fusion = bf16[2048,256]{1,0:T(8,128)(2,1)} fusion(bf16[1536,256]{1,0:T(8,128)(2,1)S(1)} %pad_maximum_fusion.1, s32[2048]{0:T(1024)S(1)} %broadcast_clamp_fusion), kind=kCustom, calls=%fused_computation | custom fusion | bytes 2105344 | tf_op jit(solution)/shard_map/jit(_take)/gather | solution.py:104
  69.3 3.1 %select_select_fusion = bf16[2048,256]{1,0:T(8,128)(2,1)S(1)} fusion(bf16[2048,256]{1,0:T(8,128)(2,1)} %param.21, bf16[2048,256]{1,0:T(8,128)(2,1)} %gather_fusion, pred[2048]{0:T(1024)(128)(4,1)S(1)} %get-tuple-element.88, pred[2048]{0:T(1024)(128)(4,1)S(1)} %get-tuple-element.89), kind=kLoop, calls=%fused_computation.40 | loop fusion | flops 1048576 | bytes 3149824 | tf_op jit(solution)/shard_map/jit(_where)/select_n | solution.py:104
  74.5 3.8 %collective-permute-done.3 = bf16[3,256]{1,0:T(4,128)(2,1)S(1)} collective-permute-done((bf16[3,256]{1,0:T(4,128)(2,1)S(1)}, bf16[3,256]{1,0:T(4,128)(2,1)S(1)}, u32[]{:S(2)}, u32[]{:S(2)}) %collective-permute-start.3) | collective-permute-done | bytes 1568 | tf_op jit(solution)/shard_map/ppermute | solution.py:18
  78.3 2.3 %multiply_convert_fusion.2 = bf16[2048,256]{1,0:T(8,128)(2,1)} fusion(bf16[2048,256]{1,0:T(8,128)(2,1)S(1)} %select_select_fusion, bf16[3,256]{1,0:T(4,128)(2,1)S(1)} %collective-permute-done.3, f32[256]{0:T(256)S(1)} %bitcast.113, f32[256]{0:T(256)S(1)} %bitcast.114, f32[256]{0:T(256)S(1)} %bitcast.112, f32[256]{0:T(256)S(1)} %bitcast.111), kind=kLoop, calls=%fused_computation.23 | loop fusion | flops 13107200 | bytes 2102784 | tf_op jit(solution)/shard_map/convert_element_type | solution.py:112
  80.6 3.3 %reshape.236 = bf16[16,128,4,64]{3,2,1,0:T(4,128)(2,1)S(1)} reshape(bf16[2048,256]{1,0:T(8,128)(2,1)} %multiply_convert_fusion.2) | data formatting | bytes 2097152 | tf_op jit(solution)/shard_map/reshape | solution.py:115
  83.9 2.1 %copy.122 = bf16[16,128,4,64]{1,3,2,0:T(8,128)(2,1)} copy(bf16[16,128,4,64]{3,2,1,0:T(4,128)(2,1)S(1)} %reshape.236) | data formatting | bytes 2097152 | tf_op jit(solution)/shard_map/reshape | solution.py:115
  86.1 2.1 %fusion.2 = f32[16,4,64,128]{3,2,1,0:T(8,128)S(1)} fusion(bf16[16,128,128,1]{2,1,3,0:T(8,128)(2,1)} %bitcast.93, bf16[16,128,4,64]{1,3,2,0:T(8,128)(2,1)} %copy.122, f32[16,128,4]{1,2,0:T(4,128)S(1)} %copy.127, f32[16,128,4]{1,2,0:T(4,128)S(1)} %bitcast.100), kind=kOutput, calls=%fused_computation.10 | convolution fusion | flops 404226048 | bytes 3735552 | tf_op jit(solution)/shard_map/cjhp,cjn->chpn/dot_general | solution.py:134
  88.2 2.2 %fusion.15 = f32[4,1,64,128]{3,1,2,0:T(1,128)S(1)} fusion(f32[16,4,1,1]{0,2,3,1:T(1,128)S(1)} %copy.142, f32[16,4,64,128]{3,2,1,0:T(8,128)S(1)} %fusion.2), kind=kOutput, calls=%fused_computation.25 | convolution fusion | flops 6291456 | bytes 2228480 | tf_op jit(solution)/shard_map/dh,dhpn->hpn/dot_general | solution.py:149
  92.8 29.9 %all-gather.1 = bf16[32,1,4]{2,1,0:T(2,128)(2,1)S(1)} all-gather(bf16[1,1,4]{2,1,0:T(2,128)(2,1)S(1)} %convert_bitcast_fusion), channel_id=1, replica_groups=mesh['seq'=32,'enc'=8,'head'=4] {'seq'}, dimensions={0}, use_global_device_ids=true | all-gather | bytes 264 | tf_op jit(solution)/shard_map/all_gather | solution.py:37
  123.0 1.6 copy.137
  124.7 1.8 fusion.125
  126.5 3.3 %fusion = f32[16,4,64,128]{3,2,1,0:T(8,128)} fusion(bf16[16,128,4,64]{1,3,2,0:T(8,128)(2,1)S(1)} %copy-done.2, f32[16,128,4]{1,2,0:T(4,128)S(1)} %bitcast.101, f32[16,128,128]{2,1,0:T(8,128)S(1)} %fusion.125, f32[16,128,4]{1,2,0:T(4,128)S(1)} %copy.119, pred[128,128]{1,0:T(8,128)(4,1)S(1)} %iota_compare_fusion.1), kind=kOutput, calls=%fused_computation.8 | convolution fusion | flops 140509184 | bytes 4276224 | tf_op jit(solution)/shard_map/cijh,cjhp->cihp/dot_general | solution.py:131
  129.8 29.9 %all-gather.4.cloned.1.call-done = bf16[128,64,128]{2,1,0:T(8,128)(2,1)} async-done(((bf16[4,64,128]{2,1,0:T(8,128)(2,1)}), bf16[128,64,128]{2,1,0:T(8,128)(2,1)}) %all-gather.4.cloned.1.call-update) | async-done | bytes 2097168 | tf_op jit(solution)/shard_map/all_gather | solution.py:37
  159.7 30.6 %while.12 = (s32[]{:T(128)}, f32[4,64,128]{2,1,0:T(8,128)S(1)}, s32[]{:T(128)}, bf16[32,4]{1,0:T(8,128)(2,1)S(1)}, bf16[32,4,64,128]{3,2,1,0:T(8,128)(2,1)}, /*index=5*/s32[]{:T(128)}, s32[]{:T(128)}, s32[]{:T(128)}) while((s32[]{:T(128)}, f32[4,64,128]{2,1,0:T(8,128)S(1)}, s32[]{:T(128)}, bf16[32,4]{1,0:T(8,128)(2,1)S(1)}, ...), condition=%wide.region_9.10_spmd, body=%wide.region_8.9_spmd.sunk | while | flops 98313 | bytes 327847 | solution.py:51
  190.3 3.2 %bitcast_add_fusion = f32[16,4,64,128]{3,0,2,1:T(8,128)S(1)} fusion(f32[16,4,64,128]{3,2,1,0:T(8,128)S(1)} %fusion.2, f32[4,64,128]{2,1,0:T(8,128)S(1)} %get-tuple-element.49, f32[16,4]{0,1:T(4,128)S(1)} %copy.133, f32[16,4]{0,1:T(4,128)S(1)} %copy.129, f32[16,4]{0,1:T(4,128)S(1)} %fusion.87, pred[16,16]{1,0:T(8,128)(4,1)S(1)} %iota_compare_fusion.2), kind=kOutput, calls=%fused_computation.15 | convolution fusion | flops 101714944 | bytes 4326400 | tf_op jit(solution)/shard_map/cdh,dhpn->chpn/dot_general | solution.py:147
  193.6 2.6 %fusion.5 = bf16[16,128,4,64]{1,3,2,0:T(8,128)(2,1)} fusion(bf16[16,128,4,64]{1,3,2,0:T(8,128)(2,1)S(1)} %copy-done.3, f32[16,4,64,128]{3,2,1,0:T(8,128)S(1)} %copy-done.4, bf16[16,128,128,1]{2,1,3,0:T(8,128)(2,1)S(1)} %bitcast.96, f32[16,4,64,128]{3,0,2,1:T(8,128)S(1)} %bitcast_add_fusion, f32[4]{0:T(128)S(1)} %copy-done.10, f32[16,128,4]{1,2,0:T(4,128)S(1)} %copy.137), kind=kOutput, calls=%fused_computation.12 | convolution fusion | flops 405798912 | bytes 6848528 | tf_op jit(solution)/shard_map/cin,chpn->cihp/dot_general | solution.py:163
  196.2 2.9 %copy.145 = bf16[16,128,4,64]{3,2,1,0:T(4,128)(2,1)S(1)} copy(bf16[16,128,4,64]{1,3,2,0:T(8,128)(2,1)} %fusion.5) | data formatting | bytes 2097152 | tf_op jit(solution)/shard_map/convert_element_type | solution.py:167
  199.1 2.2 %reshape.235 = bf16[2048,256]{1,0:T(8,128)(2,1)} reshape(bf16[16,128,4,64]{3,2,1,0:T(4,128)(2,1)S(1)} %copy.145) | data formatting | bytes 2097152 | tf_op jit(solution)/shard_map/convert_element_type | solution.py:167
  (139 shorter events, 46.7 us)
Async XLA Ops:
  6.5 16.6 %copy-start = (bf16[384,1280]{1,0:T(8,128)(2,1)S(1)}, bf16[384,1280]{1,0:T(8,128)(2,1)}, u32[]{:S(2)}) copy-start(bf16[384,1280]{1,0:T(8,128)(2,1)} %param.16) | copy-start | bytes 2949124
  6.5 9.0 %copy-start.9 = (s32[64]{0:T(128)S(1)}, s32[64]{0:T(128)}, u32[]{:S(2)}) copy-start(s32[64]{0:T(128)} %param.19) | copy-start | bytes 772
  6.5 9.0 %copy-start.8 = (s32[64]{0:T(128)S(1)}, s32[64]{0:T(128)}, u32[]{:S(2)}) copy-start(s32[64]{0:T(128)} %param.20) | copy-start | bytes 772
  7.5 15.5 %collective-permute-start = (bf16[1,128]{1,0:T(2,128)(2,1)S(1)}, bf16[1,128]{1,0:T(2,128)(2,1)S(1)}, u32[]{:S(2)}, u32[]{:S(2)}) collective-permute-start(bf16[1,128]{1,0:T(2,128)(2,1)S(1)} %slice.67), channel_id=1, source_target_pairs={{0,4},{4,8},{8,12},{12,16},{16,20},{20,24},{24,28},{28,32},{32,36}... | collective-permute-start | bytes 776 | tf_op jit(solution)/shard_map/ppermute | solution.py:18
  15.3 19.6 %copy-start.1 = (f32[16,128,4]{2,0,1:T(8,128)}, f32[16,128,4]{2,0,1:T(8,128)S(1)}, u32[]{:S(2)}) copy-start(f32[16,128,4]{2,0,1:T(8,128)S(1)} %fusion.27) | copy-start | bytes 98308
  16.0 7.2 %copy-start.11 = (f32[1280]{0:T(1024)S(1)}, f32[1280]{0:T(1024)}, u32[]{:S(2)}) copy-start(f32[1280]{0:T(1024)} %param.17) | copy-start | bytes 15364
  28.9 23.1 %all-to-all-start = ((bf16[128,8,256]{2,0,1:T(8,128)(2,1)}), bf16[128,8,256]{2,0,1:T(8,128)(2,1)}, u32[]{:S(2)}, u32[]{:S(2)}) async-start(bf16[128,8,256]{2,0,1:T(8,128)(2,1)} %bitcast.85), calls=%async_computation | async-start | bytes 1048576 | tf_op jit(solution)/shard_map/all_to_all | solution.py:88
  34.8 124.9 %all-gather.4.cloned.1.call-start = ((), (), s32[]{:S(2)}) async-start(), calls=%async_computation.1 | async-start | bytes 2162688 | tf_op jit(solution)/shard_map/all_gather | solution.py:37
  53.0 5.3 %collective-permute-start.1 = (bf16[256,256]{1,0:T(8,128)(2,1)S(1)}, bf16[256,256]{1,0:T(8,128)(2,1)S(1)}, u32[]{:S(2)}, u32[]{:S(2)}) collective-permute-start(bf16[256,256]{1,0:T(8,128)(2,1)S(1)} %bitcast.104), channel_id=1, source_target_pairs={{0,32},{32,64},{64,96},{96,128},{128,160},{160,192},{192,224},{224... | collective-permute-start | bytes 393224 | tf_op jit(solution)/shard_map/ppermute | solution.py:26
  54.3 4.9 %collective-permute-start.2 = (bf16[256,256]{1,0:T(8,128)(2,1)S(1)}, bf16[256,256]{1,0:T(8,128)(2,1)S(1)}, u32[]{:S(2)}, u32[]{:S(2)}) collective-permute-start(bf16[256,256]{1,0:T(8,128)(2,1)S(1)} %bitcast.103), channel_id=1, source_target_pairs={{32,0},{64,32},{96,64},{128,96},{160,128},{192,160},{224,192},{256... | collective-permute-start | bytes 393224 | tf_op jit(solution)/shard_map/ppermute | solution.py:29
  69.3 4.7 %copy-start.7 = (f32[4,256]{1,0:T(4,128)S(1)}, f32[4,256]{1,0:T(4,128)}, u32[]{:S(2)}) copy-start(f32[4,256]{1,0:T(4,128)} %param.22) | copy-start | bytes 12292
  72.5 5.8 %collective-permute-start.3 = (bf16[3,256]{1,0:T(4,128)(2,1)S(1)}, bf16[3,256]{1,0:T(4,128)(2,1)S(1)}, u32[]{:S(2)}, u32[]{:S(2)}) collective-permute-start(bf16[3,256]{1,0:T(4,128)(2,1)S(1)} %slice.71), channel_id=1, source_target_pairs={{0,32},{32,64},{64,96},{96,128},{128,160},{160,192},{192,224},{224... | collective-permute-start | bytes 4616 | tf_op jit(solution)/shard_map/ppermute | solution.py:18
  83.9 2.2 %copy-start.6 = (f32[4,2048]{1,0:T(4,128)S(1)}, f32[4,2048]{1,0:T(4,128)}, u32[]{:S(2)}) copy-start(f32[4,2048]{1,0:T(4,128)} %param.25) | copy-start | bytes 98308
  124.7 1.8 copy-start.2
  190.3 3.2 %copy-start.3 = (bf16[16,128,4,64]{1,3,2,0:T(8,128)(2,1)S(1)}, bf16[16,128,4,64]{1,3,2,0:T(8,128)(2,1)}, u32[]{:S(2)}) copy-start(bf16[16,128,4,64]{1,3,2,0:T(8,128)(2,1)} %copy.122) | copy-start | bytes 3145732
  190.3 3.2 %copy-start.4 = (f32[16,4,64,128]{3,2,1,0:T(8,128)S(1)}, f32[16,4,64,128]{3,2,1,0:T(8,128)}, u32[]{:S(2)}) copy-start(f32[16,4,64,128]{3,2,1,0:T(8,128)} %fusion) | copy-start | bytes 6291460
  190.3 3.2 %copy-start.5 = (bf16[2048,128]{1,0:T(8,128)(2,1)S(1)}, bf16[2048,128]{1,0:T(8,128)(2,1)}, u32[]{:S(2)}) copy-start(bf16[2048,128]{1,0:T(8,128)(2,1)} %param.24) | copy-start | bytes 1572868
  190.3 3.2 %copy-start.10 = (f32[4]{0:T(128)S(1)}, f32[4]{0:T(128)}, u32[]{:S(2)}) copy-start(f32[4]{0:T(128)} %param.27) | copy-start | bytes 52
Sparse Core Ops, SparseCore 0:
  91.2 68.4 all-gather.3
where the time goes:
time: 210 us; the launch traced here: 208 us
  waiting for transfers between devices  50.4 us (24%)
  other arithmetic  40.1 us (19%)
  local copies, waits for them, and re-layouts  36.5 us (17%)
  blocking collectives  29.9 us (14%)
  matrix products  20.1 us (10%)
  starting transfers between devices  15.9 us (8%)
  between operations  13.8 us (7%)
    all_gather x1, blocking collectives, entering(): lax.all_gather(a.astype(kind), axis)  29.9 us
    all_gather x1, waiting for transfers between devices, entering(): lax.all_gather(a.astype(kind), axis)  29.9 us
    add x31, other arithmetic, combine(): earlier_part[1] * jnp.exp(later_part[0])[:, None, None] + later_part[1]  28.9 us
    all_to_all x1, waiting for transfers between devices, shards(): lax.all_to_all(projected, 'enc', split_axis=1, concat_axis=0, tiled=True)  15.8 us
    gather x1, local copies, waits for them, and re-layouts, shards(): jnp.take(widened, local_row, axis=0)  9.06 us
    unnamed x28, local copies, waits for them, and re-layouts  7.97 us
    all_to_all x1, starting transfers between devices, shards(): lax.all_to_all(projected, 'enc', split_axis=1, concat_axis=0, tiled=True)  5.92 us
    reshape x2, local copies, waits for them, and re-layouts, shards(): plain = mixed_in.reshape(blocks, SPAN, head_count, HDIM)  5.45 us
  transfers between devices with their start and end apart: 6, of which 4 were waited for; matrix products, arithmetic and copies ran while one was open for 11% of the time, Pallas kernels for 0%

commit v1 on v0

--- a/solution.py
+++ b/solution.py
@@ -31,24 +31,32 @@
     return block
 
 
-def entering(value, axis, join, neutral):
-    place = lax.axis_index(axis)
-    gathered = jax.tree.map(
-        lambda a, kind: lax.all_gather(a.astype(kind), axis), value, (jnp.bfloat16, jnp.bfloat16)
-    )
-    state = jax.tree.map(lambda a, e: jnp.zeros_like(a) + jnp.asarray(e, a.dtype), value, neutral)
+def prefix_windows(total, axis):
+    count = lax.axis_size(axis)
+    first = [d for d in (1, 2) if d < count]
+    window = jnp.zeros_like(total)
+    for d in first:
+        window = window + from_behind(total, axis, d)
+    spans = []
+    width = len(first)
+    while width < count:
+        spans.append((width, window))
+        window = window + from_behind(window, axis, width)
+        width *= 2
+    return first, spans
 
-    def one(hop, state):
-        return join(
-            state,
-            jax.tree.map(
-                lambda a, own: lax.dynamic_index_in_dim(a, hop, 0, False).astype(own.dtype),
-                gathered,
-                value,
-            ),
-        )
 
-    return lax.fori_loop(0, place, one, state)
+def prefix_state(total, state, first, spans, axis):
+    incoming = jnp.zeros_like(state)
+    for d in first:
+        shifted = from_behind(state.astype(jnp.bfloat16), axis, d).astype(state.dtype)
+        if d == 2:
+            shifted = shifted * jnp.exp(from_behind(total, axis, 1))[:, None, None]
+        incoming = incoming + shifted
+    for width, window in spans:
+        earlier = from_behind(incoming.astype(jnp.bfloat16), axis, width).astype(state.dtype)
+        incoming = earlier * jnp.exp(window)[:, None, None] + incoming
+    return incoming
 
 
 def shards(
@@ -146,18 +154,12 @@
     )
     local_starts = jnp.einsum("cdh,dhpn->chpn", weights, block_states, precision=highest)
     device_total = through[-1]
+    first, spans = prefix_windows(device_total, "seq")
     device_state = jnp.einsum(
         "dh,dhpn->hpn", jnp.exp(device_total[None, :] - through), block_states, precision=highest
     )
 
-    def combine(earlier_part, later_part):
-        return (
-            earlier_part[0] + later_part[0],
-            earlier_part[1] * jnp.exp(later_part[0])[:, None, None] + later_part[1],
-        )
-
-    identity = (jnp.zeros_like(device_total), jnp.zeros_like(device_state))
-    passed_total, incoming = entering((device_total, device_state), "seq", combine, identity)
+    incoming = prefix_state(device_total, device_state, first, spans, "seq")
     block_in = local_starts + jnp.exp(before_block)[:, :, None, None] * incoming[None]
     carried = (
         jnp.einsum("cin,chpn->cihp", c_all, block_in, precision=high_mode)

time: 210 us -> 159 us (0.76)
  the two profiles are of different devices: /device:TPU:961 before, /device:TPU:6 now
where the time goes in v1:
time: 159 us; the launch traced here: 158 us
  starting transfers between devices  78.5 us (49%)
  local copies, waits for them, and re-layouts  33.1 us (21%)
  waiting for transfers between devices  20.3 us (13%)
  matrix products  18 us (11%)
  other arithmetic  8.07 us (5%)
    ppermute x13, starting transfers between devices, from_behind(): return lax.ppermute(value, axis, pairs)  68.9 us
    all_to_all x1, waiting for transfers between devices, shards(): lax.all_to_all(projected, 'enc', split_axis=1, concat_axis=0, tiled=True)  14.6 us
    gather x1, local copies, waits for them, and re-layouts, shards(): jnp.take(widened, local_row, axis=0)  9.06 us
    unnamed x27, local copies, waits for them, and re-layouts  8.04 us
    all_to_all x1, starting transfers between devices, shards(): lax.all_to_all(projected, 'enc', split_axis=1, concat_axis=0, tiled=True)  6.21 us
    convert_element_type x2, local copies, waits for them, and re-layouts, shards(): return output.reshape(row_count, head_count * HDIM).astype(jnp.bfloat16)  5.02 us
    dot_general x1, matrix products, shards(): jnp.dot(features, projector.reshape(projector.shape[0], -1), preferred_el...  4.91 us
    reshape x2, local copies, waits for them, and re-layouts, shards(): plain = mixed_in.reshape(blocks, SPAN, head_count, HDIM)  4.71 us
  transfers between devices with their start and end apart: 16, of which 3 were waited for; matrix products, arithmetic and copies ran while one was open for 29% of the time, Pallas kernels for 0%

profile of v1, /device:TPU:6, one launch (start us, length us, event | category | flops | bytes accessed | tf_op | source)
XLA Modules:
  0.0 158.5 jit_solution(3280242360340082667)
XLA Ops:
  4.2 4.5 %collective-permute-start.8 = (f32[4]{0:T(128)S(1)}, f32[4]{0:T(128)S(1)}, u32[]{:S(2)}, u32[]{:S(2)}) collective-permute-start(f32[4]{0:T(128)S(1)} %slice_bitcast_fusion), channel_id=1, source_target_pairs={{0,64},{32,96},{64,128},{96,160},{128,192},{160,224},{192,256},{22... | collective-permute-start | bytes 56 | tf_op jit(solution)/shard_map/ppermute | solution.py:18
  8.7 3.5 %collective-permute-start = (bf16[1,128]{1,0:T(2,128)(2,1)S(1)}, bf16[1,128]{1,0:T(2,128)(2,1)S(1)}, u32[]{:S(2)}, u32[]{:S(2)}) collective-permute-start(bf16[1,128]{1,0:T(2,128)(2,1)S(1)} %slice.67), channel_id=1, source_target_pairs={{0,4},{4,8},{8,12},{12,16},{16,20},{20,24},{24,28},{28,32},{32,36}... | collective-permute-start | bytes 776 | tf_op jit(solution)/shard_map/ppermute | solution.py:18
  13.3 7.1 %copy.141 = bf16[160,8,8,256]{3,1,2,0:T(8,128)(2,1)} copy(bf16[160,8,8,256]{3,2,1,0:T(8,128)(2,1)} %bitcast.80) | data formatting | bytes 10485760
  20.4 4.9 %convolution_convert_fusion = bf16[128,2048]{1,0:T(8,128)(2,1)S(1)} fusion(bf16[1280,2048]{1,0:T(8,128)(2,1)} %bitcast.81, bf16[384,1280]{1,0:T(8,128)(2,1)S(1)} %copy-done, f32[1280]{0:T(1024)S(1)} %copy-done.11, bf16[128,256]{1,0:T(8,128)(2,1)S(1)} %reshape.205, bf16[128,128]{1,0:T(8,128)(2,1)S(1)} %maximum_select_fusion), kind=kOutput, calls=%fused_computation.5 | convolution fusion | flops 808189952 | bytes 6853632 | tf_op jit(solution)/shard_map/dot_general | solution.py:92
  26.2 6.2 %all-to-all-start = ((bf16[128,8,256]{2,0,1:T(8,128)(2,1)}), bf16[128,8,256]{2,0,1:T(8,128)(2,1)S(1)}, u32[]{:S(2)}, u32[]{:S(2)}) async-start(bf16[128,8,256]{2,0,1:T(8,128)(2,1)} %bitcast.86), calls=%async_computation | async-start | bytes 1048576 | tf_op jit(solution)/shard_map/all_to_all | solution.py:96
  32.5 2.5 %fusion.134 = f32[16,128,128]{2,1,0:T(8,128)} fusion(bf16[16,128,128]{2,1,0:T(8,128)(2,1)} %bitcast.87, bf16[16,128,128]{2,1,0:T(8,128)(2,1)S(1)} %bitcast.84), kind=kOutput, calls=%fused_computation.178 | convolution fusion | flops 67108864 | bytes 2097152 | tf_op jit(solution)/shard_map/cin,cjn->cij/dot_general | solution.py:135
  36.6 14.6 %all-to-all-done = bf16[128,8,256]{2,0,1:T(8,128)(2,1)S(1)} async-done(((bf16[128,8,256]{2,0,1:T(8,128)(2,1)}), bf16[128,8,256]{2,0,1:T(8,128)(2,1)S(1)}, u32[]{:S(2)}, u32[]{:S(2)}) %all-to-all-start) | async-done | bytes 524320 | tf_op jit(solution)/shard_map/all_to_all | solution.py:96
  54.6 3.8 %collective-permute-done.2 = bf16[256,256]{1,0:T(8,128)(2,1)S(1)} collective-permute-done((bf16[256,256]{1,0:T(8,128)(2,1)S(1)}, bf16[256,256]{1,0:T(8,128)(2,1)S(1)}, u32[]{:S(2)}, u32[]{:S(2)}) %collective-permute-start.2) | collective-permute-done | bytes 131104 | tf_op jit(solution)/shard_map/ppermute | solution.py:29
  58.5 9.1 %gather_fusion = bf16[2048,256]{1,0:T(8,128)(2,1)} fusion(bf16[1536,256]{1,0:T(8,128)(2,1)S(1)} %pad_maximum_fusion.1, s32[2048]{0:T(1024)S(1)} %broadcast_clamp_fusion), kind=kCustom, calls=%fused_computation | custom fusion | bytes 2105344 | tf_op jit(solution)/shard_map/jit(_take)/gather | solution.py:112
  67.5 3.1 %select_select_fusion = bf16[2048,256]{1,0:T(8,128)(2,1)S(1)} fusion(bf16[2048,256]{1,0:T(8,128)(2,1)} %param.19, bf16[2048,256]{1,0:T(8,128)(2,1)} %gather_fusion, pred[2048]{0:T(1024)(128)(4,1)S(1)} %get-tuple-element.14, pred[2048]{0:T(1024)(128)(4,1)S(1)} %get-tuple-element.15), kind=kLoop, calls=%fused_computation.38 | loop fusion | flops 1048576 | bytes 3149824 | tf_op jit(solution)/shard_map/jit(_where)/select_n | solution.py:112
  70.7 5.6 %collective-permute-start.3 = (bf16[3,256]{1,0:T(4,128)(2,1)S(1)}, bf16[3,256]{1,0:T(4,128)(2,1)S(1)}, u32[]{:S(2)}, u32[]{:S(2)}) collective-permute-start(bf16[3,256]{1,0:T(4,128)(2,1)S(1)} %slice.71), channel_id=1, source_target_pairs={{0,32},{32,64},{64,96},{96,128},{128,160},{160,192},{192,224},{224... | collective-permute-start | bytes 4616 | tf_op jit(solution)/shard_map/ppermute | solution.py:18
  83.5 2.9 %copy.114 = bf16[16,128,4,64]{1,3,2,0:T(8,128)(2,1)S(1)} copy(bf16[16,128,4,64]{3,2,1,0:T(4,128)(2,1)} %reshape.227) | data formatting | bytes 2097152 | tf_op jit(solution)/shard_map/reshape | solution.py:123
  87.3 2.2 %fusion.15 = f32[4,1,64,128]{3,1,2,0:T(1,128)S(1)} fusion(f32[16,4,1,1]{0,2,3,1:T(1,128)S(1)} %copy.132, f32[16,4,64,128]{3,2,1,0:T(8,128)S(1)} %fusion.2), kind=kOutput, calls=%fused_computation.23 | convolution fusion | flops 6291456 | bytes 2228480 | tf_op jit(solution)/shard_map/dh,dhpn->hpn/dot_general | solution.py:158
  91.5 4.4 %collective-permute-start.5 = (bf16[4,64,128]{2,1,0:T(8,128)(2,1)S(1)}, bf16[4,64,128]{2,1,0:T(8,128)(2,1)S(1)}, u32[]{:S(2)}, u32[]{:S(2)}) collective-permute-start(bf16[4,64,128]{2,1,0:T(8,128)(2,1)S(1)} %convert_element_type.82), channel_id=1, source_target_pairs={{0,64},{32,96},{64,128},{96,160},{128,192},{160,224},{192,256},{22... | collective-permute-start | bytes 196616 | tf_op jit(solution)/shard_map/ppermute | solution.py:18
  95.9 5.3 %collective-permute-start.10 = (f32[4]{0:T(128)S(1)}, f32[4]{0:T(128)S(1)}, u32[]{:S(2)}, u32[]{:S(2)}) collective-permute-start(f32[4]{0:T(128)S(1)} %get-tuple-element.11), channel_id=1, source_target_pairs={{0,64},{32,96},{64,128},{96,160},{128,192},{160,224},{192,256},{22... | collective-permute-start | bytes 56 | tf_op jit(solution)/shard_map/ppermute | solution.py:18
  101.4 5.5 %collective-permute-start.7 = (bf16[4,64,128]{2,1,0:T(8,128)(2,1)S(1)}, bf16[4,64,128]{2,1,0:T(8,128)(2,1)S(1)}, u32[]{:S(2)}, u32[]{:S(2)}) collective-permute-start(bf16[4,64,128]{2,1,0:T(8,128)(2,1)S(1)} %fusion.70), channel_id=1, source_target_pairs={{0,64},{32,96},{64,128},{96,160},{128,192},{160,224},{192,256},{22... | collective-permute-start | bytes 196616 | tf_op jit(solution)/shard_map/ppermute | solution.py:18
  106.9 4.9 %collective-permute-start.12 = (f32[4]{0:T(128)S(1)}, f32[4]{0:T(128)S(1)}, u32[]{:S(2)}, u32[]{:S(2)}) collective-permute-start(f32[4]{0:T(128)S(1)} %get-tuple-element.13), channel_id=1, source_target_pairs={{0,128},{32,160},{64,192},{96,224},{128,256},{160,288},{192,320},{... | collective-permute-start | bytes 56 | tf_op jit(solution)/shard_map/ppermute | solution.py:18
  112.0 7.5 %collective-permute-start.9 = (bf16[4,64,128]{2,1,0:T(8,128)(2,1)S(1)}, bf16[4,64,128]{2,1,0:T(8,128)(2,1)S(1)}, u32[]{:S(2)}, u32[]{:S(2)}) collective-permute-start(bf16[4,64,128]{2,1,0:T(8,128)(2,1)S(1)} %fusion.127), channel_id=1, source_target_pairs={{0,128},{32,160},{64,192},{96,224},{128,256},{160,288},{192,320},{... | collective-permute-start | bytes 196616 | tf_op jit(solution)/shard_map/ppermute | solution.py:18
  119.5 6.1 %collective-permute-start.14 = (f32[4]{0:T(128)S(1)}, f32[4]{0:T(128)S(1)}, u32[]{:S(2)}, u32[]{:S(2)}) collective-permute-start(f32[4]{0:T(128)S(1)} %get-tuple-element.9), channel_id=1, source_target_pairs={{0,256},{32,288},{64,320},{96,352},{128,384},{160,416},{192,448},{... | collective-permute-start | bytes 56 | tf_op jit(solution)/shard_map/ppermute | solution.py:18
  125.7 4.9 %collective-permute-start.11 = (bf16[4,64,128]{2,1,0:T(8,128)(2,1)S(1)}, bf16[4,64,128]{2,1,0:T(8,128)(2,1)S(1)}, u32[]{:S(2)}, u32[]{:S(2)}) collective-permute-start(bf16[4,64,128]{2,1,0:T(8,128)(2,1)S(1)} %fusion.77), channel_id=1, source_target_pairs={{0,256},{32,288},{64,320},{96,352},{128,384},{160,416},{192,448},{... | collective-permute-start | bytes 196616 | tf_op jit(solution)/shard_map/ppermute | solution.py:18
  132.7 13.0 %collective-permute-start.13 = (bf16[4,64,128]{2,1,0:T(8,128)(2,1)S(1)}, bf16[4,64,128]{2,1,0:T(8,128)(2,1)S(1)}, u32[]{:S(2)}, u32[]{:S(2)}) collective-permute-start(bf16[4,64,128]{2,1,0:T(8,128)(2,1)S(1)} %fusion.126), channel_id=1, source_target_pairs={{0,512},{32,544},{64,576},{96,608},{128,640},{160,672},{192,704},{... | collective-permute-start | bytes 196616 | tf_op jit(solution)/shard_map/ppermute | solution.py:18
  147.6 3.2 %bitcast_add_fusion = f32[16,4,64,128]{3,0,2,1:T(8,128)S(1)} fusion(f32[4,64,128]{2,1,0:T(8,128)S(1)} %multiply_add_fusion, f32[16,4]{0,1:T(4,128)S(1)} %copy.125, f32[16,4,64,128]{3,2,1,0:T(8,128)S(1)} %fusion.2, f32[16,4]{0,1:T(4,128)S(1)} %copy.121, f32[16,4]{0,1:T(4,128)S(1)} %fusion.91, pred[16,16]{1,0:T(8,128)(4,1)S(1)} %iota_compare_fusion.2), kind=kOutput, calls=%fused_computation.13 | convolution fusion | flops 101714944 | bytes 4326400 | tf_op jit(solution)/shard_map/cdh,dhpn->chpn/dot_general | solution.py:155
  150.8 2.6 %fusion.5 = bf16[16,128,4,64]{1,3,2,0:T(8,128)(2,1)} fusion(bf16[16,128,4,64]{1,3,2,0:T(8,128)(2,1)S(1)} %copy.114, f32[16,4,64,128]{3,2,1,0:T(8,128)S(1)} %fusion, bf16[16,128,128,1]{2,1,3,0:T(8,128)(2,1)S(1)} %bitcast.88, f32[16,4,64,128]{3,0,2,1:T(8,128)S(1)} %bitcast_add_fusion, f32[4]{0:T(128)S(1)} %copy-done.10, f32[16,128,4]{1,2,0:T(4,128)S(1)} %copy.127), kind=kOutput, calls=%fused_computation.10 | convolution fusion | flops 405798912 | bytes 6848528 | tf_op jit(solution)/shard_map/cin,chpn->cihp/dot_general | solution.py:165
  153.4 2.9 %copy.135 = bf16[16,128,4,64]{3,2,1,0:T(4,128)(2,1)S(1)} copy(bf16[16,128,4,64]{1,3,2,0:T(8,128)(2,1)} %fusion.5) | data formatting | bytes 2097152 | tf_op jit(solution)/shard_map/convert_element_type | solution.py:169
  (99 shorter events, 27.5 us)
Async XLA Ops:
  0.0 20.4 %copy-start = (bf16[384,1280]{1,0:T(8,128)(2,1)S(1)}, bf16[384,1280]{1,0:T(8,128)(2,1)}, u32[]{:S(2)}) copy-start(bf16[384,1280]{1,0:T(8,128)(2,1)} %param.14) | copy-start | bytes 2949124
  0.0 8.7 %copy-start.6 = (bf16[256,128]{1,0:T(8,128)(2,1)S(1)}, bf16[256,128]{1,0:T(8,128)(2,1)}, u32[]{:S(2)}) copy-start(bf16[256,128]{1,0:T(8,128)(2,1)} %param.13) | copy-start | bytes 196612
  0.0 12.2 %copy-start.9 = (s32[64]{0:T(128)S(1)}, s32[64]{0:T(128)}, u32[]{:S(2)}) copy-start(s32[64]{0:T(128)} %param.17) | copy-start | bytes 772
  0.0 12.4 %copy-start.8 = (s32[64]{0:T(128)S(1)}, s32[64]{0:T(128)}, u32[]{:S(2)}) copy-start(s32[64]{0:T(128)} %param.18) | copy-start | bytes 772
  2.5 93.4 %collective-permute-start.6 = (f32[4]{0:T(128)S(1)}, f32[4]{0:T(128)S(1)}, u32[]{:S(2)}, u32[]{:S(2)}) collective-permute-start(f32[4]{0:T(128)S(1)} %slice_bitcast_fusion), channel_id=1, source_target_pairs={{0,32},{32,64},{64,96},{96,128},{128,160},{160,192},{192,224},{224... | collective-permute-start | bytes 56 | tf_op jit(solution)/shard_map/ppermute | solution.py:18
  4.2 91.7 %collective-permute-start.8 = (f32[4]{0:T(128)S(1)}, f32[4]{0:T(128)S(1)}, u32[]{:S(2)}, u32[]{:S(2)}) collective-permute-start(f32[4]{0:T(128)S(1)} %slice_bitcast_fusion), channel_id=1, source_target_pairs={{0,64},{32,96},{64,128},{96,160},{128,192},{160,224},{192,256},{22... | collective-permute-start | bytes 56 | tf_op jit(solution)/shard_map/ppermute | solution.py:18
  8.7 11.6 %collective-permute-start = (bf16[1,128]{1,0:T(2,128)(2,1)S(1)}, bf16[1,128]{1,0:T(2,128)(2,1)S(1)}, u32[]{:S(2)}, u32[]{:S(2)}) collective-permute-start(bf16[1,128]{1,0:T(2,128)(2,1)S(1)} %slice.67), channel_id=1, source_target_pairs={{0,4},{4,8},{8,12},{12,16},{16,20},{20,24},{24,28},{28,32},{32,36}... | collective-permute-start | bytes 776 | tf_op jit(solution)/shard_map/ppermute | solution.py:18
  13.2 7.2 %copy-start.11 = (f32[1280]{0:T(1024)S(1)}, f32[1280]{0:T(1024)}, u32[]{:S(2)}) copy-start(f32[1280]{0:T(1024)} %param.15) | copy-start | bytes 15364
  25.3 7.1 %copy-start.7 = (f32[4,256]{1,0:T(4,128)S(1)}, f32[4,256]{1,0:T(4,128)}, u32[]{:S(2)}) copy-start(f32[4,256]{1,0:T(4,128)} %param.20) | copy-start | bytes 12292
  25.4 7.2 %copy-start.1 = (bf16[2048,128]{1,0:T(8,128)(2,1)S(1)}, bf16[2048,128]{1,0:T(8,128)(2,1)}, u32[]{:S(2)}) copy-start(bf16[2048,128]{1,0:T(8,128)(2,1)} %param.21) | copy-start | bytes 1572868
  26.2 25.1 %all-to-all-start = ((bf16[128,8,256]{2,0,1:T(8,128)(2,1)}), bf16[128,8,256]{2,0,1:T(8,128)(2,1)S(1)}, u32[]{:S(2)}, u32[]{:S(2)}) async-start(bf16[128,8,256]{2,0,1:T(8,128)(2,1)} %bitcast.86), calls=%async_computation | async-start | bytes 1048576 | tf_op jit(solution)/shard_map/all_to_all | solution.py:96
  51.3 3.4 %collective-permute-start.1 = (bf16[256,256]{1,0:T(8,128)(2,1)S(1)}, bf16[256,256]{1,0:T(8,128)(2,1)S(1)}, u32[]{:S(2)}, u32[]{:S(2)}) collective-permute-start(bf16[256,256]{1,0:T(8,128)(2,1)S(1)} %bitcast.96), channel_id=1, source_target_pairs={{0,32},{32,64},{64,96},{96,128},{128,160},{160,192},{192,224},{224... | collective-permute-start | bytes 393224 | tf_op jit(solution)/shard_map/ppermute | solution.py:26
  53.3 5.1 %collective-permute-start.2 = (bf16[256,256]{1,0:T(8,128)(2,1)S(1)}, bf16[256,256]{1,0:T(8,128)(2,1)S(1)}, u32[]{:S(2)}, u32[]{:S(2)}) collective-permute-start(bf16[256,256]{1,0:T(8,128)(2,1)S(1)} %bitcast.95), channel_id=1, source_target_pairs={{32,0},{64,32},{96,64},{128,96},{160,128},{192,160},{224,192},{256... | collective-permute-start | bytes 393224 | tf_op jit(solution)/shard_map/ppermute | solution.py:29
  70.7 9.5 %collective-permute-start.3 = (bf16[3,256]{1,0:T(4,128)(2,1)S(1)}, bf16[3,256]{1,0:T(4,128)(2,1)S(1)}, u32[]{:S(2)}, u32[]{:S(2)}) collective-permute-start(bf16[3,256]{1,0:T(4,128)(2,1)S(1)} %slice.71), channel_id=1, source_target_pairs={{0,32},{32,64},{64,96},{96,128},{128,160},{160,192},{192,224},{224... | collective-permute-start | bytes 4616 | tf_op jit(solution)/shard_map/ppermute | solution.py:18
  87.3 58.5 %copy-start.4 = (f32[16,128,128]{2,1,0:T(8,128)S(1)}, f32[16,128,128]{2,1,0:T(8,128)}, u32[]{:S(2)}) copy-start(f32[16,128,128]{2,1,0:T(8,128)} %fusion.134) | copy-start | bytes 3145732
  89.5 11.8 %collective-permute-start.4 = (bf16[4,64,128]{2,1,0:T(8,128)(2,1)S(1)}, bf16[4,64,128]{2,1,0:T(8,128)(2,1)S(1)}, u32[]{:S(2)}, u32[]{:S(2)}) collective-permute-start(bf16[4,64,128]{2,1,0:T(8,128)(2,1)S(1)} %convert_element_type.82), channel_id=1, source_target_pairs={{0,32},{32,64},{64,96},{96,128},{128,160},{160,192},{192,224},{224... | collective-permute-start | bytes 196616 | tf_op jit(solution)/shard_map/ppermute | solution.py:18
  91.5 9.8 %collective-permute-start.5 = (bf16[4,64,128]{2,1,0:T(8,128)(2,1)S(1)}, bf16[4,64,128]{2,1,0:T(8,128)(2,1)S(1)}, u32[]{:S(2)}, u32[]{:S(2)}) collective-permute-start(bf16[4,64,128]{2,1,0:T(8,128)(2,1)S(1)} %convert_element_type.82), channel_id=1, source_target_pairs={{0,64},{32,96},{64,128},{96,160},{128,192},{160,224},{192,256},{22... | collective-permute-start | bytes 196616 | tf_op jit(solution)/shard_map/ppermute | solution.py:18
  95.9 11.0 %collective-permute-start.10 = (f32[4]{0:T(128)S(1)}, f32[4]{0:T(128)S(1)}, u32[]{:S(2)}, u32[]{:S(2)}) collective-permute-start(f32[4]{0:T(128)S(1)} %get-tuple-element.11), channel_id=1, source_target_pairs={{0,64},{32,96},{64,128},{96,160},{128,192},{160,224},{192,256},{22... | collective-permute-start | bytes 56 | tf_op jit(solution)/shard_map/ppermute | solution.py:18
  101.4 10.4 %collective-permute-start.7 = (bf16[4,64,128]{2,1,0:T(8,128)(2,1)S(1)}, bf16[4,64,128]{2,1,0:T(8,128)(2,1)S(1)}, u32[]{:S(2)}, u32[]{:S(2)}) collective-permute-start(bf16[4,64,128]{2,1,0:T(8,128)(2,1)S(1)} %fusion.70), channel_id=1, source_target_pairs={{0,64},{32,96},{64,128},{96,160},{128,192},{160,224},{192,256},{22... | collective-permute-start | bytes 196616 | tf_op jit(solution)/shard_map/ppermute | solution.py:18
  106.9 12.5 %collective-permute-start.12 = (f32[4]{0:T(128)S(1)}, f32[4]{0:T(128)S(1)}, u32[]{:S(2)}, u32[]{:S(2)}) collective-permute-start(f32[4]{0:T(128)S(1)} %get-tuple-element.13), channel_id=1, source_target_pairs={{0,128},{32,160},{64,192},{96,224},{128,256},{160,288},{192,320},{... | collective-permute-start | bytes 56 | tf_op jit(solution)/shard_map/ppermute | solution.py:18
  112.0 13.6 %collective-permute-start.9 = (bf16[4,64,128]{2,1,0:T(8,128)(2,1)S(1)}, bf16[4,64,128]{2,1,0:T(8,128)(2,1)S(1)}, u32[]{:S(2)}, u32[]{:S(2)}) collective-permute-start(bf16[4,64,128]{2,1,0:T(8,128)(2,1)S(1)} %fusion.127), channel_id=1, source_target_pairs={{0,128},{32,160},{64,192},{96,224},{128,256},{160,288},{192,320},{... | collective-permute-start | bytes 196616 | tf_op jit(solution)/shard_map/ppermute | solution.py:18
  119.5 11.2 %collective-permute-start.14 = (f32[4]{0:T(128)S(1)}, f32[4]{0:T(128)S(1)}, u32[]{:S(2)}, u32[]{:S(2)}) collective-permute-start(f32[4]{0:T(128)S(1)} %get-tuple-element.9), channel_id=1, source_target_pairs={{0,256},{32,288},{64,320},{96,352},{128,384},{160,416},{192,448},{... | collective-permute-start | bytes 56 | tf_op jit(solution)/shard_map/ppermute | solution.py:18
  125.7 6.8 %collective-permute-start.11 = (bf16[4,64,128]{2,1,0:T(8,128)(2,1)S(1)}, bf16[4,64,128]{2,1,0:T(8,128)(2,1)S(1)}, u32[]{:S(2)}, u32[]{:S(2)}) collective-permute-start(bf16[4,64,128]{2,1,0:T(8,128)(2,1)S(1)} %fusion.77), channel_id=1, source_target_pairs={{0,256},{32,288},{64,320},{96,352},{128,384},{160,416},{192,448},{... | collective-permute-start | bytes 196616 | tf_op jit(solution)/shard_map/ppermute | solution.py:18
  132.7 14.7 %collective-permute-start.13 = (bf16[4,64,128]{2,1,0:T(8,128)(2,1)S(1)}, bf16[4,64,128]{2,1,0:T(8,128)(2,1)S(1)}, u32[]{:S(2)}, u32[]{:S(2)}) collective-permute-start(bf16[4,64,128]{2,1,0:T(8,128)(2,1)S(1)} %fusion.126), channel_id=1, source_target_pairs={{0,512},{32,544},{64,576},{96,608},{128,640},{160,672},{192,704},{... | collective-permute-start | bytes 196616 | tf_op jit(solution)/shard_map/ppermute | solution.py:18
  (4 other events, 12.3 us)

commit v2 on v1

--- a/solution.py
+++ b/solution.py
@@ -31,31 +31,34 @@
     return block
 
 
-def prefix_windows(total, axis):
+def prefix_state(total, state, axis):
     count = lax.axis_size(axis)
-    first = [d for d in (1, 2) if d < count]
+    heads, rows, cols = state.shape
+
+    def pack(t, s):
+        column = jnp.broadcast_to(t[:, None, None], (heads, 1, cols))
+        return jnp.concatenate([s, column], axis=1)
+
+    def received(t, s, d):
+        message = from_behind(pack(t, s), axis, d)
+        return message[:, rows, 0], message[:, :rows]
+
     window = jnp.zeros_like(total)
-    for d in first:
-        window = window + from_behind(total, axis, d)
-    spans = []
-    width = len(first)
-    while width < count:
-        spans.append((width, window))
-        window = window + from_behind(window, axis, width)
+    incoming = jnp.zeros_like(state)
+    width = 0
+    if count > 1:
+        t_one, s_one = received(total, state, 1)
+        window, incoming, width = t_one, s_one, 1
+    if count > 2:
+        t_two, s_two = received(total, state, 2)
+        incoming = s_two * jnp.exp(window)[:, None, None] + incoming
+        window = t_two + window
+        width = 2
+    while 0 < width < count:
+        t_far, s_far = received(window, incoming, width)
+        incoming = s_far * jnp.exp(window)[:, None, None] + incoming
+        window = t_far + window
         width *= 2
-    return first, spans
-
-
-def prefix_state(total, state, first, spans, axis):
-    incoming = jnp.zeros_like(state)
-    for d in first:
-        shifted = from_behind(state.astype(jnp.bfloat16), axis, d).astype(state.dtype)
-        if d == 2:
-            shifted = shifted * jnp.exp(from_behind(total, axis, 1))[:, None, None]
-        incoming = incoming + shifted
-    for width, window in spans:
-        earlier = from_behind(incoming.astype(jnp.bfloat16), axis, width).astype(state.dtype)
-        incoming = earlier * jnp.exp(window)[:, None, None] + incoming
     return incoming
 
 
@@ -154,12 +157,11 @@
     )
     local_starts = jnp.einsum("cdh,dhpn->chpn", weights, block_states, precision=highest)
     device_total = through[-1]
-    first, spans = prefix_windows(device_total, "seq")
     device_state = jnp.einsum(
         "dh,dhpn->hpn", jnp.exp(device_total[None, :] - through), block_states, precision=highest
     )
 
-    incoming = prefix_state(device_total, device_state, first, spans, "seq")
+    incoming = prefix_state(device_total, device_state, "seq")
     block_in = local_starts + jnp.exp(before_block)[:, :, None, None] * incoming[None]
     carried = (
         jnp.einsum("cin,chpn->cihp", c_all, block_in, precision=high_mode)

time: 159 us -> 168 us (1.057)
  the two profiles are of different devices: /device:TPU:6 before, /device:TPU:132 now
where the time goes in v2:
time: 168 us; the launch traced here: 167 us
  starting transfers between devices  65.4 us (39%)
  local copies, waits for them, and re-layouts  37.9 us (23%)
  waiting for transfers between devices  29.3 us (17%)
  matrix products  20.4 us (12%)
  other arithmetic  13.3 us (8%)
    ppermute x8, starting transfers between devices, from_behind(): return lax.ppermute(value, axis, pairs)  53.6 us
    all_to_all x1, waiting for transfers between devices, shards(): lax.all_to_all(projected, 'enc', split_axis=1, concat_axis=0, tiled=True)  15.9 us
    ppermute x8, waiting for transfers between devices, from_behind(): return lax.ppermute(value, axis, pairs)  10.9 us
    gather x1, local copies, waits for them, and re-layouts, shards(): jnp.take(widened, local_row, axis=0)  9.06 us
    unnamed x31, local copies, waits for them, and re-layouts  7.99 us
    all_to_all x1, starting transfers between devices, shards(): lax.all_to_all(projected, 'enc', split_axis=1, concat_axis=0, tiled=True)  6.2 us
    reshape x2, local copies, waits for them, and re-layouts, shards(): plain = mixed_in.reshape(blocks, SPAN, head_count, HDIM)  5.45 us
    convert_element_type x2, local copies, waits for them, and re-layouts, shards(): return output.reshape(row_count, head_count * HDIM).astype(jnp.bfloat16)  5.02 us
  transfers between devices with their start and end apart: 11, of which 9 were waited for; matrix products, arithmetic and copies ran while one was open for 15% of the time, Pallas kernels for 0%

profile of v2, /device:TPU:132, one launch (start us, length us, event | category | flops | bytes accessed | tf_op | source)
XLA Modules:
  0.0 166.9 jit_solution(15920608670529953019)
XLA Ops:
  1.0 3.5 %collective-permute-start = (bf16[1,128]{1,0:T(2,128)(2,1)S(1)}, bf16[1,128]{1,0:T(2,128)(2,1)S(1)}, u32[]{:S(2)}, u32[]{:S(2)}) collective-permute-start(bf16[1,128]{1,0:T(2,128)(2,1)S(1)} %slice.111), channel_id=1, source_target_pairs={{0,4},{4,8},{8,12},{12,16},{16,20},{20,24},{24,28},{28,32},{32,36}... | collective-permute-start | bytes 776 | tf_op jit(solution)/shard_map/ppermute | solution.py:18
  9.7 7.1 %copy.172 = bf16[160,8,8,256]{3,1,2,0:T(8,128)(2,1)} copy(bf16[160,8,8,256]{3,2,1,0:T(8,128)(2,1)} %bitcast.81) | data formatting | bytes 10485760
  16.9 4.9 %convolution_convert_fusion = bf16[128,2048]{1,0:T(8,128)(2,1)S(1)} fusion(bf16[1280,2048]{1,0:T(8,128)(2,1)} %bitcast.82, bf16[384,1280]{1,0:T(8,128)(2,1)S(1)} %copy-done, f32[1280]{0:T(1024)S(1)} %copy-done.13, bf16[128,256]{1,0:T(8,128)(2,1)S(1)} %reshape.211, bf16[128,128]{1,0:T(8,128)(2,1)S(1)} %maximum_select_fusion), kind=kOutput, calls=%fused_computation.5 | convolution fusion | flops 808189952 | bytes 6853632 | tf_op jit(solution)/shard_map/dot_general | solution.py:95
  22.7 6.2 %all-to-all-start = ((bf16[128,8,256]{2,0,1:T(8,128)(2,1)}), bf16[128,8,256]{2,0,1:T(8,128)(2,1)}, u32[]{:S(2)}, u32[]{:S(2)}) async-start(bf16[128,8,256]{2,0,1:T(8,128)(2,1)} %bitcast.78), calls=%async_computation | async-start | bytes 1048576 | tf_op jit(solution)/shard_map/all_to_all | solution.py:99
  30.3 15.9 %all-to-all-done = bf16[128,8,256]{2,0,1:T(8,128)(2,1)} async-done(((bf16[128,8,256]{2,0,1:T(8,128)(2,1)}), bf16[128,8,256]{2,0,1:T(8,128)(2,1)}, u32[]{:S(2)}, u32[]{:S(2)}) %all-to-all-start) | async-done | bytes 524320 | tf_op jit(solution)/shard_map/all_to_all | solution.py:99
  49.1 3.6 %collective-permute-start.2 = (bf16[256,256]{1,0:T(8,128)(2,1)S(1)}, bf16[256,256]{1,0:T(8,128)(2,1)S(1)}, u32[]{:S(2)}, u32[]{:S(2)}) collective-permute-start(bf16[256,256]{1,0:T(8,128)(2,1)S(1)} %bitcast.93), channel_id=1, source_target_pairs={{32,0},{64,32},{96,64},{128,96},{160,128},{192,160},{224,192},{256... | collective-permute-start | bytes 393224 | tf_op jit(solution)/shard_map/ppermute | solution.py:29
  56.4 9.1 %gather_fusion = bf16[2048,256]{1,0:T(8,128)(2,1)} fusion(bf16[1536,256]{1,0:T(8,128)(2,1)S(1)} %pad_maximum_fusion.1, s32[2048]{0:T(1024)S(1)} %broadcast_clamp_fusion), kind=kCustom, calls=%fused_computation | custom fusion | bytes 2105344 | tf_op jit(solution)/shard_map/jit(_take)/gather | solution.py:115
  65.4 3.2 %select_select_fusion = bf16[2048,256]{1,0:T(8,128)(2,1)S(1)} fusion(bf16[2048,256]{1,0:T(8,128)(2,1)} %param.19, bf16[2048,256]{1,0:T(8,128)(2,1)} %gather_fusion, pred[2048]{0:T(1024)(128)(4,1)S(1)} %get-tuple-element.18, pred[2048]{0:T(1024)(128)(4,1)S(1)} %get-tuple-element.19), kind=kLoop, calls=%fused_computation.38 | loop fusion | flops 1048576 | bytes 3149824 | tf_op jit(solution)/shard_map/jit(_where)/select_n | solution.py:115
  68.6 5.0 %collective-permute-start.3 = (bf16[3,256]{1,0:T(4,128)(2,1)S(1)}, bf16[3,256]{1,0:T(4,128)(2,1)S(1)}, u32[]{:S(2)}, u32[]{:S(2)}) collective-permute-start(bf16[3,256]{1,0:T(4,128)(2,1)S(1)} %slice.115), channel_id=1, source_target_pairs={{0,32},{32,64},{64,96},{96,128},{128,160},{160,192},{192,224},{224... | collective-permute-start | bytes 4616 | tf_op jit(solution)/shard_map/ppermute | solution.py:18
  74.2 2.3 %multiply_convert_fusion.2 = bf16[2048,256]{1,0:T(8,128)(2,1)} fusion(bf16[2048,256]{1,0:T(8,128)(2,1)S(1)} %select_select_fusion, bf16[3,256]{1,0:T(4,128)(2,1)S(1)} %collective-permute-done.3, f32[256]{0:T(256)S(1)} %bitcast.102, f32[256]{0:T(256)S(1)} %bitcast.103, f32[256]{0:T(256)S(1)} %bitcast.101, f32[256]{0:T(256)S(1)} %bitcast.100), kind=kLoop, calls=%fused_computation.21 | loop fusion | flops 13107200 | bytes 2102784 | tf_op jit(solution)/shard_map/convert_element_type | solution.py:123
  76.5 3.3 %reshape.233 = bf16[16,128,4,64]{3,2,1,0:T(4,128)(2,1)S(1)} reshape(bf16[2048,256]{1,0:T(8,128)(2,1)} %multiply_convert_fusion.2) | data formatting | bytes 2097152 | tf_op jit(solution)/shard_map/reshape | solution.py:126
  84.1 2.2 %fusion.15 = f32[4,1,64,128]{3,1,2,0:T(1,128)S(1)} fusion(f32[16,4,1,1]{0,2,3,1:T(1,128)S(1)} %copy.163, f32[16,4,64,128]{3,2,1,0:T(8,128)S(1)} %fusion.2), kind=kOutput, calls=%fused_computation.23 | convolution fusion | flops 6291456 | bytes 2228480 | tf_op jit(solution)/shard_map/dh,dhpn->hpn/dot_general | solution.py:160
  86.6 6.4 %collective-permute-start.4 = (f32[4,65,128]{2,0,1:T(4,128)S(1)}, f32[4,65,128]{2,0,1:T(4,128)S(1)}, u32[]{:S(2)}, u32[]{:S(2)}) collective-permute-start(f32[4,65,128]{2,0,1:T(4,128)S(1)} %pad_maximum_fusion.2), channel_id=1, source_target_pairs={{0,64},{32,96},{64,128},{96,160},{128,192},{160,224},{192,256},{22... | collective-permute-start | bytes 399368 | tf_op jit(solution)/shard_map/ppermute | solution.py:18
  96.3 3.0 %collective-permute-done.5 = f32[4,65,128]{2,0,1:T(4,128)S(1)} collective-permute-done((f32[4,65,128]{2,0,1:T(4,128)S(1)}, f32[4,65,128]{2,0,1:T(4,128)S(1)}, u32[]{:S(2)}, u32[]{:S(2)}) %collective-permute-start.5) | collective-permute-done | bytes 133152 | tf_op jit(solution)/shard_map/ppermute | solution.py:18
  99.6 5.2 %collective-permute-start.6 = (f32[4,65,128]{2,0,1:T(4,128)S(1)}, f32[4,65,128]{2,0,1:T(4,128)S(1)}, u32[]{:S(2)}, u32[]{:S(2)}) collective-permute-start(f32[4,65,128]{2,0,1:T(4,128)S(1)} %pad_maximum_fusion.3), channel_id=1, source_target_pairs={{0,64},{32,96},{64,128},{96,160},{128,192},{160,224},{192,256},{22... | collective-permute-start | bytes 399368 | tf_op jit(solution)/shard_map/ppermute | solution.py:18
  108.3 5.9 %collective-permute-start.7 = (f32[4,65,128]{2,0,1:T(4,128)S(1)}, f32[4,65,128]{2,0,1:T(4,128)S(1)}, u32[]{:S(2)}, u32[]{:S(2)}) collective-permute-start(f32[4,65,128]{2,0,1:T(4,128)S(1)} %pad_maximum_fusion.4), channel_id=1, source_target_pairs={{0,128},{32,160},{64,192},{96,224},{128,256},{160,288},{192,320},{... | collective-permute-start | bytes 399368 | tf_op jit(solution)/shard_map/ppermute | solution.py:18
  114.2 3.8 %collective-permute-done.7 = f32[4,65,128]{2,0,1:T(4,128)S(1)} collective-permute-done((f32[4,65,128]{2,0,1:T(4,128)S(1)}, f32[4,65,128]{2,0,1:T(4,128)S(1)}, u32[]{:S(2)}, u32[]{:S(2)}) %collective-permute-start.7) | collective-permute-done | bytes 133152 | tf_op jit(solution)/shard_map/ppermute | solution.py:18
  118.9 12.4 %collective-permute-start.8 = (f32[4,65,128]{2,0,1:T(4,128)S(1)}, f32[4,65,128]{2,0,1:T(4,128)S(1)}, u32[]{:S(2)}, u32[]{:S(2)}) collective-permute-start(f32[4,65,128]{2,0,1:T(4,128)S(1)} %pad_maximum_fusion.5), channel_id=1, source_target_pairs={{0,256},{32,288},{64,320},{96,352},{128,384},{160,416},{192,448},{... | collective-permute-start | bytes 399368 | tf_op jit(solution)/shard_map/ppermute | solution.py:18
  132.0 2.2 %copy.141 = f32[16,128,4]{1,2,0:T(4,128)} copy(f32[16,128,4]{2,0,1:T(8,128)} %copy-done.1) | data formatting | bytes 65536 | tf_op jit(solution)/shard_map/jit(cumsum)/reduce_window_sum | solution.py:134
  138.7 13.3 %collective-permute-start.9 = (f32[4,65,128]{2,0,1:T(4,128)S(1)}, f32[4,65,128]{2,0,1:T(4,128)S(1)}, u32[]{:S(2)}, u32[]{:S(2)}) collective-permute-start(f32[4,65,128]{2,0,1:T(4,128)S(1)} %pad_maximum_fusion.6), channel_id=1, source_target_pairs={{0,512},{32,544},{64,576},{96,608},{128,640},{160,672},{192,704},{... | collective-permute-start | bytes 399368 | tf_op jit(solution)/shard_map/ppermute | solution.py:18
  152.0 3.8 %fusion = f32[16,4,64,128]{3,2,1,0:T(8,128)S(1)} fusion(bf16[16,128,4,64]{1,3,2,0:T(8,128)(2,1)} %copy.144, f32[16,128,4]{1,2,0:T(4,128)S(1)} %bitcast.91, f32[16,128,128]{2,1,0:T(8,128)} %fusion.135, f32[16,128,4]{1,2,0:T(4,128)} %copy.141, pred[128,128]{1,0:T(8,128)(4,1)S(1)} %iota_compare_fusion.1), kind=kOutput, calls=%fused_computation.6 | convolution fusion | flops 140509184 | bytes 4276224 | tf_op jit(solution)/shard_map/cijh,cjhp->cihp/dot_general | solution.py:142
  156.0 3.2 %bitcast_add_fusion = f32[16,4,64,128]{3,0,2,1:T(8,128)S(1)} fusion(f32[4,64,128]{2,1,0:T(8,128)S(1)} %copy.156, f32[16,4]{0,1:T(4,128)S(1)} %copy-done.7, f32[16,4,64,128]{3,2,1,0:T(8,128)S(1)} %fusion.2, f32[16,4]{0,1:T(4,128)S(1)} %copy.151, f32[16,4]{0,1:T(4,128)S(1)} %fusion.93, pred[16,16]{1,0:T(8,128)(4,1)S(1)} %copy-done.8), kind=kOutput, calls=%fused_computation.13 | convolution fusion | flops 101714944 | bytes 4326400 | tf_op jit(solution)/shard_map/cdh,dhpn->chpn/dot_general | solution.py:158
  159.3 2.6 %fusion.5 = bf16[16,128,4,64]{1,3,2,0:T(8,128)(2,1)} fusion(bf16[16,128,4,64]{1,3,2,0:T(8,128)(2,1)S(1)} %copy-done.2, f32[16,4,64,128]{3,2,1,0:T(8,128)S(1)} %fusion, bf16[16,128,128,1]{2,1,3,0:T(8,128)(2,1)S(1)} %bitcast.86, f32[16,4,64,128]{3,0,2,1:T(8,128)S(1)} %bitcast_add_fusion, f32[4]{0:T(128)S(1)} %copy-done.12, f32[16,128,4]{1,2,0:T(4,128)S(1)} %copy.158), kind=kOutput, calls=%fused_computation.10 | convolution fusion | flops 405798912 | bytes 6848528 | tf_op jit(solution)/shard_map/cin,chpn->cihp/dot_general | solution.py:167
  161.9 2.9 %copy.166 = bf16[16,128,4,64]{3,2,1,0:T(4,128)(2,1)S(1)} copy(bf16[16,128,4,64]{1,3,2,0:T(8,128)(2,1)} %fusion.5) | data formatting | bytes 2097152 | tf_op jit(solution)/shard_map/convert_element_type | solution.py:171
  (104 shorter events, 35.4 us)
Async XLA Ops:
  0.0 16.9 %copy-start = (bf16[384,1280]{1,0:T(8,128)(2,1)S(1)}, bf16[384,1280]{1,0:T(8,128)(2,1)}, u32[]{:S(2)}) copy-start(bf16[384,1280]{1,0:T(8,128)(2,1)} %param.14) | copy-start | bytes 2949124
  0.0 9.3 %copy-start.11 = (s32[64]{0:T(128)S(1)}, s32[64]{0:T(128)}, u32[]{:S(2)}) copy-start(s32[64]{0:T(128)} %param.17) | copy-start | bytes 772
  0.0 9.3 %copy-start.10 = (s32[64]{0:T(128)S(1)}, s32[64]{0:T(128)}, u32[]{:S(2)}) copy-start(s32[64]{0:T(128)} %param.18) | copy-start | bytes 772
  1.0 15.8 %collective-permute-start = (bf16[1,128]{1,0:T(2,128)(2,1)S(1)}, bf16[1,128]{1,0:T(2,128)(2,1)S(1)}, u32[]{:S(2)}, u32[]{:S(2)}) collective-permute-start(bf16[1,128]{1,0:T(2,128)(2,1)S(1)} %slice.111), channel_id=1, source_target_pairs={{0,4},{4,8},{8,12},{12,16},{16,20},{20,24},{24,28},{28,32},{32,36}... | collective-permute-start | bytes 776 | tf_op jit(solution)/shard_map/ppermute | solution.py:18
  9.0 19.9 %copy-start.1 = (f32[16,128,4]{2,0,1:T(8,128)}, f32[16,128,4]{2,0,1:T(8,128)S(1)}, u32[]{:S(2)}) copy-start(f32[16,128,4]{2,0,1:T(8,128)S(1)} %fusion.25) | copy-start | bytes 98308
  9.7 7.2 %copy-start.13 = (f32[1280]{0:T(1024)S(1)}, f32[1280]{0:T(1024)}, u32[]{:S(2)}) copy-start(f32[1280]{0:T(1024)} %param.15) | copy-start | bytes 15364
  22.7 23.5 %all-to-all-start = ((bf16[128,8,256]{2,0,1:T(8,128)(2,1)}), bf16[128,8,256]{2,0,1:T(8,128)(2,1)}, u32[]{:S(2)}, u32[]{:S(2)}) async-start(bf16[128,8,256]{2,0,1:T(8,128)(2,1)} %bitcast.78), calls=%async_computation | async-start | bytes 1048576 | tf_op jit(solution)/shard_map/all_to_all | solution.py:99
  47.2 6.3 %collective-permute-start.1 = (bf16[256,256]{1,0:T(8,128)(2,1)S(1)}, bf16[256,256]{1,0:T(8,128)(2,1)S(1)}, u32[]{:S(2)}, u32[]{:S(2)}) collective-permute-start(bf16[256,256]{1,0:T(8,128)(2,1)S(1)} %bitcast.94), channel_id=1, source_target_pairs={{0,32},{32,64},{64,96},{96,128},{128,160},{160,192},{192,224},{224... | collective-permute-start | bytes 393224 | tf_op jit(solution)/shard_map/ppermute | solution.py:26
  49.1 6.1 %collective-permute-start.2 = (bf16[256,256]{1,0:T(8,128)(2,1)S(1)}, bf16[256,256]{1,0:T(8,128)(2,1)S(1)}, u32[]{:S(2)}, u32[]{:S(2)}) collective-permute-start(bf16[256,256]{1,0:T(8,128)(2,1)S(1)} %bitcast.93), channel_id=1, source_target_pairs={{32,0},{64,32},{96,64},{128,96},{160,128},{192,160},{224,192},{256... | collective-permute-start | bytes 393224 | tf_op jit(solution)/shard_map/ppermute | solution.py:29
  65.4 8.2 %copy-start.9 = (f32[4,256]{1,0:T(4,128)S(1)}, f32[4,256]{1,0:T(4,128)}, u32[]{:S(2)}) copy-start(f32[4,256]{1,0:T(4,128)} %param.20) | copy-start | bytes 12292
  68.6 5.6 %collective-permute-start.3 = (bf16[3,256]{1,0:T(4,128)(2,1)S(1)}, bf16[3,256]{1,0:T(4,128)(2,1)S(1)}, u32[]{:S(2)}, u32[]{:S(2)}) collective-permute-start(bf16[3,256]{1,0:T(4,128)(2,1)S(1)} %slice.115), channel_id=1, source_target_pairs={{0,32},{32,64},{64,96},{96,128},{128,160},{160,192},{192,224},{224... | collective-permute-start | bytes 4616 | tf_op jit(solution)/shard_map/ppermute | solution.py:18
  84.1 20.8 %copy-start.3 = (bf16[2048,128]{1,0:T(8,128)(2,1)S(1)}, bf16[2048,128]{1,0:T(8,128)(2,1)}, u32[]{:S(2)}) copy-start(bf16[2048,128]{1,0:T(8,128)(2,1)} %param.21) | copy-start | bytes 1572868
  84.1 20.8 %copy-start.4 = (bf16[2048,128]{1,0:T(8,128)(2,1)S(1)}, bf16[2048,128]{1,0:T(8,128)(2,1)}, u32[]{:S(2)}) copy-start(bf16[2048,128]{1,0:T(8,128)(2,1)} %param.22) | copy-start | bytes 1572868
  86.6 9.7 %collective-permute-start.4 = (f32[4,65,128]{2,0,1:T(4,128)S(1)}, f32[4,65,128]{2,0,1:T(4,128)S(1)}, u32[]{:S(2)}, u32[]{:S(2)}) collective-permute-start(f32[4,65,128]{2,0,1:T(4,128)S(1)} %pad_maximum_fusion.2), channel_id=1, source_target_pairs={{0,64},{32,96},{64,128},{96,160},{128,192},{160,224},{192,256},{22... | collective-permute-start | bytes 399368 | tf_op jit(solution)/shard_map/ppermute | solution.py:18
  93.0 6.3 %collective-permute-start.5 = (f32[4,65,128]{2,0,1:T(4,128)S(1)}, f32[4,65,128]{2,0,1:T(4,128)S(1)}, u32[]{:S(2)}, u32[]{:S(2)}) collective-permute-start(f32[4,65,128]{2,0,1:T(4,128)S(1)} %pad_maximum_fusion.2), channel_id=1, source_target_pairs={{0,32},{32,64},{64,96},{96,128},{128,160},{160,192},{192,224},{224... | collective-permute-start | bytes 399368 | tf_op jit(solution)/shard_map/ppermute | solution.py:18
  99.6 8.3 %collective-permute-start.6 = (f32[4,65,128]{2,0,1:T(4,128)S(1)}, f32[4,65,128]{2,0,1:T(4,128)S(1)}, u32[]{:S(2)}, u32[]{:S(2)}) collective-permute-start(f32[4,65,128]{2,0,1:T(4,128)S(1)} %pad_maximum_fusion.3), channel_id=1, source_target_pairs={{0,64},{32,96},{64,128},{96,160},{128,192},{160,224},{192,256},{22... | collective-permute-start | bytes 399368 | tf_op jit(solution)/shard_map/ppermute | solution.py:18
  108.3 9.7 %collective-permute-start.7 = (f32[4,65,128]{2,0,1:T(4,128)S(1)}, f32[4,65,128]{2,0,1:T(4,128)S(1)}, u32[]{:S(2)}, u32[]{:S(2)}) collective-permute-start(f32[4,65,128]{2,0,1:T(4,128)S(1)} %pad_maximum_fusion.4), channel_id=1, source_target_pairs={{0,128},{32,160},{64,192},{96,224},{128,256},{160,288},{192,320},{... | collective-permute-start | bytes 399368 | tf_op jit(solution)/shard_map/ppermute | solution.py:18
  118.9 18.8 %collective-permute-start.8 = (f32[4,65,128]{2,0,1:T(4,128)S(1)}, f32[4,65,128]{2,0,1:T(4,128)S(1)}, u32[]{:S(2)}, u32[]{:S(2)}) collective-permute-start(f32[4,65,128]{2,0,1:T(4,128)S(1)} %pad_maximum_fusion.5), channel_id=1, source_target_pairs={{0,256},{32,288},{64,320},{96,352},{128,384},{160,416},{192,448},{... | collective-permute-start | bytes 399368 | tf_op jit(solution)/shard_map/ppermute | solution.py:18
  138.7 17.2 %copy-start.7 = (f32[16,4]{0,1:T(4,128)S(1)}, f32[16,4]{0,1:T(4,128)}, u32[]{:S(2)}) copy-start(f32[16,4]{0,1:T(4,128)} %copy.155) | copy-start | bytes 772
  138.7 17.2 %copy-start.8 = (pred[16,16]{1,0:T(8,128)(4,1)S(1)}, pred[16,16]{1,0:T(8,128)(4,1)}, u32[]{:S(2)}) copy-start(pred[16,16]{1,0:T(8,128)(4,1)} %iota_compare_fusion.2) | copy-start | bytes 772
  138.7 17.1 %collective-permute-start.9 = (f32[4,65,128]{2,0,1:T(4,128)S(1)}, f32[4,65,128]{2,0,1:T(4,128)S(1)}, u32[]{:S(2)}, u32[]{:S(2)}) collective-permute-start(f32[4,65,128]{2,0,1:T(4,128)S(1)} %pad_maximum_fusion.6), channel_id=1, source_target_pairs={{0,512},{32,544},{64,576},{96,608},{128,640},{160,672},{192,704},{... | collective-permute-start | bytes 399368 | tf_op jit(solution)/shard_map/ppermute | solution.py:18
  156.0 3.3 %copy-start.2 = (bf16[16,128,4,64]{1,3,2,0:T(8,128)(2,1)S(1)}, bf16[16,128,4,64]{1,3,2,0:T(8,128)(2,1)}, u32[]{:S(2)}) copy-start(bf16[16,128,4,64]{1,3,2,0:T(8,128)(2,1)} %copy.144) | copy-start | bytes 3145732
  156.0 3.3 %copy-start.5 = (bf16[2048,128]{1,0:T(8,128)(2,1)S(1)}, bf16[2048,128]{1,0:T(8,128)(2,1)}, u32[]{:S(2)}) copy-start(bf16[2048,128]{1,0:T(8,128)(2,1)} %param.22) | copy-start | bytes 1572868
  156.0 3.3 %copy-start.12 = (f32[4]{0:T(128)S(1)}, f32[4]{0:T(128)}, u32[]{:S(2)}) copy-start(f32[4]{0:T(128)} %param.25) | copy-start | bytes 52
  (1 other events, 2.2 us)

commit v3 on v2

--- a/solution.py
+++ b/solution.py
@@ -80,27 +80,26 @@
     tiles = mel_frames.shape[0] // 2
     channels = mel_frames.shape[1]
     enc_count = lax.axis_size("enc")
-    tile_first = (lax.axis_index("seq") * enc_count + lax.axis_index("enc")) * tiles
     seg_start = jnp.cumsum(seg_lengths) - seg_lengths
     frame_pairs = mel_frames.reshape(tiles, 2 * channels)
-    edge_frame = from_behind(frame_pairs[-1:, channels:], ("seq", "enc"), 1)
-    tokens = tile_first + jnp.arange(tiles, dtype=jnp.int32)
+    owner_pairs = lax.all_gather(frame_pairs, "enc", axis=0, tiled=True)
+    shard_audio = owner_pairs.shape[0]
+    behind = from_behind(owner_pairs[shard_audio - DRIFT - 1 :], "seq", 1)
+    ahead = from_behind(owner_pairs[:DRIFT], "seq", -1)
+    wide_pairs = jnp.concatenate([behind, owner_pairs, ahead], axis=0)
+    token_count = shard_audio + 2 * DRIFT
+    token_first = lax.axis_index("seq") * shard_audio - DRIFT
+    tokens = token_first + jnp.arange(token_count, dtype=jnp.int32)
     opening = jnp.any(tokens[:, None] == seg_start[None, :], axis=1)
-    left_frames = jnp.concatenate([edge_frame, frame_pairs[:-1, channels:]], axis=0)
+    left_frames = wide_pairs[:token_count, channels:]
     left_frames = jnp.where(opening[:, None], jnp.zeros_like(left_frames), left_frames)
-    stacked = jnp.concatenate([left_frames, frame_pairs], axis=1)
+    stacked = jnp.concatenate([left_frames, wide_pairs[1:]], axis=1)
     summed = jnp.dot(stacked, conv_weight, preferred_element_type=jnp.float32) + conv_bias
     features = jax.nn.gelu(summed, approximate=False).astype(jnp.bfloat16)
-    column_width = projector.shape[2]
-    projected = jnp.dot(
-        features, projector.reshape(projector.shape[0], -1), preferred_element_type=jnp.float32
+    block_columns = lax.dynamic_index_in_dim(projector, lax.axis_index("enc"), 1, False)
+    widened = jnp.dot(features, block_columns, preferred_element_type=jnp.float32).astype(
+        jnp.bfloat16
     )
-    projected = projected.astype(jnp.bfloat16).reshape(tiles, enc_count, column_width)
-    audio_rows = lax.all_to_all(projected, "enc", split_axis=1, concat_axis=0, tiled=True).reshape(
-        tiles * enc_count, column_width
-    )
-    shard_audio = audio_rows.shape[0]
-    widened = padded_2(audio_rows, (("seq", 0),), DRIFT)
     row_count = text_embed.shape[0]
     owner_index = lax.axis_index("seq")
     places = owner_index * row_count + jnp.arange(row_count, dtype=jnp.int32)

time: 168 us -> 191 us (1.14)
  the two profiles are of different devices: /device:TPU:132 before, /device:TPU:6 now
where the time goes in v3:
time: 191 us; the launch traced here: 187 us
  starting transfers between devices  65.5 us (34%)
  local copies, waits for them, and re-layouts  38 us (20%)
  matrix products  36.7 us (19%)
  blocking collectives  26.9 us (14%)
  other arithmetic  14.1 us (7%)
  waiting for transfers between devices  4.9 us (3%)
    ppermute x9, starting transfers between devices, from_behind(): return lax.ppermute(value, axis, pairs)  65.5 us
    all_gather x1, blocking collectives, shards(): owner_pairs = lax.all_gather(frame_pairs, 'enc', axis=0, tiled=True)  26.9 us
    dot_general x1, matrix products, shards(): jnp.dot(features, block_columns, preferred_element_type=jnp.float32)  20.9 us
    gather x1, local copies, waits for them, and re-layouts, shards(): jnp.take(widened, local_row, axis=0)  9.06 us
    reshape x2, local copies, waits for them, and re-layouts, shards(): plain = mixed_in.reshape(blocks, SPAN, head_count, HDIM)  5.45 us
    convert_element_type x2, local copies, waits for them, and re-layouts, shards(): return output.reshape(row_count, head_count * HDIM).astype(jnp.bfloat16)  5.02 us
    ppermute x9, waiting for transfers between devices, from_behind(): return lax.ppermute(value, axis, pairs)  4.9 us
    dynamic_slice x1, local copies, waits for them, and re-layouts, shards(): lax.dynamic_index_in_dim(projector, lax.axis_index('enc'), 1, False)  4.08 us
  transfers between devices with their start and end apart: 9, of which 4 were waited for; matrix products, arithmetic and copies ran while one was open for 13% of the time, Pallas kernels for 0%

profile of v3, /device:TPU:6, one launch (start us, length us, event | category | flops | bytes accessed | tf_op | source)
XLA Modules:
  0.0 187.0 jit_solution(2245309393810723147)
XLA Ops:
  1.0 26.9 %all_gather.3 = bf16[1024,256]{1,0:T(8,128)(2,1)S(1)} all-gather(bf16[128,256]{1,0:T(8,128)(2,1)S(1)} %reshape.199), channel_id=1, replica_groups=mesh['seq'=32,'enc'=8,'head'=4] {'enc'}, dimensions={0}, use_global_device_ids=true | all-gather | bytes 589824 | tf_op jit(solution)/shard_map/all_gather | solution.py:85
  38.7 4.1 %constant_dynamic-slice_fusion = bf16[1280,1,256]{2,1,0:T(2,128)(2,1)} fusion(bf16[1280,8,256]{2,1,0:T(8,128)(2,1)} %param.16, s32[]{:T(128)S(6)} %select_n.77), kind=kLoop, calls=%fused_computation.123 | loop fusion | bytes 1310724 | tf_op jit(solution)/shard_map/jit(dynamic_index_in_dim)/dynamic_slice | solution.py:99
  42.9 3.8 %concatenate.25 = bf16[1537,256]{1,0:T(8,128)(2,1)S(1)} concatenate(bf16[257,256]{1,0:T(8,128)(2,1)S(1)} %collective-permute-done, bf16[1024,256]{1,0:T(8,128)(2,1)} %copy-done.4, bf16[256,256]{1,0:T(8,128)(2,1)S(1)} %collective-permute-done.1), dimensions={0} | concatenate | bytes 1573888 | tf_op jit(solution)/shard_map/concatenate | solution.py:89
  48.1 20.9 %convolution_convert_fusion = bf16[1536,256]{1,0:T(8,128)(2,1)S(1)} fusion(bf16[384,1280]{1,0:T(8,128)(2,1)S(1)} %copy-done, f32[1280]{0:T(1024)S(1)} %copy-done.15, bf16[1536,256]{1,0:T(8,128)(2,1)} %slice.106, bf16[1536,128]{1,0:T(8,128)(2,1)S(1)} %slice_select_fusion, bf16[1280,1,256]{2,1,0:T(2,128)(2,1)} %constant_dynamic-slice_fusion), kind=kOutput, calls=%fused_computation.24 | convolution fusion | flops 2649096192 | bytes 3609600 | tf_op jit(solution)/shard_map/dot_general | solution.py:100
  69.0 9.1 %gather_fusion = bf16[2048,256]{1,0:T(8,128)(2,1)} fusion(bf16[1536,256]{1,0:T(8,128)(2,1)S(1)} %convolution_convert_fusion, s32[2048]{0:T(1024)S(1)} %broadcast_clamp_fusion), kind=kCustom, calls=%fused_computation | custom fusion | bytes 2105344 | tf_op jit(solution)/shard_map/jit(_take)/gather | solution.py:114
  78.1 3.1 %select_select_fusion = bf16[2048,256]{1,0:T(8,128)(2,1)S(1)} fusion(bf16[2048,256]{1,0:T(8,128)(2,1)} %param.19, bf16[2048,256]{1,0:T(8,128)(2,1)} %gather_fusion, pred[2048]{0:T(1024)(128)(4,1)S(1)} %get-tuple-element.18, pred[2048]{0:T(1024)(128)(4,1)S(1)} %get-tuple-element.19), kind=kLoop, calls=%fused_computation.60 | loop fusion | flops 1048576 | bytes 3149824 | tf_op jit(solution)/shard_map/jit(_where)/select_n | solution.py:114
  81.2 5.6 %collective-permute-start.2 = (bf16[3,256]{1,0:T(4,128)(2,1)S(1)}, bf16[3,256]{1,0:T(4,128)(2,1)S(1)}, u32[]{:S(2)}, u32[]{:S(2)}) collective-permute-start(bf16[3,256]{1,0:T(4,128)(2,1)S(1)} %slice.107), channel_id=1, source_target_pairs={{0,32},{32,64},{64,96},{96,128},{128,160},{160,192},{192,224},{224... | collective-permute-start | bytes 4616 | tf_op jit(solution)/shard_map/ppermute | solution.py:18
  87.7 2.4 %multiply_convert_fusion.2 = bf16[2048,256]{1,0:T(8,128)(2,1)} fusion(bf16[2048,256]{1,0:T(8,128)(2,1)S(1)} %select_select_fusion, bf16[3,256]{1,0:T(4,128)(2,1)S(1)} %collective-permute-done.2, f32[256]{0:T(256)S(1)} %bitcast.86, f32[256]{0:T(256)S(1)} %bitcast.87, f32[256]{0:T(256)S(1)} %bitcast.85, f32[256]{0:T(256)S(1)} %bitcast.84), kind=kLoop, calls=%fused_computation.40 | loop fusion | flops 13107200 | bytes 2102784 | tf_op jit(solution)/shard_map/convert_element_type | solution.py:122
  90.1 3.3 %reshape.218 = bf16[16,128,4,64]{3,2,1,0:T(4,128)(2,1)S(1)} reshape(bf16[2048,256]{1,0:T(8,128)(2,1)} %multiply_convert_fusion.2) | data formatting | bytes 2097152 | tf_op jit(solution)/shard_map/reshape | solution.py:125
  93.4 2.1 %copy.139 = bf16[16,128,4,64]{1,3,2,0:T(8,128)(2,1)} copy(bf16[16,128,4,64]{3,2,1,0:T(4,128)(2,1)S(1)} %reshape.218) | data formatting | bytes 2097152 | tf_op jit(solution)/shard_map/reshape | solution.py:125
  95.6 2.2 %fusion.12 = f32[16,4,64,128]{3,2,1,0:T(8,128)S(1)} fusion(bf16[16,128,128,1]{2,1,3,0:T(8,128)(2,1)} %bitcast.70, bf16[16,128,4,64]{1,3,2,0:T(8,128)(2,1)} %copy.139, f32[16,128,4]{1,2,0:T(4,128)S(1)} %copy.144, f32[16,128,4]{1,2,0:T(4,128)S(1)} %bitcast.76), kind=kOutput, calls=%fused_computation.27 | convolution fusion | flops 404226048 | bytes 3735552 | tf_op jit(solution)/shard_map/cjhp,cjn->chpn/dot_general | solution.py:144
  97.8 2.2 %fusion.25 = f32[4,1,64,128]{3,1,2,0:T(1,128)S(1)} fusion(f32[16,4,1,1]{0,2,3,1:T(1,128)S(1)} %copy.158, f32[16,4,64,128]{3,2,1,0:T(8,128)S(1)} %fusion.12), kind=kOutput, calls=%fused_computation.42 | convolution fusion | flops 6291456 | bytes 2228480 | tf_op jit(solution)/shard_map/dh,dhpn->hpn/dot_general | solution.py:159
  100.3 5.7 %collective-permute-start.3 = (f32[4,65,128]{2,0,1:T(4,128)S(1)}, f32[4,65,128]{2,0,1:T(4,128)S(1)}, u32[]{:S(2)}, u32[]{:S(2)}) collective-permute-start(f32[4,65,128]{2,0,1:T(4,128)S(1)} %pad_maximum_fusion.1), channel_id=1, source_target_pairs={{0,64},{32,96},{64,128},{96,160},{128,192},{160,224},{192,256},{22... | collective-permute-start | bytes 399368 | tf_op jit(solution)/shard_map/ppermute | solution.py:18
  109.5 7.4 %collective-permute-start.5 = (f32[4,65,128]{2,0,1:T(4,128)S(1)}, f32[4,65,128]{2,0,1:T(4,128)S(1)}, u32[]{:S(2)}, u32[]{:S(2)}) collective-permute-start(f32[4,65,128]{2,0,1:T(4,128)S(1)} %pad_maximum_fusion.2), channel_id=1, source_target_pairs={{0,64},{32,96},{64,128},{96,160},{128,192},{160,224},{192,256},{22... | collective-permute-start | bytes 399368 | tf_op jit(solution)/shard_map/ppermute | solution.py:18
  120.3 9.3 %collective-permute-start.6 = (f32[4,65,128]{2,0,1:T(4,128)S(1)}, f32[4,65,128]{2,0,1:T(4,128)S(1)}, u32[]{:S(2)}, u32[]{:S(2)}) collective-permute-start(f32[4,65,128]{2,0,1:T(4,128)S(1)} %pad_maximum_fusion.3), channel_id=1, source_target_pairs={{0,128},{32,160},{64,192},{96,224},{128,256},{160,288},{192,320},{... | collective-permute-start | bytes 399368 | tf_op jit(solution)/shard_map/ppermute | solution.py:18
  130.1 1.9 %collective-permute-done.6 = f32[4,65,128]{2,0,1:T(4,128)S(1)} collective-permute-done((f32[4,65,128]{2,0,1:T(4,128)S(1)}, f32[4,65,128]{2,0,1:T(4,128)S(1)}, u32[]{:S(2)}, u32[]{:S(2)}) %collective-permute-start.6) | collective-permute-done | bytes 133152 | tf_op jit(solution)/shard_map/ppermute | solution.py:18
  133.0 12.5 %collective-permute-start.7 = (f32[4,65,128]{2,0,1:T(4,128)S(1)}, f32[4,65,128]{2,0,1:T(4,128)S(1)}, u32[]{:S(2)}, u32[]{:S(2)}) collective-permute-start(f32[4,65,128]{2,0,1:T(4,128)S(1)} %pad_maximum_fusion.4), channel_id=1, source_target_pairs={{0,256},{32,288},{64,320},{96,352},{128,384},{160,416},{192,448},{... | collective-permute-start | bytes 399368 | tf_op jit(solution)/shard_map/ppermute | solution.py:18
  146.0 2.2 %copy.136 = f32[16,128,4]{1,2,0:T(4,128)} copy(f32[16,128,4]{2,0,1:T(8,128)} %copy-done.1) | data formatting | bytes 65536 | tf_op jit(solution)/shard_map/jit(cumsum)/reduce_window_sum | solution.py:133
  151.1 20.6 %collective-permute-start.8 = (f32[4,65,128]{2,0,1:T(4,128)S(1)}, f32[4,65,128]{2,0,1:T(4,128)S(1)}, u32[]{:S(2)}, u32[]{:S(2)}) collective-permute-start(f32[4,65,128]{2,0,1:T(4,128)S(1)} %pad_maximum_fusion.5), channel_id=1, source_target_pairs={{0,512},{32,544},{64,576},{96,608},{128,640},{160,672},{192,704},{... | collective-permute-start | bytes 399368 | tf_op jit(solution)/shard_map/ppermute | solution.py:18
  171.7 4.0 %fusion.10 = f32[16,4,64,128]{3,2,1,0:T(8,128)S(1)} fusion(bf16[16,128,4,64]{1,3,2,0:T(8,128)(2,1)} %copy.139, f32[16,128,4]{1,2,0:T(4,128)S(1)} %bitcast.77, f32[16,128,128]{2,1,0:T(8,128)} %fusion.103, f32[16,128,4]{1,2,0:T(4,128)} %copy.136, pred[128,128]{1,0:T(8,128)(4,1)S(1)} %iota_compare_fusion.1), kind=kOutput, calls=%fused_computation.25 | convolution fusion | flops 140509184 | bytes 4276224 | tf_op jit(solution)/shard_map/cijh,cjhp->cihp/dot_general | solution.py:141
  175.9 3.2 %bitcast_add_fusion = f32[16,4,64,128]{3,0,2,1:T(8,128)S(1)} fusion(f32[4,64,128]{2,1,0:T(8,128)S(1)} %copy.151, f32[16,4]{0,1:T(4,128)S(1)} %copy.150, f32[16,4,64,128]{3,2,1,0:T(8,128)S(1)} %fusion.12, f32[16,4]{0,1:T(4,128)S(1)} %copy.146, f32[16,4]{0,1:T(4,128)S(1)} %copy-done.9, pred[16,16]{1,0:T(8,128)(4,1)S(1)} %copy-done.10), kind=kOutput, calls=%fused_computation.32 | convolution fusion | flops 101714944 | bytes 4326400 | tf_op jit(solution)/shard_map/cdh,dhpn->chpn/dot_general | solution.py:157
  179.1 2.6 %fusion.15 = bf16[16,128,4,64]{1,3,2,0:T(8,128)(2,1)} fusion(bf16[16,128,4,64]{1,3,2,0:T(8,128)(2,1)S(1)} %copy-done.2, f32[16,4,64,128]{3,2,1,0:T(8,128)S(1)} %fusion.10, bf16[16,128,128,1]{2,1,3,0:T(8,128)(2,1)S(1)} %bitcast.73, f32[16,4,64,128]{3,0,2,1:T(8,128)S(1)} %bitcast_add_fusion, f32[4]{0:T(128)S(1)} %copy-done.14, f32[16,128,4]{1,2,0:T(4,128)S(1)} %copy.153), kind=kOutput, calls=%fused_computation.29 | convolution fusion | flops 405798912 | bytes 6848528 | tf_op jit(solution)/shard_map/cin,chpn->cihp/dot_general | solution.py:166
  181.8 2.9 %copy.161 = bf16[16,128,4,64]{3,2,1,0:T(4,128)(2,1)S(1)} copy(bf16[16,128,4,64]{1,3,2,0:T(8,128)(2,1)} %fusion.15) | data formatting | bytes 2097152 | tf_op jit(solution)/shard_map/convert_element_type | solution.py:170
  184.7 2.2 %reshape.217 = bf16[2048,256]{1,0:T(8,128)(2,1)} reshape(bf16[16,128,4,64]{3,2,1,0:T(4,128)(2,1)S(1)} %copy.161) | data formatting | bytes 2097152 | tf_op jit(solution)/shard_map/convert_element_type | solution.py:170
  (104 shorter events, 25.9 us)
Async XLA Ops:
  0.0 48.1 %copy-start = (bf16[384,1280]{1,0:T(8,128)(2,1)S(1)}, bf16[384,1280]{1,0:T(8,128)(2,1)}, u32[]{:S(2)}) copy-start(bf16[384,1280]{1,0:T(8,128)(2,1)} %param.14) | copy-start | bytes 2949124
  27.9 15.0 %collective-permute-start = (bf16[257,256]{1,0:T(8,128)(2,1)S(1)}, bf16[257,256]{1,0:T(8,128)(2,1)S(1)}, u32[]{:S(2)}, u32[]{:S(2)}) collective-permute-start(bf16[257,256]{1,0:T(8,128)(2,1)S(1)} %slice.103), channel_id=1, source_target_pairs={{0,32},{32,64},{64,96},{96,128},{128,160},{160,192},{192,224},{224... | collective-permute-start | bytes 394760 | tf_op jit(solution)/shard_map/ppermute | solution.py:18
  29.9 13.0 %collective-permute-start.1 = (bf16[256,256]{1,0:T(8,128)(2,1)}, bf16[256,256]{1,0:T(8,128)(2,1)S(1)}, u32[]{:S(2)}, u32[]{:S(2)}) collective-permute-start(bf16[256,256]{1,0:T(8,128)(2,1)} %slice.104), channel_id=1, source_target_pairs={{32,0},{64,32},{96,64},{128,96},{160,128},{192,160},{224,192},{256... | collective-permute-start | bytes 393224 | tf_op jit(solution)/shard_map/ppermute | solution.py:18
  36.8 11.0 %copy-start.1 = (f32[16,128,4]{2,0,1:T(8,128)}, f32[16,128,4]{2,0,1:T(8,128)S(1)}, u32[]{:S(2)}) copy-start(f32[16,128,4]{2,0,1:T(8,128)S(1)} %fusion.41) | copy-start | bytes 98308
  37.0 11.1 %copy-start.15 = (f32[1280]{0:T(1024)S(1)}, f32[1280]{0:T(1024)}, u32[]{:S(2)}) copy-start(f32[1280]{0:T(1024)} %param.15) | copy-start | bytes 15364
  38.7 4.1 %copy-start.12 = (f32[4]{0:T(128)}, f32[4]{0:T(128)S(1)}, u32[]{:S(2)}) copy-start(f32[4]{0:T(128)S(1)} %slice_bitcast_fusion) | copy-start | bytes 52
  69.0 17.9 %copy-start.11 = (f32[4,256]{1,0:T(4,128)S(1)}, f32[4,256]{1,0:T(4,128)}, u32[]{:S(2)}) copy-start(f32[4,256]{1,0:T(4,128)} %param.20) | copy-start | bytes 12292
  69.0 17.9 %copy-start.3 = (f32[16,128,4]{2,0,1:T(8,128)S(1)}, f32[16,128,4]{2,0,1:T(8,128)}, u32[]{:S(2)}) copy-start(f32[16,128,4]{2,0,1:T(8,128)} %get-tuple-element.22) | copy-start | bytes 98308
  81.2 6.4 %collective-permute-start.2 = (bf16[3,256]{1,0:T(4,128)(2,1)S(1)}, bf16[3,256]{1,0:T(4,128)(2,1)S(1)}, u32[]{:S(2)}, u32[]{:S(2)}) collective-permute-start(bf16[3,256]{1,0:T(4,128)(2,1)S(1)} %slice.107), channel_id=1, source_target_pairs={{0,32},{32,64},{64,96},{96,128},{128,160},{160,192},{192,224},{224... | collective-permute-start | bytes 4616 | tf_op jit(solution)/shard_map/ppermute | solution.py:18
  87.7 7.9 %copy-start.8 = (f32[4,2048]{1,0:T(4,128)S(1)}, f32[4,2048]{1,0:T(4,128)}, u32[]{:S(2)}) copy-start(f32[4,2048]{1,0:T(4,128)} %param.23) | copy-start | bytes 98308
  93.4 6.7 %copy-start.13 = (f32[4]{0:T(128)S(1)}, f32[4]{0:T(128)}, u32[]{:S(2)}) copy-start(f32[4]{0:T(128)} %copy-done.12) | copy-start | bytes 52
  95.6 21.4 %copy-start.5 = (bf16[2048,128]{1,0:T(8,128)(2,1)S(1)}, bf16[2048,128]{1,0:T(8,128)(2,1)}, u32[]{:S(2)}) copy-start(bf16[2048,128]{1,0:T(8,128)(2,1)} %param.21) | copy-start | bytes 1572868
  95.6 21.4 %copy-start.6 = (bf16[2048,128]{1,0:T(8,128)(2,1)S(1)}, bf16[2048,128]{1,0:T(8,128)(2,1)}, u32[]{:S(2)}) copy-start(bf16[2048,128]{1,0:T(8,128)(2,1)} %param.22) | copy-start | bytes 1572868
  100.3 8.9 %collective-permute-start.3 = (f32[4,65,128]{2,0,1:T(4,128)S(1)}, f32[4,65,128]{2,0,1:T(4,128)S(1)}, u32[]{:S(2)}, u32[]{:S(2)}) collective-permute-start(f32[4,65,128]{2,0,1:T(4,128)S(1)} %pad_maximum_fusion.1), channel_id=1, source_target_pairs={{0,64},{32,96},{64,128},{96,160},{128,192},{160,224},{192,256},{22... | collective-permute-start | bytes 399368 | tf_op jit(solution)/shard_map/ppermute | solution.py:18
  106.0 3.2 %collective-permute-start.4 = (f32[4,65,128]{2,0,1:T(4,128)S(1)}, f32[4,65,128]{2,0,1:T(4,128)S(1)}, u32[]{:S(2)}, u32[]{:S(2)}) collective-permute-start(f32[4,65,128]{2,0,1:T(4,128)S(1)} %pad_maximum_fusion.1), channel_id=1, source_target_pairs={{0,32},{32,64},{64,96},{96,128},{128,160},{160,192},{192,224},{224... | collective-permute-start | bytes 399368 | tf_op jit(solution)/shard_map/ppermute | solution.py:18
  109.5 10.4 %collective-permute-start.5 = (f32[4,65,128]{2,0,1:T(4,128)S(1)}, f32[4,65,128]{2,0,1:T(4,128)S(1)}, u32[]{:S(2)}, u32[]{:S(2)}) collective-permute-start(f32[4,65,128]{2,0,1:T(4,128)S(1)} %pad_maximum_fusion.2), channel_id=1, source_target_pairs={{0,64},{32,96},{64,128},{96,160},{128,192},{160,224},{192,256},{22... | collective-permute-start | bytes 399368 | tf_op jit(solution)/shard_map/ppermute | solution.py:18
  120.3 11.8 %collective-permute-start.6 = (f32[4,65,128]{2,0,1:T(4,128)S(1)}, f32[4,65,128]{2,0,1:T(4,128)S(1)}, u32[]{:S(2)}, u32[]{:S(2)}) collective-permute-start(f32[4,65,128]{2,0,1:T(4,128)S(1)} %pad_maximum_fusion.3), channel_id=1, source_target_pairs={{0,128},{32,160},{64,192},{96,224},{128,256},{160,288},{192,320},{... | collective-permute-start | bytes 399368 | tf_op jit(solution)/shard_map/ppermute | solution.py:18
  133.0 17.0 %collective-permute-start.7 = (f32[4,65,128]{2,0,1:T(4,128)S(1)}, f32[4,65,128]{2,0,1:T(4,128)S(1)}, u32[]{:S(2)}, u32[]{:S(2)}) collective-permute-start(f32[4,65,128]{2,0,1:T(4,128)S(1)} %pad_maximum_fusion.4), channel_id=1, source_target_pairs={{0,256},{32,288},{64,320},{96,352},{128,384},{160,416},{192,448},{... | collective-permute-start | bytes 399368 | tf_op jit(solution)/shard_map/ppermute | solution.py:18
  151.1 24.8 %copy-start.9 = (f32[16,4]{0,1:T(4,128)S(1)}, f32[16,4]{0,1:T(4,128)}, u32[]{:S(2)}) copy-start(f32[16,4]{0,1:T(4,128)} %fusion.62) | copy-start | bytes 772
  151.1 24.8 %copy-start.10 = (pred[16,16]{1,0:T(8,128)(4,1)S(1)}, pred[16,16]{1,0:T(8,128)(4,1)}, u32[]{:S(2)}) copy-start(pred[16,16]{1,0:T(8,128)(4,1)} %iota_compare_fusion.2) | copy-start | bytes 772
  151.1 24.7 %collective-permute-start.8 = (f32[4,65,128]{2,0,1:T(4,128)S(1)}, f32[4,65,128]{2,0,1:T(4,128)S(1)}, u32[]{:S(2)}, u32[]{:S(2)}) collective-permute-start(f32[4,65,128]{2,0,1:T(4,128)S(1)} %pad_maximum_fusion.5), channel_id=1, source_target_pairs={{0,512},{32,544},{64,576},{96,608},{128,640},{160,672},{192,704},{... | collective-permute-start | bytes 399368 | tf_op jit(solution)/shard_map/ppermute | solution.py:18
  175.7 3.4 %copy-start.2 = (bf16[16,128,4,64]{1,3,2,0:T(8,128)(2,1)S(1)}, bf16[16,128,4,64]{1,3,2,0:T(8,128)(2,1)}, u32[]{:S(2)}) copy-start(bf16[16,128,4,64]{1,3,2,0:T(8,128)(2,1)} %copy.139) | copy-start | bytes 3145732
  175.7 3.4 %copy-start.7 = (bf16[2048,128]{1,0:T(8,128)(2,1)S(1)}, bf16[2048,128]{1,0:T(8,128)(2,1)}, u32[]{:S(2)}) copy-start(bf16[2048,128]{1,0:T(8,128)(2,1)} %param.22) | copy-start | bytes 1572868
  175.7 3.4 %copy-start.14 = (f32[4]{0:T(128)S(1)}, f32[4]{0:T(128)}, u32[]{:S(2)}) copy-start(f32[4]{0:T(128)} %param.25) | copy-start | bytes 52
  (1 other events, 1.3 us)

commit v4 on v2

--- a/solution.py
+++ b/solution.py
@@ -43,22 +43,24 @@
         message = from_behind(pack(t, s), axis, d)
         return message[:, rows, 0], message[:, :rows]
 
-    window = jnp.zeros_like(total)
-    incoming = jnp.zeros_like(state)
-    width = 0
-    if count > 1:
-        t_one, s_one = received(total, state, 1)
-        window, incoming, width = t_one, s_one, 1
-    if count > 2:
-        t_two, s_two = received(total, state, 2)
-        incoming = s_two * jnp.exp(window)[:, None, None] + incoming
-        window = t_two + window
-        width = 2
-    while 0 < width < count:
-        t_far, s_far = received(window, incoming, width)
-        incoming = s_far * jnp.exp(window)[:, None, None] + incoming
-        window = t_far + window
-        width *= 2
+    window, incoming = total, state
+    width = 1
+    own = False
+    radix = 5
+    while width < count:
+        radix = min(radix, -(-count // width) + (0 if own else 1))
+        parts = [received(window, incoming, m * width) for m in range(radix - 1, 0, -1)]
+        if own:
+            parts.append((window, incoming))
+        window, incoming = parts[0]
+        for t_part, s_part in parts[1:]:
+            incoming = incoming * jnp.exp(t_part)[:, None, None] + s_part
+            window = window + t_part
+        width = width * (radix - 1) if not own else width * radix
+        own = True
+        radix = 4
+    if width == 1:
+        return jnp.zeros_like(state)
     return incoming
 
 

time: 168 us -> 193 us (1.15)
  the two profiles are of different devices: /device:TPU:132 before, /device:TPU:64 now
where the time goes in v4:
time: 193 us; the launch traced here: 192 us
  starting transfers between devices  94.1 us (49%)
  local copies, waits for them, and re-layouts  37.9 us (20%)
  waiting for transfers between devices  23.5 us (12%)
  matrix products  21.6 us (11%)
  other arithmetic  14.3 us (7%)
    ppermute x10, starting transfers between devices, from_behind(): return lax.ppermute(value, axis, pairs)  82.3 us
    all_to_all x1, waiting for transfers between devices, shards(): lax.all_to_all(projected, 'enc', split_axis=1, concat_axis=0, tiled=True)  16 us
    gather x1, local copies, waits for them, and re-layouts, shards(): jnp.take(widened, local_row, axis=0)  9.06 us
    unnamed x27, local copies, waits for them, and re-layouts  7.97 us
    all_to_all x1, starting transfers between devices, shards(): lax.all_to_all(projected, 'enc', split_axis=1, concat_axis=0, tiled=True)  6.21 us
    reshape x2, local copies, waits for them, and re-layouts, shards(): plain = mixed_in.reshape(blocks, SPAN, head_count, HDIM)  5.45 us
    convert_element_type x2, local copies, waits for them, and re-layouts, shards(): return output.reshape(row_count, head_count * HDIM).astype(jnp.bfloat16)  5.02 us
    ppermute x10, waiting for transfers between devices, from_behind(): return lax.ppermute(value, axis, pairs)  5.01 us
  transfers between devices with their start and end apart: 13, of which 5 were waited for; matrix products, arithmetic and copies ran while one was open for 13% of the time, Pallas kernels for 0%

profile of v4, /device:TPU:64, one launch (start us, length us, event | category | flops | bytes accessed | tf_op | source)
XLA Modules:
  0.0 191.9 jit_solution(13431844382823510300)
XLA Ops:
  1.0 3.5 %collective-permute-start = (bf16[1,128]{1,0:T(2,128)(2,1)S(1)}, bf16[1,128]{1,0:T(2,128)(2,1)S(1)}, u32[]{:S(2)}, u32[]{:S(2)}) collective-permute-start(bf16[1,128]{1,0:T(2,128)(2,1)S(1)} %slice.127), channel_id=1, source_target_pairs={{0,4},{4,8},{8,12},{12,16},{16,20},{20,24},{24,28},{28,32},{32,36}... | collective-permute-start | bytes 776 | tf_op jit(solution)/shard_map/ppermute | solution.py:18
  9.6 2.7 %fusion.138 = f32[16,128,128]{2,1,0:T(8,128)} fusion(bf16[16,128,128]{2,1,0:T(8,128)(2,1)} %bitcast.85, bf16[16,128,128]{2,1,0:T(8,128)(2,1)} %bitcast.83), kind=kOutput, calls=%fused_computation.196 | convolution fusion | flops 67108864 | bytes 2097152 | tf_op jit(solution)/shard_map/cin,cjn->cij/dot_general | solution.py:140
  12.4 7.1 %copy.172 = bf16[160,8,8,256]{3,1,2,0:T(8,128)(2,1)} copy(bf16[160,8,8,256]{3,2,1,0:T(8,128)(2,1)} %bitcast.81) | data formatting | bytes 10485760
  19.6 4.9 %convolution_convert_fusion = bf16[128,2048]{1,0:T(8,128)(2,1)S(1)} fusion(bf16[1280,2048]{1,0:T(8,128)(2,1)} %bitcast.82, bf16[384,1280]{1,0:T(8,128)(2,1)S(1)} %copy-done, f32[1280]{0:T(1024)S(1)} %copy-done.11, bf16[128,256]{1,0:T(8,128)(2,1)S(1)} %reshape.207, bf16[128,128]{1,0:T(8,128)(2,1)S(1)} %maximum_select_fusion), kind=kOutput, calls=%fused_computation.5 | convolution fusion | flops 808189952 | bytes 6853632 | tf_op jit(solution)/shard_map/dot_general | solution.py:97
  25.4 6.2 %all-to-all-start = ((bf16[128,8,256]{2,0,1:T(8,128)(2,1)}), bf16[128,8,256]{2,0,1:T(8,128)(2,1)}, u32[]{:S(2)}, u32[]{:S(2)}) async-start(bf16[128,8,256]{2,0,1:T(8,128)(2,1)} %bitcast.78), calls=%async_computation | async-start | bytes 1048576 | tf_op jit(solution)/shard_map/all_to_all | solution.py:101
  32.9 16.0 %all-to-all-done = bf16[128,8,256]{2,0,1:T(8,128)(2,1)} async-done(((bf16[128,8,256]{2,0,1:T(8,128)(2,1)}), bf16[128,8,256]{2,0,1:T(8,128)(2,1)}, u32[]{:S(2)}, u32[]{:S(2)}) %all-to-all-start) | async-done | bytes 524320 | tf_op jit(solution)/shard_map/all_to_all | solution.py:101
  51.8 3.6 %collective-permute-start.2 = (bf16[256,256]{1,0:T(8,128)(2,1)S(1)}, bf16[256,256]{1,0:T(8,128)(2,1)S(1)}, u32[]{:S(2)}, u32[]{:S(2)}) collective-permute-start(bf16[256,256]{1,0:T(8,128)(2,1)S(1)} %bitcast.93), channel_id=1, source_target_pairs={{32,0},{64,32},{96,64},{128,96},{160,128},{192,160},{224,192},{256... | collective-permute-start | bytes 393224 | tf_op jit(solution)/shard_map/ppermute | solution.py:29
  59.1 9.1 %gather_fusion = bf16[2048,256]{1,0:T(8,128)(2,1)} fusion(bf16[1536,256]{1,0:T(8,128)(2,1)S(1)} %pad_maximum_fusion.1, s32[2048]{0:T(1024)S(1)} %broadcast_clamp_fusion), kind=kCustom, calls=%fused_computation | custom fusion | bytes 2105344 | tf_op jit(solution)/shard_map/jit(_take)/gather | solution.py:117
  68.1 3.1 %select_select_fusion = bf16[2048,256]{1,0:T(8,128)(2,1)S(1)} fusion(bf16[2048,256]{1,0:T(8,128)(2,1)} %param.19, bf16[2048,256]{1,0:T(8,128)(2,1)} %gather_fusion, pred[2048]{0:T(1024)(128)(4,1)S(1)} %get-tuple-element.13, pred[2048]{0:T(1024)(128)(4,1)S(1)} %get-tuple-element.14), kind=kLoop, calls=%fused_computation.38 | loop fusion | flops 1048576 | bytes 3149824 | tf_op jit(solution)/shard_map/jit(_where)/select_n | solution.py:117
  71.3 4.7 %collective-permute-start.3 = (bf16[3,256]{1,0:T(4,128)(2,1)S(1)}, bf16[3,256]{1,0:T(4,128)(2,1)S(1)}, u32[]{:S(2)}, u32[]{:S(2)}) collective-permute-start(bf16[3,256]{1,0:T(4,128)(2,1)S(1)} %slice.131), channel_id=1, source_target_pairs={{0,32},{32,64},{64,96},{96,128},{128,160},{160,192},{192,224},{224... | collective-permute-start | bytes 4616 | tf_op jit(solution)/shard_map/ppermute | solution.py:18
  78.9 3.3 %reshape.229 = bf16[16,128,4,64]{3,2,1,0:T(4,128)(2,1)S(1)} reshape(bf16[2048,256]{1,0:T(8,128)(2,1)} %multiply_convert_fusion.2) | data formatting | bytes 2097152 | tf_op jit(solution)/shard_map/reshape | solution.py:128
  88.9 8.5 %collective-permute-start.4 = (f32[4,65,128]{2,0,1:T(4,128)S(1)}, f32[4,65,128]{2,0,1:T(4,128)S(1)}, u32[]{:S(2)}, u32[]{:S(2)}) collective-permute-start(f32[4,65,128]{2,0,1:T(4,128)S(1)} %pad_maximum_fusion.2), channel_id=1, source_target_pairs={{0,128},{32,160},{64,192},{96,224},{128,256},{160,288},{192,320},{... | collective-permute-start | bytes 399368 | tf_op jit(solution)/shard_map/ppermute | solution.py:18
  97.5 2.7 %collective-permute-start.5 = (f32[4,65,128]{2,0,1:T(4,128)S(1)}, f32[4,65,128]{2,0,1:T(4,128)S(1)}, u32[]{:S(2)}, u32[]{:S(2)}) collective-permute-start(f32[4,65,128]{2,0,1:T(4,128)S(1)} %pad_maximum_fusion.2), channel_id=1, source_target_pairs={{0,96},{32,128},{64,160},{96,192},{128,224},{160,256},{192,288},{2... | collective-permute-start | bytes 399368 | tf_op jit(solution)/shard_map/ppermute | solution.py:18
  100.2 4.4 %collective-permute-start.6 = (f32[4,65,128]{2,0,1:T(4,128)S(1)}, f32[4,65,128]{2,0,1:T(4,128)S(1)}, u32[]{:S(2)}, u32[]{:S(2)}) collective-permute-start(f32[4,65,128]{2,0,1:T(4,128)S(1)} %pad_maximum_fusion.2), channel_id=1, source_target_pairs={{0,64},{32,96},{64,128},{96,160},{128,192},{160,224},{192,256},{22... | collective-permute-start | bytes 399368 | tf_op jit(solution)/shard_map/ppermute | solution.py:18
  104.6 4.1 %collective-permute-start.7 = (f32[4,65,128]{2,0,1:T(4,128)S(1)}, f32[4,65,128]{2,0,1:T(4,128)S(1)}, u32[]{:S(2)}, u32[]{:S(2)}) collective-permute-start(f32[4,65,128]{2,0,1:T(4,128)S(1)} %pad_maximum_fusion.2), channel_id=1, source_target_pairs={{0,32},{32,64},{64,96},{96,128},{128,160},{160,192},{192,224},{224... | collective-permute-start | bytes 399368 | tf_op jit(solution)/shard_map/ppermute | solution.py:18
  112.4 8.4 %collective-permute-start.10 = (f32[4,65,128]{2,0,1:T(4,128)S(1)}, f32[4,65,128]{2,0,1:T(4,128)S(1)}, u32[]{:S(2)}, u32[]{:S(2)}) collective-permute-start(f32[4,65,128]{2,0,1:T(4,128)S(1)} %pad_maximum_fusion.3), channel_id=1, source_target_pairs={{0,128},{32,160},{64,192},{96,224},{128,256},{160,288},{192,320},{... | collective-permute-start | bytes 399368 | tf_op jit(solution)/shard_map/ppermute | solution.py:18
  120.8 10.3 %collective-permute-start.8 = (f32[4,65,128]{2,0,1:T(4,128)S(1)}, f32[4,65,128]{2,0,1:T(4,128)}, u32[]{:S(2)}, u32[]{:S(2)}) collective-permute-start(f32[4,65,128]{2,0,1:T(4,128)S(1)} %pad_maximum_fusion.3), channel_id=1, source_target_pairs={{0,384},{32,416},{64,448},{96,480},{128,512},{160,544},{192,576},{... | collective-permute-start | bytes 399368 | tf_op jit(solution)/shard_map/ppermute | solution.py:18
  131.1 6.8 %collective-permute-start.9 = (f32[4,65,128]{2,0,1:T(4,128)S(1)}, f32[4,65,128]{2,0,1:T(4,128)}, u32[]{:S(2)}, u32[]{:S(2)}) collective-permute-start(f32[4,65,128]{2,0,1:T(4,128)S(1)} %pad_maximum_fusion.3), channel_id=1, source_target_pairs={{0,256},{32,288},{64,320},{96,352},{128,384},{160,416},{192,448},{... | collective-permute-start | bytes 399368 | tf_op jit(solution)/shard_map/ppermute | solution.py:18
  145.3 28.9 %collective-permute-start.11 = (f32[4,65,128]{2,0,1:T(4,128)S(1)}, f32[4,65,128]{2,0,1:T(4,128)S(1)}, u32[]{:S(2)}, u32[]{:S(2)}) collective-permute-start(f32[4,65,128]{2,0,1:T(4,128)S(1)} %pad_maximum_fusion.4), channel_id=1, source_target_pairs={{0,512},{32,544},{64,576},{96,608},{128,640},{160,672},{192,704},{... | collective-permute-start | bytes 399368 | tf_op jit(solution)/shard_map/ppermute | solution.py:18
  174.2 3.8 %fusion = f32[16,4,64,128]{3,2,1,0:T(8,128)S(1)} fusion(bf16[16,128,4,64]{1,3,2,0:T(8,128)(2,1)} %copy.144, f32[16,128,4]{1,2,0:T(4,128)S(1)} %bitcast.91, f32[16,128,128]{2,1,0:T(8,128)} %fusion.138, f32[16,128,4]{1,2,0:T(4,128)} %copy.141, pred[128,128]{1,0:T(8,128)(4,1)S(1)} %iota_compare_fusion.1), kind=kOutput, calls=%fused_computation.6 | convolution fusion | flops 140509184 | bytes 4276224 | tf_op jit(solution)/shard_map/cijh,cjhp->cihp/dot_general | solution.py:144
  178.0 2.8 %collective-permute-done.11 = f32[4,65,128]{2,0,1:T(4,128)S(1)} collective-permute-done((f32[4,65,128]{2,0,1:T(4,128)S(1)}, f32[4,65,128]{2,0,1:T(4,128)S(1)}, u32[]{:S(2)}, u32[]{:S(2)}) %collective-permute-start.11) | collective-permute-done | bytes 133152 | tf_op jit(solution)/shard_map/ppermute | solution.py:18
  181.0 3.2 %bitcast_add_fusion = f32[16,4,64,128]{3,0,2,1:T(8,128)S(1)} fusion(f32[4,64,128]{2,1,0:T(8,128)S(1)} %copy.156, f32[16,4]{0,1:T(4,128)S(1)} %copy-done.5, f32[16,4,64,128]{3,2,1,0:T(8,128)S(1)} %fusion.2, f32[16,4]{0,1:T(4,128)S(1)} %copy.151, f32[16,4]{0,1:T(4,128)S(1)} %fusion.99, pred[16,16]{1,0:T(8,128)(4,1)S(1)} %copy-done.6), kind=kOutput, calls=%fused_computation.13 | convolution fusion | flops 101714944 | bytes 4326400 | tf_op jit(solution)/shard_map/cdh,dhpn->chpn/dot_general | solution.py:160
  184.3 2.6 %fusion.5 = bf16[16,128,4,64]{1,3,2,0:T(8,128)(2,1)} fusion(bf16[16,128,4,64]{1,3,2,0:T(8,128)(2,1)S(1)} %copy-done.2, f32[16,4,64,128]{3,2,1,0:T(8,128)S(1)} %fusion, bf16[16,128,128,1]{2,1,3,0:T(8,128)(2,1)S(1)} %bitcast.86, f32[16,4,64,128]{3,0,2,1:T(8,128)S(1)} %bitcast_add_fusion, f32[4]{0:T(128)S(1)} %copy-done.10, f32[16,128,4]{1,2,0:T(4,128)S(1)} %copy.158), kind=kOutput, calls=%fused_computation.10 | convolution fusion | flops 405798912 | bytes 6848528 | tf_op jit(solution)/shard_map/cin,chpn->cihp/dot_general | solution.py:169
  186.9 2.9 %copy.166 = bf16[16,128,4,64]{3,2,1,0:T(4,128)(2,1)S(1)} copy(bf16[16,128,4,64]{1,3,2,0:T(8,128)(2,1)} %fusion.5) | data formatting | bytes 2097152 | tf_op jit(solution)/shard_map/convert_element_type | solution.py:173
  (97 shorter events, 37.7 us)
Async XLA Ops:
  0.0 19.6 %copy-start = (bf16[384,1280]{1,0:T(8,128)(2,1)S(1)}, bf16[384,1280]{1,0:T(8,128)(2,1)}, u32[]{:S(2)}) copy-start(bf16[384,1280]{1,0:T(8,128)(2,1)} %param.14) | copy-start | bytes 2949124
  0.0 9.3 %copy-start.9 = (s32[64]{0:T(128)S(1)}, s32[64]{0:T(128)}, u32[]{:S(2)}) copy-start(s32[64]{0:T(128)} %param.17) | copy-start | bytes 772
  0.0 9.3 %copy-start.8 = (s32[64]{0:T(128)S(1)}, s32[64]{0:T(128)}, u32[]{:S(2)}) copy-start(s32[64]{0:T(128)} %param.18) | copy-start | bytes 772
  1.0 18.5 %collective-permute-start = (bf16[1,128]{1,0:T(2,128)(2,1)S(1)}, bf16[1,128]{1,0:T(2,128)(2,1)S(1)}, u32[]{:S(2)}, u32[]{:S(2)}) collective-permute-start(bf16[1,128]{1,0:T(2,128)(2,1)S(1)} %slice.127), channel_id=1, source_target_pairs={{0,4},{4,8},{8,12},{12,16},{16,20},{20,24},{24,28},{28,32},{32,36}... | collective-permute-start | bytes 776 | tf_op jit(solution)/shard_map/ppermute | solution.py:18
  9.0 22.5 %copy-start.1 = (f32[16,128,4]{2,0,1:T(8,128)}, f32[16,128,4]{2,0,1:T(8,128)S(1)}, u32[]{:S(2)}) copy-start(f32[16,128,4]{2,0,1:T(8,128)S(1)} %fusion.25) | copy-start | bytes 98308
  12.4 7.2 %copy-start.11 = (f32[1280]{0:T(1024)S(1)}, f32[1280]{0:T(1024)}, u32[]{:S(2)}) copy-start(f32[1280]{0:T(1024)} %param.15) | copy-start | bytes 15364
  25.4 23.5 %all-to-all-start = ((bf16[128,8,256]{2,0,1:T(8,128)(2,1)}), bf16[128,8,256]{2,0,1:T(8,128)(2,1)}, u32[]{:S(2)}, u32[]{:S(2)}) async-start(bf16[128,8,256]{2,0,1:T(8,128)(2,1)} %bitcast.78), calls=%async_computation | async-start | bytes 1048576 | tf_op jit(solution)/shard_map/all_to_all | solution.py:101
  49.9 6.3 %collective-permute-start.1 = (bf16[256,256]{1,0:T(8,128)(2,1)S(1)}, bf16[256,256]{1,0:T(8,128)(2,1)S(1)}, u32[]{:S(2)}, u32[]{:S(2)}) collective-permute-start(bf16[256,256]{1,0:T(8,128)(2,1)S(1)} %bitcast.94), channel_id=1, source_target_pairs={{0,32},{32,64},{64,96},{96,128},{128,160},{160,192},{192,224},{224... | collective-permute-start | bytes 393224 | tf_op jit(solution)/shard_map/ppermute | solution.py:26
  51.8 6.1 %collective-permute-start.2 = (bf16[256,256]{1,0:T(8,128)(2,1)S(1)}, bf16[256,256]{1,0:T(8,128)(2,1)S(1)}, u32[]{:S(2)}, u32[]{:S(2)}) collective-permute-start(bf16[256,256]{1,0:T(8,128)(2,1)S(1)} %bitcast.93), channel_id=1, source_target_pairs={{32,0},{64,32},{96,64},{128,96},{160,128},{192,160},{224,192},{256... | collective-permute-start | bytes 393224 | tf_op jit(solution)/shard_map/ppermute | solution.py:29
  68.1 7.9 %copy-start.7 = (f32[4,256]{1,0:T(4,128)S(1)}, f32[4,256]{1,0:T(4,128)}, u32[]{:S(2)}) copy-start(f32[4,256]{1,0:T(4,128)} %param.20) | copy-start | bytes 12292
  71.3 5.3 %collective-permute-start.3 = (bf16[3,256]{1,0:T(4,128)(2,1)S(1)}, bf16[3,256]{1,0:T(4,128)(2,1)S(1)}, u32[]{:S(2)}, u32[]{:S(2)}) collective-permute-start(bf16[3,256]{1,0:T(4,128)(2,1)S(1)} %slice.131), channel_id=1, source_target_pairs={{0,32},{32,64},{64,96},{96,128},{128,160},{160,192},{192,224},{224... | collective-permute-start | bytes 4616 | tf_op jit(solution)/shard_map/ppermute | solution.py:18
  88.9 19.8 %collective-permute-start.4 = (f32[4,65,128]{2,0,1:T(4,128)S(1)}, f32[4,65,128]{2,0,1:T(4,128)S(1)}, u32[]{:S(2)}, u32[]{:S(2)}) collective-permute-start(f32[4,65,128]{2,0,1:T(4,128)S(1)} %pad_maximum_fusion.2), channel_id=1, source_target_pairs={{0,128},{32,160},{64,192},{96,224},{128,256},{160,288},{192,320},{... | collective-permute-start | bytes 399368 | tf_op jit(solution)/shard_map/ppermute | solution.py:18
  97.5 11.3 %collective-permute-start.5 = (f32[4,65,128]{2,0,1:T(4,128)S(1)}, f32[4,65,128]{2,0,1:T(4,128)S(1)}, u32[]{:S(2)}, u32[]{:S(2)}) collective-permute-start(f32[4,65,128]{2,0,1:T(4,128)S(1)} %pad_maximum_fusion.2), channel_id=1, source_target_pairs={{0,96},{32,128},{64,160},{96,192},{128,224},{160,256},{192,288},{2... | collective-permute-start | bytes 399368 | tf_op jit(solution)/shard_map/ppermute | solution.py:18
  100.2 8.5 %collective-permute-start.6 = (f32[4,65,128]{2,0,1:T(4,128)S(1)}, f32[4,65,128]{2,0,1:T(4,128)S(1)}, u32[]{:S(2)}, u32[]{:S(2)}) collective-permute-start(f32[4,65,128]{2,0,1:T(4,128)S(1)} %pad_maximum_fusion.2), channel_id=1, source_target_pairs={{0,64},{32,96},{64,128},{96,160},{128,192},{160,224},{192,256},{22... | collective-permute-start | bytes 399368 | tf_op jit(solution)/shard_map/ppermute | solution.py:18
  104.6 6.3 %collective-permute-start.7 = (f32[4,65,128]{2,0,1:T(4,128)S(1)}, f32[4,65,128]{2,0,1:T(4,128)S(1)}, u32[]{:S(2)}, u32[]{:S(2)}) collective-permute-start(f32[4,65,128]{2,0,1:T(4,128)S(1)} %pad_maximum_fusion.2), channel_id=1, source_target_pairs={{0,32},{32,64},{64,96},{96,128},{128,160},{160,192},{192,224},{224... | collective-permute-start | bytes 399368 | tf_op jit(solution)/shard_map/ppermute | solution.py:18
  112.4 30.6 %collective-permute-start.10 = (f32[4,65,128]{2,0,1:T(4,128)S(1)}, f32[4,65,128]{2,0,1:T(4,128)S(1)}, u32[]{:S(2)}, u32[]{:S(2)}) collective-permute-start(f32[4,65,128]{2,0,1:T(4,128)S(1)} %pad_maximum_fusion.3), channel_id=1, source_target_pairs={{0,128},{32,160},{64,192},{96,224},{128,256},{160,288},{192,320},{... | collective-permute-start | bytes 399368 | tf_op jit(solution)/shard_map/ppermute | solution.py:18
  120.8 22.2 %collective-permute-start.8 = (f32[4,65,128]{2,0,1:T(4,128)S(1)}, f32[4,65,128]{2,0,1:T(4,128)}, u32[]{:S(2)}, u32[]{:S(2)}) collective-permute-start(f32[4,65,128]{2,0,1:T(4,128)S(1)} %pad_maximum_fusion.3), channel_id=1, source_target_pairs={{0,384},{32,416},{64,448},{96,480},{128,512},{160,544},{192,576},{... | collective-permute-start | bytes 399368 | tf_op jit(solution)/shard_map/ppermute | solution.py:18
  131.1 11.9 %collective-permute-start.9 = (f32[4,65,128]{2,0,1:T(4,128)S(1)}, f32[4,65,128]{2,0,1:T(4,128)}, u32[]{:S(2)}, u32[]{:S(2)}) collective-permute-start(f32[4,65,128]{2,0,1:T(4,128)S(1)} %pad_maximum_fusion.3), channel_id=1, source_target_pairs={{0,256},{32,288},{64,320},{96,352},{128,384},{160,416},{192,448},{... | collective-permute-start | bytes 399368 | tf_op jit(solution)/shard_map/ppermute | solution.py:18
  145.2 35.7 %copy-start.5 = (f32[16,4]{0,1:T(4,128)S(1)}, f32[16,4]{0,1:T(4,128)}, u32[]{:S(2)}) copy-start(f32[16,4]{0,1:T(4,128)} %copy.155) | copy-start | bytes 772
  145.3 35.7 %copy-start.6 = (pred[16,16]{1,0:T(8,128)(4,1)S(1)}, pred[16,16]{1,0:T(8,128)(4,1)}, u32[]{:S(2)}) copy-start(pred[16,16]{1,0:T(8,128)(4,1)} %iota_compare_fusion.2) | copy-start | bytes 772
  145.3 35.6 %collective-permute-start.11 = (f32[4,65,128]{2,0,1:T(4,128)S(1)}, f32[4,65,128]{2,0,1:T(4,128)S(1)}, u32[]{:S(2)}, u32[]{:S(2)}) collective-permute-start(f32[4,65,128]{2,0,1:T(4,128)S(1)} %pad_maximum_fusion.4), channel_id=1, source_target_pairs={{0,512},{32,544},{64,576},{96,608},{128,640},{160,672},{192,704},{... | collective-permute-start | bytes 399368 | tf_op jit(solution)/shard_map/ppermute | solution.py:18
  181.0 3.3 %copy-start.2 = (bf16[16,128,4,64]{1,3,2,0:T(8,128)(2,1)S(1)}, bf16[16,128,4,64]{1,3,2,0:T(8,128)(2,1)}, u32[]{:S(2)}) copy-start(bf16[16,128,4,64]{1,3,2,0:T(8,128)(2,1)} %copy.144) | copy-start | bytes 3145732
  181.0 3.3 %copy-start.3 = (bf16[2048,128]{1,0:T(8,128)(2,1)S(1)}, bf16[2048,128]{1,0:T(8,128)(2,1)}, u32[]{:S(2)}) copy-start(bf16[2048,128]{1,0:T(8,128)(2,1)} %param.22) | copy-start | bytes 1572868
  181.0 3.3 %copy-start.10 = (f32[4]{0:T(128)S(1)}, f32[4]{0:T(128)}, u32[]{:S(2)}) copy-start(f32[4]{0:T(128)} %param.25) | copy-start | bytes 52
  (1 other events, 2.2 us)

commit v5 on v1

--- a/solution.py
+++ b/solution.py
@@ -97,10 +97,16 @@
         tiles * enc_count, column_width
     )
     shard_audio = audio_rows.shape[0]
-    widened = padded_2(audio_rows, (("seq", 0),), DRIFT)
+    extra = 3
+    edge = DRIFT + extra
+    low_message = jnp.concatenate([audio_rows[shard_audio - edge :], text_embed[-extra:]], axis=0)
+    low_received = from_behind(low_message, "seq", 1)
+    high = from_behind(audio_rows[:DRIFT], "seq", -1)
+    widened = jnp.concatenate([low_received[:edge], audio_rows, high], axis=0)
+    text_behind = low_received[edge:]
     row_count = text_embed.shape[0]
     owner_index = lax.axis_index("seq")
-    places = owner_index * row_count + jnp.arange(row_count, dtype=jnp.int32)
+    places = owner_index * row_count - extra + jnp.arange(row_count + extra, dtype=jnp.int32)
     segment = jnp.sum((places[:, None] >= seg_offsets[None, :]).astype(jnp.int32), axis=1) - 1
     chosen = jnp.arange(seg_offsets.shape[0], dtype=jnp.int32)[None, :] == segment[:, None]
     offset_here = jnp.sum(jnp.where(chosen, seg_offsets[None, :], 0), axis=1)
@@ -108,11 +114,10 @@
     start_here = jnp.sum(jnp.where(chosen, seg_start[None, :], 0), axis=1)
     within = places - offset_here
     is_audio = (segment >= 0) & (within < length_here)
-    local_row = jnp.where(is_audio, start_here + within - owner_index * shard_audio + DRIFT, 0)
-    x_raw = jnp.where(is_audio[:, None], jnp.take(widened, local_row, axis=0), text_embed)
-    previous = from_behind(x_raw[-3:], "seq", 1)
-    padded = jnp.concatenate([previous, x_raw], axis=0)
-    summed_mix = jnp.zeros(x_raw.shape, jnp.float32)
+    local_row = jnp.where(is_audio, start_here + within - owner_index * shard_audio + edge, 0)
+    text_rows = jnp.concatenate([text_behind, text_embed], axis=0)
+    padded = jnp.where(is_audio[:, None], jnp.take(widened, local_row, axis=0), text_rows)
+    summed_mix = jnp.zeros((row_count, padded.shape[1]), jnp.float32)
     for offset in range(4):
         summed_mix = (
             summed_mix + padded[offset : offset + row_count].astype(jnp.float32) * mix_taps[offset]

time: 159 us -> 164 us (1.031)
  local copies, waits for them, and re-layouts: 33.1 us -> 40.7 us
  starting transfers between devices: 78.5 us -> 74.9 us
  waiting for transfers between devices: 20.3 us -> 16.8 us
  other arithmetic: 8.07 us -> 11.1 us
    ppermute x2 -> x0, waiting for transfers between devices: 3.78 us -> none  [the longest x1 3.77 us: padded_2(): lax.ppermute(lax.slice_in_dim(block, 0, width, axis=dim), axis, backward)]
    concatenate x0 -> x1, local copies, waits for them, and re-layouts: none -> 3.49 us  [shards(): widened = jnp.concatenate([low_received[:edge], audio_rows, high], axis=0)]
    ppermute x2 -> x0, starting transfers between devices: 3.32 us -> none  [the longest x1 2.03 us: padded_2(): lax.ppermute(lax.slice_in_dim(block, block.shape[dim] - width, None, axis...]
    slice x2 -> x4, local copies, waits for them, and re-layouts: 0.02 us -> 3.2 us  [the longest x1 1.56 us: shards(): high = from_behind(audio_rows[:DRIFT], 'seq', -1)]
    gather x1, local copies, waits for them, and re-layouts: 9.06 us -> 7.12 us  [shards(): jnp.take(widened, local_row, axis=0)]
    ppermute x13 -> x14, starting transfers between devices: 68.9 us -> 68.7 us  [from_behind(): return lax.ppermute(value, axis, pairs)]
    unnamed x27 -> x49, local copies, waits for them, and re-layouts: 8.04 us -> 8.09 us
  transfers between devices with their start and end apart: 16 -> 15, of which waited for: 3 -> 2; matrix products, arithmetic and copies ran while one was open for 29% -> 34% of each run, Pallas kernels for 0% -> 0%
where the time goes in v5:
time: 164 us; the launch traced here: 162 us
  starting transfers between devices  74.9 us (46%)
  local copies, waits for them, and re-layouts  40.7 us (25%)
  matrix products  17.7 us (11%)
  waiting for transfers between devices  16.8 us (10%)
  other arithmetic  11.1 us (7%)
    ppermute x14, starting transfers between devices, from_behind(): return lax.ppermute(value, axis, pairs)  68.7 us
    all_to_all x1, waiting for transfers between devices, shards(): lax.all_to_all(projected, 'enc', split_axis=1, concat_axis=0, tiled=True)  14.9 us
    unnamed x49, local copies, waits for them, and re-layouts  8.09 us
    gather x1, local copies, waits for them, and re-layouts, shards(): jnp.take(widened, local_row, axis=0)  7.12 us
    all_to_all x1, starting transfers between devices, shards(): lax.all_to_all(projected, 'enc', split_axis=1, concat_axis=0, tiled=True)  6.21 us
    dot_general x1, matrix products, shards(): jnp.dot(features, projector.reshape(projector.shape[0], -1), preferred_el...  5.71 us
    convert_element_type x2, local copies, waits for them, and re-layouts, shards(): return output.reshape(row_count, head_count * HDIM).astype(jnp.bfloat16)  5.02 us
    reshape x2, local copies, waits for them, and re-layouts, shards(): plain = mixed_in.reshape(blocks, SPAN, head_count, HDIM)  4.71 us
  transfers between devices with their start and end apart: 15, of which 2 were waited for; matrix products, arithmetic and copies ran while one was open for 34% of the time, Pallas kernels for 0%

profile of v5, /device:TPU:6, one launch (start us, length us, event | category | flops | bytes accessed | tf_op | source)
XLA Modules:
  0.0 162.0 jit_solution(1228455761371586230)
XLA Ops:
  3.1 2.2 %collective-permute-start.5 = (f32[4]{0:T(128)}, f32[4]{0:T(128)}, u32[]{:S(2)}, u32[]{:S(2)}) collective-permute-start(f32[4]{0:T(128)} %slice_bitcast_fusion), channel_id=1, source_target_pairs={{0,32},{32,64},{64,96},{96,128},{128,160},{160,192},{192,224},{224... | collective-permute-start | bytes 56 | tf_op jit(solution)/shard_map/ppermute | solution.py:18
  5.3 4.5 %collective-permute-start.7 = (f32[4]{0:T(128)}, f32[4]{0:T(128)}, u32[]{:S(2)}, u32[]{:S(2)}) collective-permute-start(f32[4]{0:T(128)} %slice_bitcast_fusion), channel_id=1, source_target_pairs={{0,64},{32,96},{64,128},{96,160},{128,192},{160,224},{192,256},{22... | collective-permute-start | bytes 56 | tf_op jit(solution)/shard_map/ppermute | solution.py:18
  9.9 3.5 %collective-permute-start = (bf16[1,128]{1,0:T(2,128)(2,1)S(1)}, bf16[1,128]{1,0:T(2,128)(2,1)S(1)}, u32[]{:S(2)}, u32[]{:S(2)}) collective-permute-start(bf16[1,128]{1,0:T(2,128)(2,1)S(1)} %slice.75), channel_id=1, source_target_pairs={{0,4},{4,8},{8,12},{12,16},{16,20},{20,24},{24,28},{28,32},{32,36}... | collective-permute-start | bytes 776 | tf_op jit(solution)/shard_map/ppermute | solution.py:18
  16.3 7.1 %copy.139 = bf16[160,8,8,256]{3,1,2,0:T(8,128)(2,1)} copy(bf16[160,8,8,256]{3,2,1,0:T(8,128)(2,1)} %bitcast.76) | data formatting | bytes 10485760
  24.1 5.7 %convolution_convert_fusion = bf16[128,2048]{1,0:T(8,128)(2,1)} fusion(bf16[1280,2048]{1,0:T(8,128)(2,1)} %bitcast.77, bf16[384,1280]{1,0:T(8,128)(2,1)S(1)} %copy-done, f32[1280]{0:T(1024)S(1)} %copy-done.22, bf16[128,256]{1,0:T(8,128)(2,1)S(1)} %reshape.204, bf16[128,128]{1,0:T(8,128)(2,1)S(1)} %maximum_select_fusion.1), kind=kOutput, calls=%fused_computation.5 | convolution fusion | flops 808189952 | bytes 6853632 | tf_op jit(solution)/shard_map/dot_general | solution.py:92
  31.8 6.2 %all-to-all-start = ((bf16[128,8,256]{2,0,1:T(8,128)(2,1)}), bf16[128,8,256]{2,0,1:T(8,128)(2,1)}, u32[]{:S(2)}, u32[]{:S(2)}) async-start(bf16[128,8,256]{2,0,1:T(8,128)(2,1)} %bitcast.73), calls=%async_computation | async-start | bytes 1048576 | tf_op jit(solution)/shard_map/all_to_all | solution.py:96
  42.1 14.9 %all-to-all-done = bf16[128,8,256]{2,0,1:T(8,128)(2,1)} async-done(((bf16[128,8,256]{2,0,1:T(8,128)(2,1)}), bf16[128,8,256]{2,0,1:T(8,128)(2,1)}, u32[]{:S(2)}, u32[]{:S(2)}) %all-to-all-start) | async-done | bytes 524320 | tf_op jit(solution)/shard_map/all_to_all | solution.py:96
  68.1 3.5 %concatenate.18 = bf16[1539,256]{1,0:T(8,128)(2,1)S(1)} concatenate(bf16[259,256]{1,0:T(8,128)(2,1)S(1)} %bitcast.84, bf16[1024,256]{1,0:T(8,128)(2,1)} %bitcast.3, bf16[256,256]{1,0:T(8,128)(2,1)S(1)} %collective-permute-done.2), dimensions={0} | concatenate | bytes 1575936 | tf_op jit(solution)/shard_map/concatenate | solution.py:105
  71.6 7.1 %gather_fusion = bf16[2051,256]{1,0:T(8,128)(2,1)S(1)} fusion(bf16[1539,256]{1,0:T(8,128)(2,1)S(1)} %concatenate.18, s32[3072]{0:T(1024)} %pad_clamp_fusion), kind=kCustom, calls=%fused_computation | custom fusion | bytes 2108428 | tf_op jit(solution)/shard_map/jit(_take)/gather | solution.py:119
  78.8 3.0 %maximum_select_fusion = bf16[2051,256]{1,0:T(8,128)(2,1)S(1)} fusion(bf16[2048,256]{1,0:T(8,128)(2,1)} %param.19, bf16[3,256]{1,0:T(4,128)(2,1)S(1)} %slice.80, bf16[2051,256]{1,0:T(8,128)(2,1)S(1)} %gather_fusion, pred[2051]{0:T(1024)(128)(4,1)S(1)} %get-tuple-element.14, pred[2051]{0:T(1024)(128)(4,1)S(1)} %copy-done.9), kind=kLoop, calls=%fused_computation.27 | loop fusion | flops 3150336 | bytes 3154438 | tf_op jit(solution)/shard_map/jit(_where)/select_n | solution.py:119
  85.0 2.9 %copy.112 = bf16[16,128,4,64]{1,3,2,0:T(8,128)(2,1)S(1)} copy(bf16[16,128,4,64]{3,2,1,0:T(4,128)(2,1)} %reshape.226) | data formatting | bytes 2097152 | tf_op jit(solution)/shard_map/reshape | solution.py:128
  88.7 2.2 %fusion.15 = f32[4,1,64,128]{3,1,2,0:T(1,128)S(1)} fusion(f32[16,4,1,1]{0,2,3,1:T(1,128)S(1)} %copy-done.12, f32[16,4,64,128]{3,2,1,0:T(8,128)S(1)} %fusion.2), kind=kOutput, calls=%fused_computation.23 | convolution fusion | flops 6291456 | bytes 2228480 | tf_op jit(solution)/shard_map/dh,dhpn->hpn/dot_general | solution.py:163
  91.0 4.3 %collective-permute-start.3 = (bf16[4,64,128]{2,1,0:T(8,128)(2,1)S(1)}, bf16[4,64,128]{2,1,0:T(8,128)(2,1)S(1)}, u32[]{:S(2)}, u32[]{:S(2)}) collective-permute-start(bf16[4,64,128]{2,1,0:T(8,128)(2,1)S(1)} %convert_element_type.82), channel_id=1, source_target_pairs={{0,32},{32,64},{64,96},{96,128},{128,160},{160,192},{192,224},{224... | collective-permute-start | bytes 196616 | tf_op jit(solution)/shard_map/ppermute | solution.py:18
  95.4 3.5 %collective-permute-start.4 = (bf16[4,64,128]{2,1,0:T(8,128)(2,1)S(1)}, bf16[4,64,128]{2,1,0:T(8,128)(2,1)S(1)}, u32[]{:S(2)}, u32[]{:S(2)}) collective-permute-start(bf16[4,64,128]{2,1,0:T(8,128)(2,1)S(1)} %convert_element_type.82), channel_id=1, source_target_pairs={{0,64},{32,96},{64,128},{96,160},{128,192},{160,224},{192,256},{22... | collective-permute-start | bytes 196616 | tf_op jit(solution)/shard_map/ppermute | solution.py:18
  99.6 6.2 %collective-permute-start.9 = (f32[4]{0:T(128)S(1)}, f32[4]{0:T(128)S(1)}, u32[]{:S(2)}, u32[]{:S(2)}) collective-permute-start(f32[4]{0:T(128)S(1)} %get-tuple-element.11), channel_id=1, source_target_pairs={{0,64},{32,96},{64,128},{96,160},{128,192},{160,224},{192,256},{22... | collective-permute-start | bytes 56 | tf_op jit(solution)/shard_map/ppermute | solution.py:18
  106.0 4.8 %collective-permute-start.6 = (bf16[4,64,128]{2,1,0:T(8,128)(2,1)S(1)}, bf16[4,64,128]{2,1,0:T(8,128)(2,1)S(1)}, u32[]{:S(2)}, u32[]{:S(2)}) collective-permute-start(bf16[4,64,128]{2,1,0:T(8,128)(2,1)S(1)} %fusion.68), channel_id=1, source_target_pairs={{0,64},{32,96},{64,128},{96,160},{128,192},{160,224},{192,256},{22... | collective-permute-start | bytes 196616 | tf_op jit(solution)/shard_map/ppermute | solution.py:18
  110.8 4.8 %collective-permute-start.11 = (f32[4]{0:T(128)S(1)}, f32[4]{0:T(128)S(1)}, u32[]{:S(2)}, u32[]{:S(2)}) collective-permute-start(f32[4]{0:T(128)S(1)} %get-tuple-element.13), channel_id=1, source_target_pairs={{0,128},{32,160},{64,192},{96,224},{128,256},{160,288},{192,320},{... | collective-permute-start | bytes 56 | tf_op jit(solution)/shard_map/ppermute | solution.py:18
  115.7 7.6 %collective-permute-start.8 = (bf16[4,64,128]{2,1,0:T(8,128)(2,1)S(1)}, bf16[4,64,128]{2,1,0:T(8,128)(2,1)S(1)}, u32[]{:S(2)}, u32[]{:S(2)}) collective-permute-start(bf16[4,64,128]{2,1,0:T(8,128)(2,1)S(1)} %fusion.126), channel_id=1, source_target_pairs={{0,128},{32,160},{64,192},{96,224},{128,256},{160,288},{192,320},{... | collective-permute-start | bytes 196616 | tf_op jit(solution)/shard_map/ppermute | solution.py:18
  123.3 6.1 %collective-permute-start.13 = (f32[4]{0:T(128)S(1)}, f32[4]{0:T(128)S(1)}, u32[]{:S(2)}, u32[]{:S(2)}) collective-permute-start(f32[4]{0:T(128)S(1)} %get-tuple-element.9), channel_id=1, source_target_pairs={{0,256},{32,288},{64,320},{96,352},{128,384},{160,416},{192,448},{... | collective-permute-start | bytes 56 | tf_op jit(solution)/shard_map/ppermute | solution.py:18
  129.6 5.5 %collective-permute-start.10 = (bf16[4,64,128]{2,1,0:T(8,128)(2,1)S(1)}, bf16[4,64,128]{2,1,0:T(8,128)(2,1)S(1)}, u32[]{:S(2)}, u32[]{:S(2)}) collective-permute-start(bf16[4,64,128]{2,1,0:T(8,128)(2,1)S(1)} %fusion.75), channel_id=1, source_target_pairs={{0,256},{32,288},{64,320},{96,352},{128,384},{160,416},{192,448},{... | collective-permute-start | bytes 196616 | tf_op jit(solution)/shard_map/ppermute | solution.py:18
  137.1 12.1 %collective-permute-start.12 = (bf16[4,64,128]{2,1,0:T(8,128)(2,1)S(1)}, bf16[4,64,128]{2,1,0:T(8,128)(2,1)S(1)}, u32[]{:S(2)}, u32[]{:S(2)}) collective-permute-start(bf16[4,64,128]{2,1,0:T(8,128)(2,1)S(1)} %fusion.125), channel_id=1, source_target_pairs={{0,512},{32,544},{64,576},{96,608},{128,640},{160,672},{192,704},{... | collective-permute-start | bytes 196616 | tf_op jit(solution)/shard_map/ppermute | solution.py:18
  151.1 3.2 %bitcast_add_fusion = f32[16,4,64,128]{3,0,2,1:T(8,128)S(1)} fusion(f32[4,64,128]{2,1,0:T(8,128)S(1)} %multiply_add_fusion, f32[16,4]{0,1:T(4,128)S(1)} %copy-done.11, f32[16,4,64,128]{3,2,1,0:T(8,128)S(1)} %fusion.2, f32[16,4]{0,1:T(4,128)S(1)} %copy.119, f32[16,4]{0,1:T(4,128)S(1)} %copy-done.10, pred[16,16]{1,0:T(8,128)(4,1)S(1)} %copy-done.13), kind=kOutput, calls=%fused_computation.13 | convolution fusion | flops 101714944 | bytes 4326400 | tf_op jit(solution)/shard_map/cdh,dhpn->chpn/dot_general | solution.py:160
  154.3 2.6 %fusion.5 = bf16[16,128,4,64]{1,3,2,0:T(8,128)(2,1)} fusion(bf16[16,128,4,64]{1,3,2,0:T(8,128)(2,1)S(1)} %copy.112, f32[16,4,64,128]{3,2,1,0:T(8,128)S(1)} %fusion, bf16[16,128,128,1]{2,1,3,0:T(8,128)(2,1)S(1)} %bitcast.81, f32[16,4,64,128]{3,0,2,1:T(8,128)S(1)} %bitcast_add_fusion, f32[4]{0:T(128)S(1)} %copy-done.21, f32[16,128,4]{1,2,0:T(4,128)S(1)} %copy.125), kind=kOutput, calls=%fused_computation.10 | convolution fusion | flops 405798912 | bytes 6848528 | tf_op jit(solution)/shard_map/cin,chpn->cihp/dot_general | solution.py:170
  157.0 2.9 %copy.133 = bf16[16,128,4,64]{3,2,1,0:T(4,128)(2,1)S(1)} copy(bf16[16,128,4,64]{1,3,2,0:T(8,128)(2,1)} %fusion.5) | data formatting | bytes 2097152 | tf_op jit(solution)/shard_map/convert_element_type | solution.py:174
  (122 shorter events, 34.8 us)
Async XLA Ops:
  0.0 24.1 %copy-start = (bf16[384,1280]{1,0:T(8,128)(2,1)S(1)}, bf16[384,1280]{1,0:T(8,128)(2,1)}, u32[]{:S(2)}) copy-start(bf16[384,1280]{1,0:T(8,128)(2,1)} %param.14) | copy-start | bytes 2949124
  0.0 13.5 %copy-start.20 = (s32[64]{0:T(128)S(1)}, s32[64]{0:T(128)}, u32[]{:S(2)}) copy-start(s32[64]{0:T(128)} %param.17) | copy-start | bytes 772
  0.0 13.6 %copy-start.19 = (s32[64]{0:T(128)S(1)}, s32[64]{0:T(128)}, u32[]{:S(2)}) copy-start(s32[64]{0:T(128)} %param.18) | copy-start | bytes 772
  0.0 15.1 %copy-start.18 = (f32[4,256]{1,0:T(4,128)S(1)}, f32[4,256]{1,0:T(4,128)}, u32[]{:S(2)}) copy-start(f32[4,256]{1,0:T(4,128)} %param.20) | copy-start | bytes 12292
  3.1 95.9 %collective-permute-start.5 = (f32[4]{0:T(128)}, f32[4]{0:T(128)}, u32[]{:S(2)}, u32[]{:S(2)}) collective-permute-start(f32[4]{0:T(128)} %slice_bitcast_fusion), channel_id=1, source_target_pairs={{0,32},{32,64},{64,96},{96,128},{128,160},{160,192},{192,224},{224... | collective-permute-start | bytes 56 | tf_op jit(solution)/shard_map/ppermute | solution.py:18
  5.3 93.6 %collective-permute-start.7 = (f32[4]{0:T(128)}, f32[4]{0:T(128)}, u32[]{:S(2)}, u32[]{:S(2)}) collective-permute-start(f32[4]{0:T(128)} %slice_bitcast_fusion), channel_id=1, source_target_pairs={{0,64},{32,96},{64,128},{96,160},{128,192},{160,224},{192,256},{22... | collective-permute-start | bytes 56 | tf_op jit(solution)/shard_map/ppermute | solution.py:18
  9.9 14.1 %collective-permute-start = (bf16[1,128]{1,0:T(2,128)(2,1)S(1)}, bf16[1,128]{1,0:T(2,128)(2,1)S(1)}, u32[]{:S(2)}, u32[]{:S(2)}) collective-permute-start(bf16[1,128]{1,0:T(2,128)(2,1)S(1)} %slice.75), channel_id=1, source_target_pairs={{0,4},{4,8},{8,12},{12,16},{16,20},{20,24},{24,28},{28,32},{32,36}... | collective-permute-start | bytes 776 | tf_op jit(solution)/shard_map/ppermute | solution.py:18
  31.8 25.2 %all-to-all-start = ((bf16[128,8,256]{2,0,1:T(8,128)(2,1)}), bf16[128,8,256]{2,0,1:T(8,128)(2,1)}, u32[]{:S(2)}, u32[]{:S(2)}) async-start(bf16[128,8,256]{2,0,1:T(8,128)(2,1)} %bitcast.73), calls=%async_computation | async-start | bytes 1048576 | tf_op jit(solution)/shard_map/all_to_all | solution.py:96
  57.9 10.1 %collective-permute-start.1 = (bf16[262,256]{1,0:T(8,128)(2,1)S(1)}, bf16[262,256]{1,0:T(8,128)(2,1)S(1)}, u32[]{:S(2)}, u32[]{:S(2)}) collective-permute-start(bf16[262,256]{1,0:T(8,128)(2,1)S(1)} %pad_maximum_fusion), channel_id=1, source_target_pairs={{0,32},{32,64},{64,96},{96,128},{128,160},{160,192},{192,224},{224... | collective-permute-start | bytes 402440 | tf_op jit(solution)/shard_map/ppermute | solution.py:18
  61.5 6.5 %collective-permute-start.2 = (bf16[256,256]{1,0:T(8,128)(2,1)}, bf16[256,256]{1,0:T(8,128)(2,1)S(1)}, u32[]{:S(2)}, u32[]{:S(2)}) collective-permute-start(bf16[256,256]{1,0:T(8,128)(2,1)} %bitcast.5), channel_id=1, source_target_pairs={{32,0},{64,32},{96,64},{128,96},{160,128},{192,160},{224,192},{256... | collective-permute-start | bytes 393224 | tf_op jit(solution)/shard_map/ppermute | solution.py:18
  88.7 60.5 %copy-start.5 = (f32[16,128,128]{2,1,0:T(8,128)S(1)}, f32[16,128,128]{2,1,0:T(8,128)}, u32[]{:S(2)}) copy-start(f32[16,128,128]{2,1,0:T(8,128)} %fusion.132) | copy-start | bytes 3145732
  88.7 60.5 %copy-start.8 = (f32[16,128,4]{1,2,0:T(4,128)S(1)}, f32[16,128,4]{1,2,0:T(4,128)}, u32[]{:S(2)}) copy-start(f32[16,128,4]{1,2,0:T(4,128)} %copy.109) | copy-start | bytes 98308
  91.0 14.8 %collective-permute-start.3 = (bf16[4,64,128]{2,1,0:T(8,128)(2,1)S(1)}, bf16[4,64,128]{2,1,0:T(8,128)(2,1)S(1)}, u32[]{:S(2)}, u32[]{:S(2)}) collective-permute-start(bf16[4,64,128]{2,1,0:T(8,128)(2,1)S(1)} %convert_element_type.82), channel_id=1, source_target_pairs={{0,32},{32,64},{64,96},{96,128},{128,160},{160,192},{192,224},{224... | collective-permute-start | bytes 196616 | tf_op jit(solution)/shard_map/ppermute | solution.py:18
  95.4 10.5 %collective-permute-start.4 = (bf16[4,64,128]{2,1,0:T(8,128)(2,1)S(1)}, bf16[4,64,128]{2,1,0:T(8,128)(2,1)S(1)}, u32[]{:S(2)}, u32[]{:S(2)}) collective-permute-start(bf16[4,64,128]{2,1,0:T(8,128)(2,1)S(1)} %convert_element_type.82), channel_id=1, source_target_pairs={{0,64},{32,96},{64,128},{96,160},{128,192},{160,224},{192,256},{22... | collective-permute-start | bytes 196616 | tf_op jit(solution)/shard_map/ppermute | solution.py:18
  99.6 11.2 %collective-permute-start.9 = (f32[4]{0:T(128)S(1)}, f32[4]{0:T(128)S(1)}, u32[]{:S(2)}, u32[]{:S(2)}) collective-permute-start(f32[4]{0:T(128)S(1)} %get-tuple-element.11), channel_id=1, source_target_pairs={{0,64},{32,96},{64,128},{96,160},{128,192},{160,224},{192,256},{22... | collective-permute-start | bytes 56 | tf_op jit(solution)/shard_map/ppermute | solution.py:18
  106.0 9.7 %collective-permute-start.6 = (bf16[4,64,128]{2,1,0:T(8,128)(2,1)S(1)}, bf16[4,64,128]{2,1,0:T(8,128)(2,1)S(1)}, u32[]{:S(2)}, u32[]{:S(2)}) collective-permute-start(bf16[4,64,128]{2,1,0:T(8,128)(2,1)S(1)} %fusion.68), channel_id=1, source_target_pairs={{0,64},{32,96},{64,128},{96,160},{128,192},{160,224},{192,256},{22... | collective-permute-start | bytes 196616 | tf_op jit(solution)/shard_map/ppermute | solution.py:18
  110.8 12.5 %collective-permute-start.11 = (f32[4]{0:T(128)S(1)}, f32[4]{0:T(128)S(1)}, u32[]{:S(2)}, u32[]{:S(2)}) collective-permute-start(f32[4]{0:T(128)S(1)} %get-tuple-element.13), channel_id=1, source_target_pairs={{0,128},{32,160},{64,192},{96,224},{128,256},{160,288},{192,320},{... | collective-permute-start | bytes 56 | tf_op jit(solution)/shard_map/ppermute | solution.py:18
  115.7 13.7 %collective-permute-start.8 = (bf16[4,64,128]{2,1,0:T(8,128)(2,1)S(1)}, bf16[4,64,128]{2,1,0:T(8,128)(2,1)S(1)}, u32[]{:S(2)}, u32[]{:S(2)}) collective-permute-start(bf16[4,64,128]{2,1,0:T(8,128)(2,1)S(1)} %fusion.126), channel_id=1, source_target_pairs={{0,128},{32,160},{64,192},{96,224},{128,256},{160,288},{192,320},{... | collective-permute-start | bytes 196616 | tf_op jit(solution)/shard_map/ppermute | solution.py:18
  123.3 11.7 %collective-permute-start.13 = (f32[4]{0:T(128)S(1)}, f32[4]{0:T(128)S(1)}, u32[]{:S(2)}, u32[]{:S(2)}) collective-permute-start(f32[4]{0:T(128)S(1)} %get-tuple-element.9), channel_id=1, source_target_pairs={{0,256},{32,288},{64,320},{96,352},{128,384},{160,416},{192,448},{... | collective-permute-start | bytes 56 | tf_op jit(solution)/shard_map/ppermute | solution.py:18
  129.6 7.4 %collective-permute-start.10 = (bf16[4,64,128]{2,1,0:T(8,128)(2,1)S(1)}, bf16[4,64,128]{2,1,0:T(8,128)(2,1)S(1)}, u32[]{:S(2)}, u32[]{:S(2)}) collective-permute-start(bf16[4,64,128]{2,1,0:T(8,128)(2,1)S(1)} %fusion.75), channel_id=1, source_target_pairs={{0,256},{32,288},{64,320},{96,352},{128,384},{160,416},{192,448},{... | collective-permute-start | bytes 196616 | tf_op jit(solution)/shard_map/ppermute | solution.py:18
  137.1 13.9 %copy-start.10 = (f32[16,4]{0,1:T(4,128)S(1)}, f32[16,4]{0,1:T(4,128)}, u32[]{:S(2)}) copy-start(f32[16,4]{0,1:T(4,128)} %fusion.90) | copy-start | bytes 772
  137.1 13.9 %copy-start.11 = (f32[16,4]{0,1:T(4,128)S(1)}, f32[16,4]{0,1:T(4,128)}, u32[]{:S(2)}) copy-start(f32[16,4]{0,1:T(4,128)} %copy.123) | copy-start | bytes 772
  137.1 13.9 %copy-start.13 = (pred[16,16]{1,0:T(8,128)(4,1)S(1)}, pred[16,16]{1,0:T(8,128)(4,1)}, u32[]{:S(2)}) copy-start(pred[16,16]{1,0:T(8,128)(4,1)} %iota_compare_fusion.2) | copy-start | bytes 772
  137.1 13.7 %collective-permute-start.12 = (bf16[4,64,128]{2,1,0:T(8,128)(2,1)S(1)}, bf16[4,64,128]{2,1,0:T(8,128)(2,1)S(1)}, u32[]{:S(2)}, u32[]{:S(2)}) collective-permute-start(bf16[4,64,128]{2,1,0:T(8,128)(2,1)S(1)} %fusion.125), channel_id=1, source_target_pairs={{0,512},{32,544},{64,576},{96,608},{128,640},{160,672},{192,704},{... | collective-permute-start | bytes 196616 | tf_op jit(solution)/shard_map/ppermute | solution.py:18
  (14 other events, 69.2 us)

commit v6 on v5

--- a/solution.py
+++ b/solution.py
@@ -89,10 +89,9 @@
     summed = jnp.dot(stacked, conv_weight, preferred_element_type=jnp.float32) + conv_bias
     features = jax.nn.gelu(summed, approximate=False).astype(jnp.bfloat16)
     column_width = projector.shape[2]
-    projected = jnp.dot(
-        features, projector.reshape(projector.shape[0], -1), preferred_element_type=jnp.float32
-    )
-    projected = projected.astype(jnp.bfloat16).reshape(tiles, enc_count, column_width)
+    projected = jnp.einsum(
+        "cbk,tc->btk", projector, features, preferred_element_type=jnp.float32
+    ).astype(jnp.bfloat16).transpose(1, 0, 2)
     audio_rows = lax.all_to_all(projected, "enc", split_axis=1, concat_axis=0, tiled=True).reshape(
         tiles * enc_count, column_width
     )

time: 164 us -> 155 us (0.945)
  local copies, waits for them, and re-layouts: 40.7 us -> 31.6 us
    unnamed x49 -> x48, local copies, waits for them, and re-layouts: 8.09 us -> 1.03 us
    reshape x1 -> x0, local copies, waits for them, and re-layouts: 1.98 us -> none  [shards(): projected.astype(jnp.bfloat16).reshape(tiles, enc_count, column_width)]
  transfers between devices with their start and end apart: 15 -> 15, of which waited for: 2 -> 2; matrix products, arithmetic and copies ran while one was open for 34% -> 30% of each run, Pallas kernels for 0% -> 0%
where the time goes in v6:
time: 155 us; the launch traced here: 153 us
  starting transfers between devices  74.8 us (48%)
  local copies, waits for them, and re-layouts  31.6 us (20%)
  matrix products  18 us (12%)
  waiting for transfers between devices  17 us (11%)
  other arithmetic  11 us (7%)
    ppermute x14, starting transfers between devices, from_behind(): return lax.ppermute(value, axis, pairs)  68.1 us
    all_to_all x1, waiting for transfers between devices, shards(): lax.all_to_all(projected, 'enc', split_axis=1, concat_axis=0, tiled=True)  15.1 us
    gather x1, local copies, waits for them, and re-layouts, shards(): jnp.take(widened, local_row, axis=0)  7.12 us
    all_to_all x1, starting transfers between devices, shards(): lax.all_to_all(projected, 'enc', split_axis=1, concat_axis=0, tiled=True)  6.72 us
    dot_general x1, matrix products, shards(): jnp.einsum('cbk,tc->btk', projector, features, preferred_element_type=jnp...  6.02 us
    convert_element_type x2, local copies, waits for them, and re-layouts, shards(): return output.reshape(row_count, head_count * HDIM).astype(jnp.bfloat16)  5.02 us
    reshape x2, local copies, waits for them, and re-layouts, shards(): plain = mixed_in.reshape(blocks, SPAN, head_count, HDIM)  4.71 us
    concatenate x1, local copies, waits for them, and re-layouts, shards(): widened = jnp.concatenate([low_received[:edge], audio_rows, high], axis=0)  3.49 us
  transfers between devices with their start and end apart: 15, of which 2 were waited for; matrix products, arithmetic and copies ran while one was open for 30% of the time, Pallas kernels for 0%

profile of v6, /device:TPU:6, one launch (start us, length us, event | category | flops | bytes accessed | tf_op | source)
XLA Modules:
  0.0 153.2 jit_solution(9372085072695902371)
XLA Ops:
  3.0 2.3 %collective-permute-start.5 = (f32[4]{0:T(128)}, f32[4]{0:T(128)}, u32[]{:S(2)}, u32[]{:S(2)}) collective-permute-start(f32[4]{0:T(128)} %slice_bitcast_fusion), channel_id=1, source_target_pairs={{0,32},{32,64},{64,96},{96,128},{128,160},{160,192},{192,224},{224... | collective-permute-start | bytes 56 | tf_op jit(solution)/shard_map/ppermute | solution.py:18
  5.3 4.4 %collective-permute-start.7 = (f32[4]{0:T(128)}, f32[4]{0:T(128)}, u32[]{:S(2)}, u32[]{:S(2)}) collective-permute-start(f32[4]{0:T(128)} %slice_bitcast_fusion), channel_id=1, source_target_pairs={{0,64},{32,96},{64,128},{96,160},{128,192},{160,224},{192,256},{22... | collective-permute-start | bytes 56 | tf_op jit(solution)/shard_map/ppermute | solution.py:18
  9.7 3.5 %collective-permute-start = (bf16[1,128]{1,0:T(2,128)(2,1)S(1)}, bf16[1,128]{1,0:T(2,128)(2,1)S(1)}, u32[]{:S(2)}, u32[]{:S(2)}) collective-permute-start(bf16[1,128]{1,0:T(2,128)(2,1)S(1)} %slice.75), channel_id=1, source_target_pairs={{0,4},{4,8},{8,12},{12,16},{16,20},{20,24},{24,28},{28,32},{32,36}... | collective-permute-start | bytes 776 | tf_op jit(solution)/shard_map/ppermute | solution.py:18
  16.9 6.0 %fusion.23 = bf16[128,8,256]{2,0,1:T(8,128)(2,1)} fusion(bf16[1280,8,256]{2,1,0:T(8,128)(2,1)} %param.16, bf16[384,1280]{1,0:T(8,128)(2,1)S(1)} %copy-done, f32[1280]{0:T(1024)S(1)} %copy-done.22, bf16[128,256]{1,0:T(8,128)(2,1)S(1)} %reshape.198, bf16[128,128]{1,0:T(8,128)(2,1)S(1)} %maximum_select_fusion.1), kind=kOutput, calls=%fused_computation.28 | convolution fusion | flops 808189952 | bytes 6853632 | tf_op jit(solution)/shard_map/cbk,tc->btk/dot_general | solution.py:92
  22.9 6.7 %all-to-all-start = ((bf16[128,8,256]{2,0,1:T(8,128)(2,1)}), bf16[128,8,256]{2,0,1:T(8,128)(2,1)}, u32[]{:S(2)}, u32[]{:S(2)}) async-start(bf16[128,8,256]{2,0,1:T(8,128)(2,1)} %fusion.23), calls=%async_computation | async-start | bytes 1048576 | tf_op jit(solution)/shard_map/all_to_all | solution.py:95
  33.6 15.1 %all-to-all-done = bf16[128,8,256]{2,0,1:T(8,128)(2,1)} async-done(((bf16[128,8,256]{2,0,1:T(8,128)(2,1)}), bf16[128,8,256]{2,0,1:T(8,128)(2,1)}, u32[]{:S(2)}, u32[]{:S(2)}) %all-to-all-start) | async-done | bytes 524320 | tf_op jit(solution)/shard_map/all_to_all | solution.py:95
  59.8 3.5 %concatenate.18 = bf16[1539,256]{1,0:T(8,128)(2,1)S(1)} concatenate(bf16[259,256]{1,0:T(8,128)(2,1)S(1)} %bitcast.78, bf16[1024,256]{1,0:T(8,128)(2,1)} %bitcast.4, bf16[256,256]{1,0:T(8,128)(2,1)S(1)} %collective-permute-done.2), dimensions={0} | concatenate | bytes 1575936 | tf_op jit(solution)/shard_map/concatenate | solution.py:104
  63.3 7.1 %gather_fusion = bf16[2051,256]{1,0:T(8,128)(2,1)S(1)} fusion(bf16[1539,256]{1,0:T(8,128)(2,1)S(1)} %concatenate.18, s32[3072]{0:T(1024)} %pad_clamp_fusion), kind=kCustom, calls=%fused_computation | custom fusion | bytes 2108428 | tf_op jit(solution)/shard_map/jit(_take)/gather | solution.py:118
  70.5 3.0 %maximum_select_fusion = bf16[2051,256]{1,0:T(8,128)(2,1)S(1)} fusion(bf16[2048,256]{1,0:T(8,128)(2,1)} %param.19, bf16[3,256]{1,0:T(4,128)(2,1)S(1)} %slice.80, bf16[2051,256]{1,0:T(8,128)(2,1)S(1)} %gather_fusion, pred[2051]{0:T(1024)(128)(4,1)S(1)} %get-tuple-element.14, pred[2051]{0:T(1024)(128)(4,1)S(1)} %copy-done.9), kind=kLoop, calls=%fused_computation.29 | loop fusion | flops 3150336 | bytes 3154438 | tf_op jit(solution)/shard_map/jit(_where)/select_n | solution.py:118
  76.7 2.9 %copy.85 = bf16[16,128,4,64]{1,3,2,0:T(8,128)(2,1)S(1)} copy(bf16[16,128,4,64]{3,2,1,0:T(4,128)(2,1)} %reshape.219) | data formatting | bytes 2097152 | tf_op jit(solution)/shard_map/reshape | solution.py:127
  80.5 2.2 %fusion.17 = f32[4,1,64,128]{3,1,2,0:T(1,128)S(1)} fusion(f32[16,4,1,1]{0,2,3,1:T(1,128)S(1)} %copy-done.12, f32[16,4,64,128]{3,2,1,0:T(8,128)S(1)} %fusion.4), kind=kOutput, calls=%fused_computation.24 | convolution fusion | flops 6291456 | bytes 2228480 | tf_op jit(solution)/shard_map/dh,dhpn->hpn/dot_general | solution.py:162
  82.7 4.4 %collective-permute-start.3 = (bf16[4,64,128]{2,1,0:T(8,128)(2,1)S(1)}, bf16[4,64,128]{2,1,0:T(8,128)(2,1)S(1)}, u32[]{:S(2)}, u32[]{:S(2)}) collective-permute-start(bf16[4,64,128]{2,1,0:T(8,128)(2,1)S(1)} %convert_element_type.83), channel_id=1, source_target_pairs={{0,32},{32,64},{64,96},{96,128},{128,160},{160,192},{192,224},{224... | collective-permute-start | bytes 196616 | tf_op jit(solution)/shard_map/ppermute | solution.py:18
  87.2 3.9 %collective-permute-start.4 = (bf16[4,64,128]{2,1,0:T(8,128)(2,1)S(1)}, bf16[4,64,128]{2,1,0:T(8,128)(2,1)S(1)}, u32[]{:S(2)}, u32[]{:S(2)}) collective-permute-start(bf16[4,64,128]{2,1,0:T(8,128)(2,1)S(1)} %convert_element_type.83), channel_id=1, source_target_pairs={{0,64},{32,96},{64,128},{96,160},{128,192},{160,224},{192,256},{22... | collective-permute-start | bytes 196616 | tf_op jit(solution)/shard_map/ppermute | solution.py:18
  91.7 5.9 %collective-permute-start.9 = (f32[4]{0:T(128)S(1)}, f32[4]{0:T(128)S(1)}, u32[]{:S(2)}, u32[]{:S(2)}) collective-permute-start(f32[4]{0:T(128)S(1)} %get-tuple-element.11), channel_id=1, source_target_pairs={{0,64},{32,96},{64,128},{96,160},{128,192},{160,224},{192,256},{22... | collective-permute-start | bytes 56 | tf_op jit(solution)/shard_map/ppermute | solution.py:18
  97.7 4.8 %collective-permute-start.6 = (bf16[4,64,128]{2,1,0:T(8,128)(2,1)S(1)}, bf16[4,64,128]{2,1,0:T(8,128)(2,1)S(1)}, u32[]{:S(2)}, u32[]{:S(2)}) collective-permute-start(bf16[4,64,128]{2,1,0:T(8,128)(2,1)S(1)} %fusion.74), channel_id=1, source_target_pairs={{0,64},{32,96},{64,128},{96,160},{128,192},{160,224},{192,256},{22... | collective-permute-start | bytes 196616 | tf_op jit(solution)/shard_map/ppermute | solution.py:18
  102.6 5.1 %collective-permute-start.11 = (f32[4]{0:T(128)S(1)}, f32[4]{0:T(128)S(1)}, u32[]{:S(2)}, u32[]{:S(2)}) collective-permute-start(f32[4]{0:T(128)S(1)} %get-tuple-element.13), channel_id=1, source_target_pairs={{0,128},{32,160},{64,192},{96,224},{128,256},{160,288},{192,320},{... | collective-permute-start | bytes 56 | tf_op jit(solution)/shard_map/ppermute | solution.py:18
  107.9 6.6 %collective-permute-start.8 = (bf16[4,64,128]{2,1,0:T(8,128)(2,1)S(1)}, bf16[4,64,128]{2,1,0:T(8,128)(2,1)S(1)}, u32[]{:S(2)}, u32[]{:S(2)}) collective-permute-start(bf16[4,64,128]{2,1,0:T(8,128)(2,1)S(1)} %fusion.132), channel_id=1, source_target_pairs={{0,128},{32,160},{64,192},{96,224},{128,256},{160,288},{192,320},{... | collective-permute-start | bytes 196616 | tf_op jit(solution)/shard_map/ppermute | solution.py:18
  114.5 6.1 %collective-permute-start.13 = (f32[4]{0:T(128)S(1)}, f32[4]{0:T(128)S(1)}, u32[]{:S(2)}, u32[]{:S(2)}) collective-permute-start(f32[4]{0:T(128)S(1)} %get-tuple-element.9), channel_id=1, source_target_pairs={{0,256},{32,288},{64,320},{96,352},{128,384},{160,416},{192,448},{... | collective-permute-start | bytes 56 | tf_op jit(solution)/shard_map/ppermute | solution.py:18
  120.8 5.5 %collective-permute-start.10 = (bf16[4,64,128]{2,1,0:T(8,128)(2,1)S(1)}, bf16[4,64,128]{2,1,0:T(8,128)(2,1)S(1)}, u32[]{:S(2)}, u32[]{:S(2)}) collective-permute-start(bf16[4,64,128]{2,1,0:T(8,128)(2,1)S(1)} %fusion.81), channel_id=1, source_target_pairs={{0,256},{32,288},{64,320},{96,352},{128,384},{160,416},{192,448},{... | collective-permute-start | bytes 196616 | tf_op jit(solution)/shard_map/ppermute | solution.py:18
  128.3 12.1 %collective-permute-start.12 = (bf16[4,64,128]{2,1,0:T(8,128)(2,1)S(1)}, bf16[4,64,128]{2,1,0:T(8,128)(2,1)S(1)}, u32[]{:S(2)}, u32[]{:S(2)}) collective-permute-start(bf16[4,64,128]{2,1,0:T(8,128)(2,1)S(1)} %fusion.131), channel_id=1, source_target_pairs={{0,512},{32,544},{64,576},{96,608},{128,640},{160,672},{192,704},{... | collective-permute-start | bytes 196616 | tf_op jit(solution)/shard_map/ppermute | solution.py:18
  142.3 3.2 %bitcast_add_fusion = f32[16,4,64,128]{3,0,2,1:T(8,128)S(1)} fusion(f32[4,64,128]{2,1,0:T(8,128)S(1)} %multiply_add_fusion, f32[16,4]{0,1:T(4,128)S(1)} %copy-done.11, f32[16,4,64,128]{3,2,1,0:T(8,128)S(1)} %fusion.4, f32[16,4]{0,1:T(4,128)S(1)} %copy.92, f32[16,4]{0,1:T(4,128)S(1)} %copy-done.10, pred[16,16]{1,0:T(8,128)(4,1)S(1)} %copy-done.13), kind=kOutput, calls=%fused_computation.14 | convolution fusion | flops 101714944 | bytes 4326400 | tf_op jit(solution)/shard_map/cdh,dhpn->chpn/dot_general | solution.py:159
  145.5 2.6 %fusion.7 = bf16[16,128,4,64]{1,3,2,0:T(8,128)(2,1)} fusion(bf16[16,128,4,64]{1,3,2,0:T(8,128)(2,1)S(1)} %copy.85, f32[16,4,64,128]{3,2,1,0:T(8,128)S(1)} %fusion.2, bf16[16,128,128,1]{2,1,3,0:T(8,128)(2,1)S(1)} %bitcast.76, f32[16,4,64,128]{3,0,2,1:T(8,128)S(1)} %bitcast_add_fusion, f32[4]{0:T(128)S(1)} %copy-done.21, f32[16,128,4]{1,2,0:T(4,128)S(1)} %copy.98), kind=kOutput, calls=%fused_computation.11 | convolution fusion | flops 405798912 | bytes 6848528 | tf_op jit(solution)/shard_map/cin,chpn->cihp/dot_general | solution.py:169
  148.1 2.9 %copy.106 = bf16[16,128,4,64]{3,2,1,0:T(4,128)(2,1)S(1)} copy(bf16[16,128,4,64]{1,3,2,0:T(8,128)(2,1)} %fusion.7) | data formatting | bytes 2097152 | tf_op jit(solution)/shard_map/convert_element_type | solution.py:173
  151.0 2.2 %reshape.218 = bf16[2048,256]{1,0:T(8,128)(2,1)} reshape(bf16[16,128,4,64]{3,2,1,0:T(4,128)(2,1)S(1)} %copy.106) | data formatting | bytes 2097152 | tf_op jit(solution)/shard_map/convert_element_type | solution.py:173
  (120 shorter events, 30.4 us)
Async XLA Ops:
  0.0 16.9 %copy-start = (bf16[384,1280]{1,0:T(8,128)(2,1)S(1)}, bf16[384,1280]{1,0:T(8,128)(2,1)}, u32[]{:S(2)}) copy-start(bf16[384,1280]{1,0:T(8,128)(2,1)} %param.14) | copy-start | bytes 2949124
  0.0 14.2 %copy-start.18 = (f32[4,256]{1,0:T(4,128)S(1)}, f32[4,256]{1,0:T(4,128)}, u32[]{:S(2)}) copy-start(f32[4,256]{1,0:T(4,128)} %param.20) | copy-start | bytes 12292
  0.0 16.9 %copy-start.22 = (f32[1280]{0:T(1024)S(1)}, f32[1280]{0:T(1024)}, u32[]{:S(2)}) copy-start(f32[1280]{0:T(1024)} %param.15) | copy-start | bytes 15364
  3.0 88.1 %collective-permute-start.5 = (f32[4]{0:T(128)}, f32[4]{0:T(128)}, u32[]{:S(2)}, u32[]{:S(2)}) collective-permute-start(f32[4]{0:T(128)} %slice_bitcast_fusion), channel_id=1, source_target_pairs={{0,32},{32,64},{64,96},{96,128},{128,160},{160,192},{192,224},{224... | collective-permute-start | bytes 56 | tf_op jit(solution)/shard_map/ppermute | solution.py:18
  5.3 85.8 %collective-permute-start.7 = (f32[4]{0:T(128)}, f32[4]{0:T(128)}, u32[]{:S(2)}, u32[]{:S(2)}) collective-permute-start(f32[4]{0:T(128)} %slice_bitcast_fusion), channel_id=1, source_target_pairs={{0,64},{32,96},{64,128},{96,160},{128,192},{160,224},{192,256},{22... | collective-permute-start | bytes 56 | tf_op jit(solution)/shard_map/ppermute | solution.py:18
  9.7 7.1 %collective-permute-start = (bf16[1,128]{1,0:T(2,128)(2,1)S(1)}, bf16[1,128]{1,0:T(2,128)(2,1)S(1)}, u32[]{:S(2)}, u32[]{:S(2)}) collective-permute-start(bf16[1,128]{1,0:T(2,128)(2,1)S(1)} %slice.75), channel_id=1, source_target_pairs={{0,4},{4,8},{8,12},{12,16},{16,20},{20,24},{24,28},{28,32},{32,36}... | collective-permute-start | bytes 776 | tf_op jit(solution)/shard_map/ppermute | solution.py:18
  16.9 14.0 %copy-start.1 = (bf16[2048,128]{1,0:T(8,128)(2,1)S(1)}, bf16[2048,128]{1,0:T(8,128)(2,1)}, u32[]{:S(2)}) copy-start(bf16[2048,128]{1,0:T(8,128)(2,1)} %param.21) | copy-start | bytes 1572868
  16.9 14.0 %copy-start.3 = (bf16[2048,128]{1,0:T(8,128)(2,1)S(1)}, bf16[2048,128]{1,0:T(8,128)(2,1)}, u32[]{:S(2)}) copy-start(bf16[2048,128]{1,0:T(8,128)(2,1)} %param.22) | copy-start | bytes 1572868
  22.9 25.8 %all-to-all-start = ((bf16[128,8,256]{2,0,1:T(8,128)(2,1)}), bf16[128,8,256]{2,0,1:T(8,128)(2,1)}, u32[]{:S(2)}, u32[]{:S(2)}) async-start(bf16[128,8,256]{2,0,1:T(8,128)(2,1)} %fusion.23), calls=%async_computation | async-start | bytes 1048576 | tf_op jit(solution)/shard_map/all_to_all | solution.py:95
  49.7 10.1 %collective-permute-start.1 = (bf16[262,256]{1,0:T(8,128)(2,1)S(1)}, bf16[262,256]{1,0:T(8,128)(2,1)S(1)}, u32[]{:S(2)}, u32[]{:S(2)}) collective-permute-start(bf16[262,256]{1,0:T(8,128)(2,1)S(1)} %pad_maximum_fusion), channel_id=1, source_target_pairs={{0,32},{32,64},{64,96},{96,128},{128,160},{160,192},{192,224},{224... | collective-permute-start | bytes 402440 | tf_op jit(solution)/shard_map/ppermute | solution.py:18
  53.3 6.5 %collective-permute-start.2 = (bf16[256,256]{1,0:T(8,128)(2,1)}, bf16[256,256]{1,0:T(8,128)(2,1)S(1)}, u32[]{:S(2)}, u32[]{:S(2)}) collective-permute-start(bf16[256,256]{1,0:T(8,128)(2,1)} %bitcast.6), channel_id=1, source_target_pairs={{32,0},{64,32},{96,64},{128,96},{160,128},{192,160},{224,192},{256... | collective-permute-start | bytes 393224 | tf_op jit(solution)/shard_map/ppermute | solution.py:18
  80.4 59.9 %copy-start.5 = (f32[16,128,128]{2,1,0:T(8,128)S(1)}, f32[16,128,128]{2,1,0:T(8,128)}, u32[]{:S(2)}) copy-start(f32[16,128,128]{2,1,0:T(8,128)} %fusion.138) | copy-start | bytes 3145732
  80.5 59.9 %copy-start.8 = (f32[16,128,4]{1,2,0:T(4,128)S(1)}, f32[16,128,4]{1,2,0:T(4,128)}, u32[]{:S(2)}) copy-start(f32[16,128,4]{1,2,0:T(4,128)} %copy.82) | copy-start | bytes 98308
  82.7 14.9 %collective-permute-start.3 = (bf16[4,64,128]{2,1,0:T(8,128)(2,1)S(1)}, bf16[4,64,128]{2,1,0:T(8,128)(2,1)S(1)}, u32[]{:S(2)}, u32[]{:S(2)}) collective-permute-start(bf16[4,64,128]{2,1,0:T(8,128)(2,1)S(1)} %convert_element_type.83), channel_id=1, source_target_pairs={{0,32},{32,64},{64,96},{96,128},{128,160},{160,192},{192,224},{224... | collective-permute-start | bytes 196616 | tf_op jit(solution)/shard_map/ppermute | solution.py:18
  87.2 10.5 %collective-permute-start.4 = (bf16[4,64,128]{2,1,0:T(8,128)(2,1)S(1)}, bf16[4,64,128]{2,1,0:T(8,128)(2,1)S(1)}, u32[]{:S(2)}, u32[]{:S(2)}) collective-permute-start(bf16[4,64,128]{2,1,0:T(8,128)(2,1)S(1)} %convert_element_type.83), channel_id=1, source_target_pairs={{0,64},{32,96},{64,128},{96,160},{128,192},{160,224},{192,256},{22... | collective-permute-start | bytes 196616 | tf_op jit(solution)/shard_map/ppermute | solution.py:18
  91.7 10.9 %collective-permute-start.9 = (f32[4]{0:T(128)S(1)}, f32[4]{0:T(128)S(1)}, u32[]{:S(2)}, u32[]{:S(2)}) collective-permute-start(f32[4]{0:T(128)S(1)} %get-tuple-element.11), channel_id=1, source_target_pairs={{0,64},{32,96},{64,128},{96,160},{128,192},{160,224},{192,256},{22... | collective-permute-start | bytes 56 | tf_op jit(solution)/shard_map/ppermute | solution.py:18
  97.7 10.0 %collective-permute-start.6 = (bf16[4,64,128]{2,1,0:T(8,128)(2,1)S(1)}, bf16[4,64,128]{2,1,0:T(8,128)(2,1)S(1)}, u32[]{:S(2)}, u32[]{:S(2)}) collective-permute-start(bf16[4,64,128]{2,1,0:T(8,128)(2,1)S(1)} %fusion.74), channel_id=1, source_target_pairs={{0,64},{32,96},{64,128},{96,160},{128,192},{160,224},{192,256},{22... | collective-permute-start | bytes 196616 | tf_op jit(solution)/shard_map/ppermute | solution.py:18
  102.6 11.9 %collective-permute-start.11 = (f32[4]{0:T(128)S(1)}, f32[4]{0:T(128)S(1)}, u32[]{:S(2)}, u32[]{:S(2)}) collective-permute-start(f32[4]{0:T(128)S(1)} %get-tuple-element.13), channel_id=1, source_target_pairs={{0,128},{32,160},{64,192},{96,224},{128,256},{160,288},{192,320},{... | collective-permute-start | bytes 56 | tf_op jit(solution)/shard_map/ppermute | solution.py:18
  107.9 12.8 %collective-permute-start.8 = (bf16[4,64,128]{2,1,0:T(8,128)(2,1)S(1)}, bf16[4,64,128]{2,1,0:T(8,128)(2,1)S(1)}, u32[]{:S(2)}, u32[]{:S(2)}) collective-permute-start(bf16[4,64,128]{2,1,0:T(8,128)(2,1)S(1)} %fusion.132), channel_id=1, source_target_pairs={{0,128},{32,160},{64,192},{96,224},{128,256},{160,288},{192,320},{... | collective-permute-start | bytes 196616 | tf_op jit(solution)/shard_map/ppermute | solution.py:18
  114.5 11.7 %collective-permute-start.13 = (f32[4]{0:T(128)S(1)}, f32[4]{0:T(128)S(1)}, u32[]{:S(2)}, u32[]{:S(2)}) collective-permute-start(f32[4]{0:T(128)S(1)} %get-tuple-element.9), channel_id=1, source_target_pairs={{0,256},{32,288},{64,320},{96,352},{128,384},{160,416},{192,448},{... | collective-permute-start | bytes 56 | tf_op jit(solution)/shard_map/ppermute | solution.py:18
  120.8 7.4 %collective-permute-start.10 = (bf16[4,64,128]{2,1,0:T(8,128)(2,1)S(1)}, bf16[4,64,128]{2,1,0:T(8,128)(2,1)S(1)}, u32[]{:S(2)}, u32[]{:S(2)}) collective-permute-start(bf16[4,64,128]{2,1,0:T(8,128)(2,1)S(1)} %fusion.81), channel_id=1, source_target_pairs={{0,256},{32,288},{64,320},{96,352},{128,384},{160,416},{192,448},{... | collective-permute-start | bytes 196616 | tf_op jit(solution)/shard_map/ppermute | solution.py:18
  128.3 13.9 %copy-start.10 = (f32[16,4]{0,1:T(4,128)S(1)}, f32[16,4]{0,1:T(4,128)}, u32[]{:S(2)}) copy-start(f32[16,4]{0,1:T(4,128)} %fusion.96) | copy-start | bytes 772
  128.3 13.9 %copy-start.11 = (f32[16,4]{0,1:T(4,128)S(1)}, f32[16,4]{0,1:T(4,128)}, u32[]{:S(2)}) copy-start(f32[16,4]{0,1:T(4,128)} %copy.96) | copy-start | bytes 772
  128.3 13.7 %collective-permute-start.12 = (bf16[4,64,128]{2,1,0:T(8,128)(2,1)S(1)}, bf16[4,64,128]{2,1,0:T(8,128)(2,1)S(1)}, u32[]{:S(2)}, u32[]{:S(2)}) collective-permute-start(bf16[4,64,128]{2,1,0:T(8,128)(2,1)S(1)} %fusion.131), channel_id=1, source_target_pairs={{0,512},{32,544},{64,576},{96,608},{128,640},{160,672},{192,704},{... | collective-permute-start | bytes 196616 | tf_op jit(solution)/shard_map/ppermute | solution.py:18
  (14 other events, 82.9 us)

commit v7 on v6

--- a/solution.py
+++ b/solution.py
@@ -124,12 +124,18 @@
     mixed_in = jax.nn.silu(summed_mix).astype(jnp.bfloat16)
     head_count = step_size.shape[0]
     blocks = row_count // SPAN
-    plain = mixed_in.reshape(blocks, SPAN, head_count, HDIM)
+    width = head_count * HDIM
+    plain = mixed_in.reshape(blocks, SPAN, width)
     values = plain.astype(jnp.float32)
     b_rows = input_map.reshape(blocks, SPAN, -1)
     c_rows = output_map.reshape(blocks, SPAN, -1)
     b_all = b_rows.astype(jnp.float32)
     c_all = c_rows.astype(jnp.float32)
+    column_head = jnp.arange(width, dtype=jnp.int32) // HDIM
+
+    def spread(per_head):
+        return jnp.repeat(per_head, HDIM, axis=-1)
+
     step_sizes = step_size.T.reshape(blocks, SPAN, head_count)
     log_decay = -step_sizes * jnp.exp(decay_log)[None, None, :]
     running = jnp.cumsum(log_decay, axis=1)
@@ -140,11 +146,16 @@
     weight = (decay_table * intersection[..., None] * step_sizes[:, None, :, :]).astype(
         jnp.bfloat16
     )
-    inner_part = jnp.einsum("cijh,cjhp->cihp", weight, plain, preferred_element_type=jnp.float32)
-    inputs = values * step_sizes[..., None]
+    inner_part = jnp.zeros(values.shape, jnp.float32)
+    for head in range(head_count):
+        per_head = jnp.einsum(
+            "cij,cjw->ciw", weight[..., head], plain, preferred_element_type=jnp.float32
+        )
+        inner_part = jnp.where(column_head == head, per_head, inner_part)
+    inputs = values * spread(step_sizes)
     tail_decay = jnp.exp(running[:, -1:, :] - running)
     block_states = jnp.einsum(
-        "cjhp,cjn->chpn", inputs * tail_decay[..., None], b_all, precision=high_mode
+        "cjw,cjn->cwn", inputs * spread(tail_decay), b_all, precision=high_mode
     )
     totals = running[:, -1, :]
     through = jnp.cumsum(totals, axis=0)
@@ -156,21 +167,23 @@
         jnp.exp(jnp.where(earlier, before_block[:, None, :] - through[None, :, :], 0.0)),
         0.0,
     )
-    local_starts = jnp.einsum("cdh,dhpn->chpn", weights, block_states, precision=highest)
+    local_starts = jnp.einsum("cdw,dwn->cwn", spread(weights), block_states, precision=highest)
     device_total = through[-1]
+    device_state = jnp.einsum(
+        "dw,dwn->wn", spread(jnp.exp(device_total[None, :] - through)), block_states,
+        precision=highest,
+    )
     first, spans = prefix_windows(device_total, "seq")
-    device_state = jnp.einsum(
-        "dh,dhpn->hpn", jnp.exp(device_total[None, :] - through), block_states, precision=highest
-    )
-
-    incoming = prefix_state(device_total, device_state, first, spans, "seq")
-    block_in = local_starts + jnp.exp(before_block)[:, :, None, None] * incoming[None]
+    incoming = prefix_state(
+        device_total, device_state.reshape(head_count, HDIM, -1), first, spans, "seq"
+    ).reshape(width, -1)
+    block_in = local_starts + spread(jnp.exp(before_block))[:, :, None] * incoming[None]
     carried = (
-        jnp.einsum("cin,chpn->cihp", c_all, block_in, precision=high_mode)
-        * jnp.exp(running)[..., None]
-    )
-    output = inner_part + carried + skip_gain[None, None, :, None] * values
-    return output.reshape(row_count, head_count * HDIM).astype(jnp.bfloat16)
+        jnp.einsum("cin,cwn->ciw", c_all, block_in, precision=high_mode)
+        * spread(jnp.exp(running))
+    )
+    output = inner_part + carried + spread(skip_gain)[None, None, :] * values
+    return output.reshape(row_count, width).astype(jnp.bfloat16)
 
 
 def solution(mesh):

time: 155 us -> 154 us (level)
  local copies, waits for them, and re-layouts: 31.6 us -> 23.4 us
  starting transfers between devices: 74.8 us -> 80.7 us
    ppermute x14, starting transfers between devices: 68.1 us -> 74.5 us  [from_behind(): return lax.ppermute(value, axis, pairs)]
    convert_element_type x2 -> x0, local copies, waits for them, and re-layouts: 5.02 us -> none  [shards(): return output.reshape(row_count, head_count * HDIM).astype(jnp.bfloat16)]
    ppermute x14, waiting for transfers between devices: 1.89 us -> 6.04 us  [from_behind(): return lax.ppermute(value, axis, pairs)]
    all_to_all x1, waiting for transfers between devices: 15.1 us -> 11.1 us  [shards(): lax.all_to_all(projected, 'enc', split_axis=1, concat_axis=0, tiled=True)]
    convert_element_type x0 -> x1, other arithmetic: none -> 2.38 us  [shards(): (decay_table * intersection[..., None] * step_sizes[:, None, :, :]).astyp...]
    concatenate x1, local copies, waits for them, and re-layouts: 3.49 us -> 1.34 us  [shards(): widened = jnp.concatenate([low_received[:edge], audio_rows, high], axis=0)]
    unnamed x48 -> x53, local copies, waits for them, and re-layouts: 1.03 us -> 2.81 us
    dot_general x5 -> x8, matrix products: 10.5 us -> 12.2 us  [the longest x1 3.34 us: shards(): jnp.einsum('cdw,dwn->cwn', spread(weights), block_states, precision=highest)]
  transfers between devices with their start and end apart: 15 -> 15, of which waited for: 2 -> 5; matrix products, arithmetic and copies ran while one was open for 30% -> 28% of each run, Pallas kernels for 0% -> 0%
where the time goes in v7:
time: 154 us; the launch traced here: 153 us
  starting transfers between devices  80.7 us (52%)
  local copies, waits for them, and re-layouts  23.4 us (15%)
  matrix products  18.7 us (12%)
  waiting for transfers between devices  17.1 us (11%)
  other arithmetic  12.2 us (8%)
    ppermute x14, starting transfers between devices, from_behind(): return lax.ppermute(value, axis, pairs)  74.5 us
    all_to_all x1, waiting for transfers between devices, shards(): lax.all_to_all(projected, 'enc', split_axis=1, concat_axis=0, tiled=True)  11.1 us
    gather x1, local copies, waits for them, and re-layouts, shards(): jnp.take(widened, local_row, axis=0)  6.99 us
    all_to_all x1, starting transfers between devices, shards(): lax.all_to_all(projected, 'enc', split_axis=1, concat_axis=0, tiled=True)  6.21 us
    ppermute x14, waiting for transfers between devices, from_behind(): return lax.ppermute(value, axis, pairs)  6.04 us
    dot_general x1, matrix products, shards(): jnp.einsum('cbk,tc->btk', projector, features, preferred_element_type=jnp...  5.99 us
    reshape x3, local copies, waits for them, and re-layouts, spread(): return jnp.repeat(per_head, HDIM, axis=-1)  5.5 us
    dot_general x1, matrix products, shards(): jnp.einsum('cdw,dwn->cwn', spread(weights), block_states, precision=highest)  3.34 us
  transfers between devices with their start and end apart: 15, of which 5 were waited for; matrix products, arithmetic and copies ran while one was open for 28% of the time, Pallas kernels for 0%

profile of v7, /device:TPU:6, one launch (start us, length us, event | category | flops | bytes accessed | tf_op | source)
XLA Modules:
  0.0 152.9 jit_solution(2346751440967687817)
XLA Ops:
  4.2 4.5 %collective-permute-start.7 = (f32[4]{0:T(128)S(1)}, f32[4]{0:T(128)S(1)}, u32[]{:S(2)}, u32[]{:S(2)}) collective-permute-start(f32[4]{0:T(128)S(1)} %slice_bitcast_fusion.8), channel_id=1, source_target_pairs={{0,64},{32,96},{64,128},{96,160},{128,192},{160,224},{192,256},{22... | collective-permute-start | bytes 56 | tf_op jit(solution)/shard_map/ppermute | solution.py:18
  8.7 3.5 %collective-permute-start = (bf16[1,128]{1,0:T(2,128)(2,1)S(1)}, bf16[1,128]{1,0:T(2,128)(2,1)S(1)}, u32[]{:S(2)}, u32[]{:S(2)}) collective-permute-start(bf16[1,128]{1,0:T(2,128)(2,1)S(1)} %slice.92), channel_id=1, source_target_pairs={{0,4},{4,8},{8,12},{12,16},{16,20},{20,24},{24,28},{28,32},{32,36}... | collective-permute-start | bytes 776 | tf_op jit(solution)/shard_map/ppermute | solution.py:18
  17.6 1.8 %copy.94 = f32[16,128,256]{2,1,0:T(8,128)} copy(f32[16,128,256]{1,2,0:T(8,128)S(1)} %bitcast.85) | data formatting | bytes 4194304 | tf_op jit(solution)/shard_map/reshape | solution.py:137
  23.9 1.8 %copy.80 = f32[16,128,256]{2,1,0:T(8,128)} copy(f32[16,128,256]{1,2,0:T(8,128)S(1)} %bitcast.87) | data formatting | bytes 4194304 | tf_op jit(solution)/shard_map/reshape | solution.py:137
  26.8 6.0 %fusion.14 = bf16[128,8,256]{2,0,1:T(8,128)(2,1)} fusion(bf16[1280,8,256]{2,1,0:T(8,128)(2,1)} %param.16, bf16[384,1280]{1,0:T(8,128)(2,1)S(1)} %copy-done, f32[1280]{0:T(1024)S(1)} %copy-done.24, bf16[128,256]{1,0:T(8,128)(2,1)S(1)} %reshape.203, bf16[128,128]{1,0:T(8,128)(2,1)S(1)} %maximum_select_fusion.1), kind=kOutput, calls=%fused_computation.21 | convolution fusion | flops 808189952 | bytes 6853632 | tf_op jit(solution)/shard_map/cbk,tc->btk/dot_general | solution.py:92
  32.7 6.2 %all-to-all-start = ((bf16[128,8,256]{2,0,1:T(8,128)(2,1)}), bf16[128,8,256]{2,0,1:T(8,128)(2,1)S(1)}, u32[]{:S(2)}, u32[]{:S(2)}) async-start(bf16[128,8,256]{2,0,1:T(8,128)(2,1)} %fusion.14), calls=%async_computation | async-start | bytes 1048576 | tf_op jit(solution)/shard_map/all_to_all | solution.py:95
  40.0 2.4 %multiply_convert_fusion = bf16[16,128,128,4]{2,1,0,3:T(8,128)(2,1)} fusion(f32[16,128,4]{1,0,2:T(8,128)S(1)} %bitcast.100, f32[16,128,128]{2,1,0:T(8,128)S(1)} %fusion.114, f32[16,128,4]{1,0,2:T(8,128)S(1)} %copy.75, pred[128,128]{1,0:T(8,128)(4,1)S(1)} %iota_compare_fusion.1), kind=kLoop, calls=%fused_computation.3 | loop fusion | flops 6291456 | bytes 3227648 | tf_op jit(solution)/shard_map/convert_element_type | solution.py:146
  42.4 4.3 %collective-permute-start.9 = (f32[4]{0:T(128)S(1)}, f32[4]{0:T(128)S(1)}, u32[]{:S(2)}, u32[]{:S(2)}) collective-permute-start(f32[4]{0:T(128)S(1)} %get-tuple-element.11), channel_id=1, source_target_pairs={{0,64},{32,96},{64,128},{96,160},{128,192},{160,224},{192,256},{22... | collective-permute-start | bytes 56 | tf_op jit(solution)/shard_map/ppermute | solution.py:18
  46.7 11.1 %all-to-all-done = bf16[128,8,256]{2,0,1:T(8,128)(2,1)S(1)} async-done(((bf16[128,8,256]{2,0,1:T(8,128)(2,1)}), bf16[128,8,256]{2,0,1:T(8,128)(2,1)S(1)}, u32[]{:S(2)}, u32[]{:S(2)}) %all-to-all-start) | async-done | bytes 524320 | tf_op jit(solution)/shard_map/all_to_all | solution.py:95
  57.9 2.0 %collective-permute-start.1 = (bf16[262,256]{1,0:T(8,128)(2,1)S(1)}, bf16[262,256]{1,0:T(8,128)(2,1)S(1)}, u32[]{:S(2)}, u32[]{:S(2)}) collective-permute-start(bf16[262,256]{1,0:T(8,128)(2,1)S(1)} %pad_maximum_fusion), channel_id=1, source_target_pairs={{0,32},{32,64},{64,96},{96,128},{128,160},{160,192},{192,224},{224... | collective-permute-start | bytes 402440 | tf_op jit(solution)/shard_map/ppermute | solution.py:18
  61.7 7.1 %collective-permute-start.11 = (f32[4]{0:T(128)}, f32[4]{0:T(128)}, u32[]{:S(2)}, u32[]{:S(2)}) collective-permute-start(f32[4]{0:T(128)} %get-tuple-element.13), channel_id=1, source_target_pairs={{0,128},{32,160},{64,192},{96,224},{128,256},{160,288},{192,320},{... | collective-permute-start | bytes 56 | tf_op jit(solution)/shard_map/ppermute | solution.py:18
  70.2 7.0 %gather_fusion = bf16[2051,256]{1,0:T(8,128)(2,1)S(1)} fusion(bf16[1539,256]{1,0:T(8,128)(2,1)S(1)} %concatenate.18, s32[3072]{0:T(1024)S(1)} %pad_clamp_fusion), kind=kCustom, calls=%fused_computation | custom fusion | bytes 2108428 | tf_op jit(solution)/shard_map/jit(_take)/gather | solution.py:118
  77.2 3.0 %maximum_select_fusion = bf16[2051,256]{1,0:T(8,128)(2,1)S(1)} fusion(bf16[2048,256]{1,0:T(8,128)(2,1)} %param.19, bf16[3,256]{1,0:T(4,128)(2,1)S(1)} %slice.97, bf16[2051,256]{1,0:T(8,128)(2,1)S(1)} %gather_fusion, pred[2051]{0:T(1024)(128)(4,1)S(1)} %get-tuple-element.14, pred[2051]{0:T(1024)(128)(4,1)S(1)} %get-tuple-element.15), kind=kLoop, calls=%fused_computation.22 | loop fusion | flops 3150336 | bytes 3154438 | tf_op jit(solution)/shard_map/jit(_where)/select_n | solution.py:118
  84.0 3.0 %fusion.10 = f32[256,1,128]{2,1,0:T(1,128)S(1)} fusion(f32[16,256,1]{0,2,1:T(1,128)S(1)} %bitcast.97, f32[16,256,128]{2,1,0:T(8,128)S(1)} %fusion.3), kind=kOutput, calls=%fused_computation.17 | convolution fusion | flops 6291456 | bytes 2244608 | tf_op jit(solution)/shard_map/dw,dwn->wn/dot_general | solution.py:172
  87.1 7.3 %collective-permute-start.4 = (bf16[4,64,128]{2,1,0:T(8,128)(2,1)S(1)}, bf16[4,64,128]{2,1,0:T(8,128)(2,1)S(1)}, u32[]{:S(2)}, u32[]{:S(2)}) collective-permute-start(bf16[4,64,128]{2,1,0:T(8,128)(2,1)S(1)} %bitcast.105), channel_id=1, source_target_pairs={{0,64},{32,96},{64,128},{96,160},{128,192},{160,224},{192,256},{22... | collective-permute-start | bytes 196616 | tf_op jit(solution)/shard_map/ppermute | solution.py:18
  94.3 2.1 %collective-permute-start.3 = (bf16[4,64,128]{2,1,0:T(8,128)(2,1)S(1)}, bf16[4,64,128]{2,1,0:T(8,128)(2,1)S(1)}, u32[]{:S(2)}, u32[]{:S(2)}) collective-permute-start(bf16[4,64,128]{2,1,0:T(8,128)(2,1)S(1)} %bitcast.106), channel_id=1, source_target_pairs={{0,32},{32,64},{64,96},{96,128},{128,160},{160,192},{192,224},{224... | collective-permute-start | bytes 196616 | tf_op jit(solution)/shard_map/ppermute | solution.py:18
  97.1 10.3 %collective-permute-start.13 = (f32[4]{0:T(128)S(1)}, f32[4]{0:T(128)S(1)}, u32[]{:S(2)}, u32[]{:S(2)}) collective-permute-start(f32[4]{0:T(128)S(1)} %get-tuple-element.9), channel_id=1, source_target_pairs={{0,256},{32,288},{64,320},{96,352},{128,384},{160,416},{192,448},{... | collective-permute-start | bytes 56 | tf_op jit(solution)/shard_map/ppermute | solution.py:18
  107.5 4.6 %collective-permute-start.6 = (bf16[4,64,128]{2,1,0:T(8,128)(2,1)S(1)}, bf16[4,64,128]{2,1,0:T(8,128)(2,1)S(1)}, u32[]{:S(2)}, u32[]{:S(2)}) collective-permute-start(bf16[4,64,128]{2,1,0:T(8,128)(2,1)S(1)} %fusion.66), channel_id=1, source_target_pairs={{0,64},{32,96},{64,128},{96,160},{128,192},{160,224},{192,256},{22... | collective-permute-start | bytes 196616 | tf_op jit(solution)/shard_map/ppermute | solution.py:18
  112.1 1.9 %collective-permute-done.6 = bf16[4,64,128]{2,1,0:T(8,128)(2,1)S(1)} collective-permute-done((bf16[4,64,128]{2,1,0:T(8,128)(2,1)S(1)}, bf16[4,64,128]{2,1,0:T(8,128)(2,1)S(1)}, u32[]{:S(2)}, u32[]{:S(2)}) %collective-permute-start.6) | collective-permute-done | bytes 65568 | tf_op jit(solution)/shard_map/ppermute | solution.py:18
  114.1 4.6 %collective-permute-start.8 = (bf16[4,64,128]{2,1,0:T(8,128)(2,1)S(1)}, bf16[4,64,128]{2,1,0:T(8,128)(2,1)S(1)}, u32[]{:S(2)}, u32[]{:S(2)}) collective-permute-start(bf16[4,64,128]{2,1,0:T(8,128)(2,1)S(1)} %fusion.109), channel_id=1, source_target_pairs={{0,128},{32,160},{64,192},{96,224},{128,256},{160,288},{192,320},{... | collective-permute-start | bytes 196616 | tf_op jit(solution)/shard_map/ppermute | solution.py:18
  120.7 10.6 %collective-permute-start.10 = (bf16[4,64,128]{2,1,0:T(8,128)(2,1)S(1)}, bf16[4,64,128]{2,1,0:T(8,128)(2,1)S(1)}, u32[]{:S(2)}, u32[]{:S(2)}) collective-permute-start(bf16[4,64,128]{2,1,0:T(8,128)(2,1)S(1)} %fusion.73), channel_id=1, source_target_pairs={{0,256},{32,288},{64,320},{96,352},{128,384},{160,416},{192,448},{... | collective-permute-start | bytes 196616 | tf_op jit(solution)/shard_map/ppermute | solution.py:18
  133.3 10.8 %collective-permute-start.12 = (bf16[4,64,128]{2,1,0:T(8,128)(2,1)S(1)}, bf16[4,64,128]{2,1,0:T(8,128)(2,1)S(1)}, u32[]{:S(2)}, u32[]{:S(2)}) collective-permute-start(bf16[4,64,128]{2,1,0:T(8,128)(2,1)S(1)} %fusion.108), channel_id=1, source_target_pairs={{0,512},{32,544},{64,576},{96,608},{128,640},{160,672},{192,704},{... | collective-permute-start | bytes 196616 | tf_op jit(solution)/shard_map/ppermute | solution.py:18
  146.1 3.3 %bitcast_add_fusion = f32[16,256,128]{2,0,1:T(8,128)S(1)} fusion(f32[256,128]{1,0:T(8,128)S(1)} %bitcast.95, f32[16,256]{0,1:T(8,128)S(1)} %bitcast.96, f32[16,16,256]{1,0,2:T(8,128)S(1)} %bitcast.84, f32[16,256,128]{2,1,0:T(8,128)S(1)} %fusion.3), kind=kOutput, calls=%fused_computation.13 | convolution fusion | flops 101711872 | bytes 4603904 | tf_op jit(solution)/shard_map/cdw,dwn->cwn/dot_general | solution.py:170
  151.0 1.9 %fusion.6 = bf16[16,128,256]{2,1,0:T(8,128)(2,1)} fusion(bf16[16,128,256]{2,1,0:T(8,128)(2,1)S(1)} %bitcast.83, f32[16,128,256]{2,1,0:T(8,128)S(1)} %copy-done.2, f32[16,256,128]{1,2,0:T(8,128)S(1)} %fusion.8, f32[16,128,256]{2,1,0:T(8,128)S(1)} %fusion.33, f32[16,128,256]{2,1,0:T(8,128)S(1)} %fusion.32, f32[16,128,256]{2,1,0:T(8,128)S(1)} %fusion.31, ...), kind=kOutput, calls=%fused_computation.10 | convolution fusion | flops 139460608 | bytes 14158848 | tf_op jit(solution)/shard_map/cij,cjw->ciw/dot_general | solution.py:151
  (138 shorter events, 31.3 us)
Async XLA Ops:
  0.0 26.7 %copy-start = (bf16[384,1280]{1,0:T(8,128)(2,1)S(1)}, bf16[384,1280]{1,0:T(8,128)(2,1)}, u32[]{:S(2)}) copy-start(bf16[384,1280]{1,0:T(8,128)(2,1)} %param.14) | copy-start | bytes 2949124
  0.0 8.6 %copy-start.9 = (bf16[256,128]{1,0:T(8,128)(2,1)S(1)}, bf16[256,128]{1,0:T(8,128)(2,1)}, u32[]{:S(2)}) copy-start(bf16[256,128]{1,0:T(8,128)(2,1)} %param.13) | copy-start | bytes 196612
  2.4 40.0 %collective-permute-start.5 = (f32[4]{0:T(128)S(1)}, f32[4]{0:T(128)S(1)}, u32[]{:S(2)}, u32[]{:S(2)}) collective-permute-start(f32[4]{0:T(128)S(1)} %slice_bitcast_fusion.8), channel_id=1, source_target_pairs={{0,32},{32,64},{64,96},{96,128},{128,160},{160,192},{192,224},{224... | collective-permute-start | bytes 56 | tf_op jit(solution)/shard_map/ppermute | solution.py:18
  4.2 38.2 %collective-permute-start.7 = (f32[4]{0:T(128)S(1)}, f32[4]{0:T(128)S(1)}, u32[]{:S(2)}, u32[]{:S(2)}) collective-permute-start(f32[4]{0:T(128)S(1)} %slice_bitcast_fusion.8), channel_id=1, source_target_pairs={{0,64},{32,96},{64,128},{96,160},{128,192},{160,224},{192,256},{22... | collective-permute-start | bytes 56 | tf_op jit(solution)/shard_map/ppermute | solution.py:18
  8.7 17.9 %collective-permute-start = (bf16[1,128]{1,0:T(2,128)(2,1)S(1)}, bf16[1,128]{1,0:T(2,128)(2,1)S(1)}, u32[]{:S(2)}, u32[]{:S(2)}) collective-permute-start(bf16[1,128]{1,0:T(2,128)(2,1)S(1)} %slice.92), channel_id=1, source_target_pairs={{0,4},{4,8},{8,12},{12,16},{16,20},{20,24},{24,28},{28,32},{32,36}... | collective-permute-start | bytes 776 | tf_op jit(solution)/shard_map/ppermute | solution.py:18
  12.2 3.1 %copy-start.17 = (s32[64]{0:T(128)S(1)}, s32[64]{0:T(128)}, u32[]{:S(2)}) copy-start(s32[64]{0:T(128)} %param.18) | copy-start | bytes 772
  12.2 3.5 %copy-start.18 = (s32[64]{0:T(128)S(1)}, s32[64]{0:T(128)}, u32[]{:S(2)}) copy-start(s32[64]{0:T(128)} %param.17) | copy-start | bytes 772
  12.2 4.2 %copy-start.16 = (f32[4,256]{1,0:T(4,128)S(1)}, f32[4,256]{1,0:T(4,128)}, u32[]{:S(2)}) copy-start(f32[4,256]{1,0:T(4,128)} %param.20) | copy-start | bytes 12292
  26.7 12.8 %copy-start.5 = (bf16[2048,128]{1,0:T(8,128)(2,1)S(1)}, bf16[2048,128]{1,0:T(8,128)(2,1)}, u32[]{:S(2)}) copy-start(bf16[2048,128]{1,0:T(8,128)(2,1)} %param.22) | copy-start | bytes 1572868
  26.7 12.8 %copy-start.6 = (bf16[2048,128]{1,0:T(8,128)(2,1)S(1)}, bf16[2048,128]{1,0:T(8,128)(2,1)}, u32[]{:S(2)}) copy-start(bf16[2048,128]{1,0:T(8,128)(2,1)} %param.21) | copy-start | bytes 1572868
  32.7 25.1 %all-to-all-start = ((bf16[128,8,256]{2,0,1:T(8,128)(2,1)}), bf16[128,8,256]{2,0,1:T(8,128)(2,1)S(1)}, u32[]{:S(2)}, u32[]{:S(2)}) async-start(bf16[128,8,256]{2,0,1:T(8,128)(2,1)} %fusion.14), calls=%async_computation | async-start | bytes 1048576 | tf_op jit(solution)/shard_map/all_to_all | solution.py:95
  42.4 18.8 %collective-permute-start.9 = (f32[4]{0:T(128)S(1)}, f32[4]{0:T(128)S(1)}, u32[]{:S(2)}, u32[]{:S(2)}) collective-permute-start(f32[4]{0:T(128)S(1)} %get-tuple-element.11), channel_id=1, source_target_pairs={{0,64},{32,96},{64,128},{96,160},{128,192},{160,224},{192,256},{22... | collective-permute-start | bytes 56 | tf_op jit(solution)/shard_map/ppermute | solution.py:18
  57.9 11.0 %collective-permute-start.1 = (bf16[262,256]{1,0:T(8,128)(2,1)S(1)}, bf16[262,256]{1,0:T(8,128)(2,1)S(1)}, u32[]{:S(2)}, u32[]{:S(2)}) collective-permute-start(bf16[262,256]{1,0:T(8,128)(2,1)S(1)} %pad_maximum_fusion), channel_id=1, source_target_pairs={{0,32},{32,64},{64,96},{96,128},{128,160},{160,192},{192,224},{224... | collective-permute-start | bytes 402440 | tf_op jit(solution)/shard_map/ppermute | solution.py:18
  59.9 8.9 %collective-permute-start.2 = (bf16[256,256]{1,0:T(8,128)(2,1)S(1)}, bf16[256,256]{1,0:T(8,128)(2,1)S(1)}, u32[]{:S(2)}, u32[]{:S(2)}) collective-permute-start(bf16[256,256]{1,0:T(8,128)(2,1)S(1)} %bitcast.104), channel_id=1, source_target_pairs={{32,0},{64,32},{96,64},{128,96},{160,128},{192,160},{224,192},{256... | collective-permute-start | bytes 393224 | tf_op jit(solution)/shard_map/ppermute | solution.py:18
  61.7 34.7 %collective-permute-start.11 = (f32[4]{0:T(128)}, f32[4]{0:T(128)}, u32[]{:S(2)}, u32[]{:S(2)}) collective-permute-start(f32[4]{0:T(128)} %get-tuple-element.13), channel_id=1, source_target_pairs={{0,128},{32,160},{64,192},{96,224},{128,256},{160,288},{192,320},{... | collective-permute-start | bytes 56 | tf_op jit(solution)/shard_map/ppermute | solution.py:18
  77.2 3.0 %copy-start.12 = (f32[1,256]{1,0:T(1,128)S(1)}, f32[1,256]{1,0:T(1,128)}, u32[]{:S(2)}) copy-start(f32[1,256]{1,0:T(1,128)} %get-tuple-element.21) | copy-start | bytes 3076
  84.0 34.7 %copy-start.1 = (bf16[16,128,128,4]{2,1,0,3:T(8,128)(2,1)S(1)}, bf16[16,128,128,4]{2,1,0,3:T(8,128)(2,1)}, u32[]{:S(2)}) copy-start(bf16[16,128,128,4]{2,1,0,3:T(8,128)(2,1)} %multiply_convert_fusion) | copy-start | bytes 6291460
  87.1 20.3 %collective-permute-start.4 = (bf16[4,64,128]{2,1,0:T(8,128)(2,1)S(1)}, bf16[4,64,128]{2,1,0:T(8,128)(2,1)S(1)}, u32[]{:S(2)}, u32[]{:S(2)}) collective-permute-start(bf16[4,64,128]{2,1,0:T(8,128)(2,1)S(1)} %bitcast.105), channel_id=1, source_target_pairs={{0,64},{32,96},{64,128},{96,160},{128,192},{160,224},{192,256},{22... | collective-permute-start | bytes 196616 | tf_op jit(solution)/shard_map/ppermute | solution.py:18
  94.3 13.1 %collective-permute-start.3 = (bf16[4,64,128]{2,1,0:T(8,128)(2,1)S(1)}, bf16[4,64,128]{2,1,0:T(8,128)(2,1)S(1)}, u32[]{:S(2)}, u32[]{:S(2)}) collective-permute-start(bf16[4,64,128]{2,1,0:T(8,128)(2,1)S(1)} %bitcast.106), channel_id=1, source_target_pairs={{0,32},{32,64},{64,96},{96,128},{128,160},{160,192},{192,224},{224... | collective-permute-start | bytes 196616 | tf_op jit(solution)/shard_map/ppermute | solution.py:18
  97.1 15.0 %collective-permute-start.13 = (f32[4]{0:T(128)S(1)}, f32[4]{0:T(128)S(1)}, u32[]{:S(2)}, u32[]{:S(2)}) collective-permute-start(f32[4]{0:T(128)S(1)} %get-tuple-element.9), channel_id=1, source_target_pairs={{0,256},{32,288},{64,320},{96,352},{128,384},{160,416},{192,448},{... | collective-permute-start | bytes 56 | tf_op jit(solution)/shard_map/ppermute | solution.py:18
  107.5 6.5 %collective-permute-start.6 = (bf16[4,64,128]{2,1,0:T(8,128)(2,1)S(1)}, bf16[4,64,128]{2,1,0:T(8,128)(2,1)S(1)}, u32[]{:S(2)}, u32[]{:S(2)}) collective-permute-start(bf16[4,64,128]{2,1,0:T(8,128)(2,1)S(1)} %fusion.66), channel_id=1, source_target_pairs={{0,64},{32,96},{64,128},{96,160},{128,192},{160,224},{192,256},{22... | collective-permute-start | bytes 196616 | tf_op jit(solution)/shard_map/ppermute | solution.py:18
  114.1 6.5 %collective-permute-start.8 = (bf16[4,64,128]{2,1,0:T(8,128)(2,1)S(1)}, bf16[4,64,128]{2,1,0:T(8,128)(2,1)S(1)}, u32[]{:S(2)}, u32[]{:S(2)}) collective-permute-start(bf16[4,64,128]{2,1,0:T(8,128)(2,1)S(1)} %fusion.109), channel_id=1, source_target_pairs={{0,128},{32,160},{64,192},{96,224},{128,256},{160,288},{192,320},{... | collective-permute-start | bytes 196616 | tf_op jit(solution)/shard_map/ppermute | solution.py:18
  120.7 12.5 %collective-permute-start.10 = (bf16[4,64,128]{2,1,0:T(8,128)(2,1)S(1)}, bf16[4,64,128]{2,1,0:T(8,128)(2,1)S(1)}, u32[]{:S(2)}, u32[]{:S(2)}) collective-permute-start(bf16[4,64,128]{2,1,0:T(8,128)(2,1)S(1)} %fusion.73), channel_id=1, source_target_pairs={{0,256},{32,288},{64,320},{96,352},{128,384},{160,416},{192,448},{... | collective-permute-start | bytes 196616 | tf_op jit(solution)/shard_map/ppermute | solution.py:18
  133.3 12.5 %collective-permute-start.12 = (bf16[4,64,128]{2,1,0:T(8,128)(2,1)S(1)}, bf16[4,64,128]{2,1,0:T(8,128)(2,1)S(1)}, u32[]{:S(2)}, u32[]{:S(2)}) collective-permute-start(bf16[4,64,128]{2,1,0:T(8,128)(2,1)S(1)} %fusion.108), channel_id=1, source_target_pairs={{0,512},{32,544},{64,576},{96,608},{128,640},{160,672},{192,704},{... | collective-permute-start | bytes 196616 | tf_op jit(solution)/shard_map/ppermute | solution.py:18
  (16 other events, 32.8 us)

commit v8 on v7

--- a/solution.py
+++ b/solution.py
@@ -74,6 +74,17 @@
     decay_log,
     skip_gain,
 ):
+    head_count = step_size.shape[0]
+    blocks = text_embed.shape[0] // SPAN
+    step_sizes = step_size.T.reshape(blocks, SPAN, head_count)
+    log_decay = -step_sizes * jnp.exp(decay_log)[None, None, :]
+    running = jnp.cumsum(log_decay, axis=1)
+    totals = running[:, -1, :]
+    through = jnp.cumsum(totals, axis=0)
+    device_total = through[-1]
+    first, spans = prefix_windows(device_total, "seq")
+    mel_frames, windows = lax.optimization_barrier((mel_frames, [w for _, w in spans]))
+    spans = [(width, w) for (width, _), w in zip(spans, windows)]
     tiles = mel_frames.shape[0] // 2
     channels = mel_frames.shape[1]
     enc_count = lax.axis_size("enc")
@@ -122,8 +133,6 @@
             summed_mix + padded[offset : offset + row_count].astype(jnp.float32) * mix_taps[offset]
         )
     mixed_in = jax.nn.silu(summed_mix).astype(jnp.bfloat16)
-    head_count = step_size.shape[0]
-    blocks = row_count // SPAN
     width = head_count * HDIM
     plain = mixed_in.reshape(blocks, SPAN, width)
     values = plain.astype(jnp.float32)
@@ -136,9 +145,6 @@
     def spread(per_head):
         return jnp.repeat(per_head, HDIM, axis=-1)
 
-    step_sizes = step_size.T.reshape(blocks, SPAN, head_count)
-    log_decay = -step_sizes * jnp.exp(decay_log)[None, None, :]
-    running = jnp.cumsum(log_decay, axis=1)
     lower_mask = (jnp.arange(SPAN)[:, None] >= jnp.arange(SPAN)[None, :])[None, :, :, None]
     gap_logs = running[:, :, None, :] - running[:, None, :, :]
     decay_table = jnp.where(lower_mask, jnp.exp(jnp.where(lower_mask, gap_logs, 0.0)), 0.0)
@@ -157,8 +163,6 @@
     block_states = jnp.einsum(
         "cjw,cjn->cwn", inputs * spread(tail_decay), b_all, precision=high_mode
     )
-    totals = running[:, -1, :]
-    through = jnp.cumsum(totals, axis=0)
     before_block = through - totals
     block_order = jnp.arange(blocks)
     earlier = (block_order[None, :] < block_order[:, None])[:, :, None]
@@ -168,12 +172,10 @@
         0.0,
     )
     local_starts = jnp.einsum("cdw,dwn->cwn", spread(weights), block_states, precision=highest)
-    device_total = through[-1]
     device_state = jnp.einsum(
         "dw,dwn->wn", spread(jnp.exp(device_total[None, :] - through)), block_states,
         precision=highest,
     )
-    first, spans = prefix_windows(device_total, "seq")
     incoming = prefix_state(
         device_total, device_state.reshape(head_count, HDIM, -1), first, spans, "seq"
     ).reshape(width, -1)

time: 154 us -> 177 us (1.15)
  starting transfers between devices: 80.7 us -> 93.1 us
  waiting for transfers between devices: 17.1 us -> 22.4 us
  local copies, waits for them, and re-layouts: 23.4 us -> 28.3 us
    ppermute x14, starting transfers between devices: 74.5 us -> 84.1 us  [from_behind(): return lax.ppermute(value, axis, pairs)]
    ppermute x14, waiting for transfers between devices: 6.04 us -> 10.7 us  [from_behind(): return lax.ppermute(value, axis, pairs)]
    all_to_all x1, starting transfers between devices: 6.21 us -> 9.01 us  [shards(): lax.all_to_all(projected, 'enc', split_axis=1, concat_axis=0, tiled=True)]
    concatenate x1, local copies, waits for them, and re-layouts: 1.34 us -> 3.49 us  [shards(): widened = jnp.concatenate([low_received[:edge], audio_rows, high], axis=0)]
  transfers between devices with their start and end apart: 15 -> 15, of which waited for: 5 -> 10; matrix products, arithmetic and copies ran while one was open for 28% -> 12% of each run, Pallas kernels for 0% -> 0%
where the time goes in v8:
time: 177 us; the launch traced here: 176 us
  starting transfers between devices  93.1 us (53%)
  local copies, waits for them, and re-layouts  28.3 us (16%)
  waiting for transfers between devices  22.4 us (13%)
  matrix products  18.7 us (11%)
  other arithmetic  12.9 us (7%)
    ppermute x14, starting transfers between devices, from_behind(): return lax.ppermute(value, axis, pairs)  84.1 us
    all_to_all x1, waiting for transfers between devices, shards(): lax.all_to_all(projected, 'enc', split_axis=1, concat_axis=0, tiled=True)  11.7 us
    ppermute x14, waiting for transfers between devices, from_behind(): return lax.ppermute(value, axis, pairs)  10.7 us
    all_to_all x1, starting transfers between devices, shards(): lax.all_to_all(projected, 'enc', split_axis=1, concat_axis=0, tiled=True)  9.01 us
    gather x1, local copies, waits for them, and re-layouts, shards(): jnp.take(widened, local_row, axis=0)  6.99 us
    dot_general x1, matrix products, shards(): jnp.einsum('cbk,tc->btk', projector, features, preferred_element_type=jnp...  6.02 us
    reshape x3, local copies, waits for them, and re-layouts, spread(): return jnp.repeat(per_head, HDIM, axis=-1)  5.6 us
  transfers between devices with their start and end apart: 15, of which 10 were waited for; matrix products, arithmetic and copies ran while one was open for 12% of the time, Pallas kernels for 0%

profile of v8, /device:TPU:6, one launch (start us, length us, event | category | flops | bytes accessed | tf_op | source)
XLA Modules:
  0.0 176.2 jit_solution(10827415186321209176)
XLA Ops:
  4.2 4.5 %collective-permute-start.1 = (f32[4]{0:T(128)S(1)}, f32[4]{0:T(128)S(1)}, u32[]{:S(2)}, u32[]{:S(2)}) collective-permute-start(f32[4]{0:T(128)S(1)} %slice_bitcast_fusion.8), channel_id=1, source_target_pairs={{0,64},{32,96},{64,128},{96,160},{128,192},{160,224},{192,256},{22... | collective-permute-start | bytes 56 | tf_op jit(solution)/shard_map/ppermute | solution.py:18
  11.7 4.3 %collective-permute-start.2 = (f32[4]{0:T(128)S(1)}, f32[4]{0:T(128)S(1)}, u32[]{:S(2)}, u32[]{:S(2)}) collective-permute-start(f32[4]{0:T(128)S(1)} %get-tuple-element.11), channel_id=1, source_target_pairs={{0,64},{32,96},{64,128},{96,160},{128,192},{160,224},{192,256},{22... | collective-permute-start | bytes 56 | tf_op jit(solution)/shard_map/ppermute | solution.py:18
  17.3 7.3 %collective-permute-start.3 = (f32[4]{0:T(128)S(1)}, f32[4]{0:T(128)S(1)}, u32[]{:S(2)}, u32[]{:S(2)}) collective-permute-start(f32[4]{0:T(128)S(1)} %add.179), channel_id=1, source_target_pairs={{0,128},{32,160},{64,192},{96,224},{128,256},{160,288},{192,320},{... | collective-permute-start | bytes 56 | tf_op jit(solution)/shard_map/ppermute | solution.py:18
  25.8 11.0 %collective-permute-start.4 = (f32[4]{0:T(128)S(1)}, f32[4]{0:T(128)S(1)}, u32[]{:S(2)}, u32[]{:S(2)}) collective-permute-start(f32[4]{0:T(128)S(1)} %add.180), channel_id=1, source_target_pairs={{0,256},{32,288},{64,320},{96,352},{128,384},{160,416},{192,448},{... | collective-permute-start | bytes 56 | tf_op jit(solution)/shard_map/ppermute | solution.py:18
  38.7 3.5 %collective-permute-start.5 = (bf16[1,128]{1,0:T(2,128)(2,1)S(1)}, bf16[1,128]{1,0:T(2,128)(2,1)S(1)}, u32[]{:S(2)}, u32[]{:S(2)}) collective-permute-start(bf16[1,128]{1,0:T(2,128)(2,1)S(1)} %slice.94), channel_id=1, source_target_pairs={{0,4},{4,8},{8,12},{12,16},{16,20},{20,24},{24,28},{28,32},{32,36}... | collective-permute-start | bytes 776 | tf_op jit(solution)/shard_map/ppermute | solution.py:18
  43.6 6.0 %fusion.14 = bf16[128,8,256]{2,0,1:T(8,128)(2,1)} fusion(bf16[1280,8,256]{2,1,0:T(8,128)(2,1)} %param.16, bf16[384,1280]{1,0:T(8,128)(2,1)S(1)} %copy-done, f32[1280]{0:T(1024)S(1)} %copy-done.31, bf16[128,256]{1,0:T(8,128)(2,1)S(1)} %reshape.203, bf16[128,128]{1,0:T(8,128)(2,1)S(1)} %maximum_select_fusion.1), kind=kOutput, calls=%fused_computation.21 | convolution fusion | flops 808189952 | bytes 6853632 | tf_op jit(solution)/shard_map/cbk,tc->btk/dot_general | solution.py:103
  49.6 9.0 %all-to-all-start = ((bf16[128,8,256]{2,0,1:T(8,128)(2,1)}), bf16[128,8,256]{2,0,1:T(8,128)(2,1)}, u32[]{:S(2)}, u32[]{:S(2)}) async-start(bf16[128,8,256]{2,0,1:T(8,128)(2,1)} %fusion.14), calls=%async_computation | async-start | bytes 1048576 | tf_op jit(solution)/shard_map/all_to_all | solution.py:106
  60.4 2.4 %multiply_convert_fusion = bf16[16,128,128,4]{2,1,0,3:T(8,128)(2,1)} fusion(f32[16,128,4]{1,0,2:T(8,128)S(1)} %bitcast.97, f32[16,128,128]{2,1,0:T(8,128)S(1)} %fusion.112, f32[16,128,4]{1,0,2:T(8,128)S(1)} %copy.75, pred[128,128]{1,0:T(8,128)(4,1)S(1)} %iota_compare_fusion.1), kind=kLoop, calls=%fused_computation.3 | loop fusion | flops 6291456 | bytes 3227648 | tf_op jit(solution)/shard_map/convert_element_type | solution.py:152
  62.8 11.7 %all-to-all-done = bf16[128,8,256]{2,0,1:T(8,128)(2,1)} async-done(((bf16[128,8,256]{2,0,1:T(8,128)(2,1)}), bf16[128,8,256]{2,0,1:T(8,128)(2,1)}, u32[]{:S(2)}, u32[]{:S(2)}) %all-to-all-start) | async-done | bytes 524320 | tf_op jit(solution)/shard_map/all_to_all | solution.py:106
  80.9 1.8 %copy.94 = f32[16,128,256]{2,1,0:T(8,128)} copy(f32[16,128,256]{1,2,0:T(8,128)S(1)} %bitcast.85) | data formatting | bytes 4194304 | tf_op jit(solution)/shard_map/reshape | solution.py:146
  85.1 1.9 %copy.85 = f32[16,128,256]{2,1,0:T(8,128)} copy(f32[16,128,256]{1,2,0:T(8,128)S(1)} %bitcast.86) | data formatting | bytes 4194304 | tf_op jit(solution)/shard_map/reshape | solution.py:146
  87.2 1.9 %copy.82 = f32[16,128,256]{2,1,0:T(8,128)} copy(f32[16,128,256]{1,2,0:T(8,128)S(1)} %bitcast.87) | data formatting | bytes 4194304 | tf_op jit(solution)/shard_map/reshape | solution.py:146
  90.8 3.5 %concatenate.18 = bf16[1539,256]{1,0:T(8,128)(2,1)S(1)} concatenate(bf16[259,256]{1,0:T(8,128)(2,1)S(1)} %bitcast.98, bf16[1024,256]{1,0:T(8,128)(2,1)} %bitcast.10, bf16[256,256]{1,0:T(8,128)(2,1)S(1)} %collective-permute-done.7), dimensions={0} | concatenate | bytes 1575936 | tf_op jit(solution)/shard_map/concatenate | solution.py:115
  94.3 7.0 %gather_fusion = bf16[2051,256]{1,0:T(8,128)(2,1)S(1)} fusion(bf16[1539,256]{1,0:T(8,128)(2,1)S(1)} %concatenate.18, s32[3072]{0:T(1024)S(1)} %pad_clamp_fusion), kind=kCustom, calls=%fused_computation | custom fusion | bytes 2108428 | tf_op jit(solution)/shard_map/jit(_take)/gather | solution.py:129
  101.4 3.0 %maximum_select_fusion = bf16[2051,256]{1,0:T(8,128)(2,1)S(1)} fusion(bf16[2048,256]{1,0:T(8,128)(2,1)} %param.19, bf16[3,256]{1,0:T(4,128)(2,1)S(1)} %slice.99, bf16[2051,256]{1,0:T(8,128)(2,1)S(1)} %gather_fusion, pred[2051]{0:T(1024)(128)(4,1)S(1)} %copy-done.18, pred[2051]{0:T(1024)(128)(4,1)S(1)} %copy-done.19), kind=kLoop, calls=%fused_computation.22 | loop fusion | flops 3150336 | bytes 3154438 | tf_op jit(solution)/shard_map/jit(_where)/select_n | solution.py:129
  108.2 3.0 %fusion.10 = f32[256,1,128]{2,1,0:T(1,128)S(1)} fusion(f32[16,256,1]{0,2,1:T(1,128)S(1)} %bitcast.94, f32[16,256,128]{2,1,0:T(8,128)S(1)} %fusion.3), kind=kOutput, calls=%fused_computation.17 | convolution fusion | flops 6291456 | bytes 2244608 | tf_op jit(solution)/shard_map/dw,dwn->wn/dot_general | solution.py:175
  111.3 7.6 %collective-permute-start.9 = (bf16[4,64,128]{2,1,0:T(8,128)(2,1)S(1)}, bf16[4,64,128]{2,1,0:T(8,128)(2,1)S(1)}, u32[]{:S(2)}, u32[]{:S(2)}) collective-permute-start(bf16[4,64,128]{2,1,0:T(8,128)(2,1)S(1)} %bitcast.101), channel_id=1, source_target_pairs={{0,64},{32,96},{64,128},{96,160},{128,192},{160,224},{192,256},{22... | collective-permute-start | bytes 196616 | tf_op jit(solution)/shard_map/ppermute | solution.py:18
  118.8 2.4 %collective-permute-start.8 = (bf16[4,64,128]{2,1,0:T(8,128)(2,1)S(1)}, bf16[4,64,128]{2,1,0:T(8,128)(2,1)S(1)}, u32[]{:S(2)}, u32[]{:S(2)}) collective-permute-start(bf16[4,64,128]{2,1,0:T(8,128)(2,1)S(1)} %bitcast.102), channel_id=1, source_target_pairs={{0,32},{32,64},{64,96},{96,128},{128,160},{160,192},{192,224},{224... | collective-permute-start | bytes 196616 | tf_op jit(solution)/shard_map/ppermute | solution.py:18
  122.1 6.6 %collective-permute-start.10 = (bf16[4,64,128]{2,1,0:T(8,128)(2,1)S(1)}, bf16[4,64,128]{2,1,0:T(8,128)(2,1)S(1)}, u32[]{:S(2)}, u32[]{:S(2)}) collective-permute-start(bf16[4,64,128]{2,1,0:T(8,128)(2,1)S(1)} %fusion.66), channel_id=1, source_target_pairs={{0,64},{32,96},{64,128},{96,160},{128,192},{160,224},{192,256},{22... | collective-permute-start | bytes 196616 | tf_op jit(solution)/shard_map/ppermute | solution.py:18
  130.7 7.5 %collective-permute-start.11 = (bf16[4,64,128]{2,1,0:T(8,128)(2,1)S(1)}, bf16[4,64,128]{2,1,0:T(8,128)(2,1)S(1)}, u32[]{:S(2)}, u32[]{:S(2)}) collective-permute-start(bf16[4,64,128]{2,1,0:T(8,128)(2,1)S(1)} %fusion.109), channel_id=1, source_target_pairs={{0,128},{32,160},{64,192},{96,224},{128,256},{160,288},{192,320},{... | collective-permute-start | bytes 196616 | tf_op jit(solution)/shard_map/ppermute | solution.py:18
  140.3 10.0 %collective-permute-start.12 = (bf16[4,64,128]{2,1,0:T(8,128)(2,1)S(1)}, bf16[4,64,128]{2,1,0:T(8,128)(2,1)S(1)}, u32[]{:S(2)}, u32[]{:S(2)}) collective-permute-start(bf16[4,64,128]{2,1,0:T(8,128)(2,1)S(1)} %fusion.73), channel_id=1, source_target_pairs={{0,256},{32,288},{64,320},{96,352},{128,384},{160,416},{192,448},{... | collective-permute-start | bytes 196616 | tf_op jit(solution)/shard_map/ppermute | solution.py:18
  152.3 15.0 %collective-permute-start.13 = (bf16[4,64,128]{2,1,0:T(8,128)(2,1)S(1)}, bf16[4,64,128]{2,1,0:T(8,128)(2,1)S(1)}, u32[]{:S(2)}, u32[]{:S(2)}) collective-permute-start(bf16[4,64,128]{2,1,0:T(8,128)(2,1)S(1)} %fusion.108), channel_id=1, source_target_pairs={{0,512},{32,544},{64,576},{96,608},{128,640},{160,672},{192,704},{... | collective-permute-start | bytes 196616 | tf_op jit(solution)/shard_map/ppermute | solution.py:18
  169.4 3.3 %bitcast_add_fusion = f32[16,256,128]{2,0,1:T(8,128)S(1)} fusion(f32[256,128]{1,0:T(8,128)S(1)} %bitcast.92, f32[16,256]{0,1:T(8,128)S(1)} %bitcast.93, f32[16,16,256]{1,0,2:T(8,128)S(1)} %bitcast.84, f32[16,256,128]{2,1,0:T(8,128)S(1)} %fusion.3), kind=kOutput, calls=%fused_computation.13 | convolution fusion | flops 101711872 | bytes 4603904 | tf_op jit(solution)/shard_map/cdw,dwn->cwn/dot_general | solution.py:174
  174.3 1.9 %fusion.6 = bf16[16,128,256]{2,1,0:T(8,128)(2,1)} fusion(bf16[16,128,256]{2,1,0:T(8,128)(2,1)S(1)} %bitcast.83, f32[16,128,256]{2,1,0:T(8,128)S(1)} %copy-done.2, f32[16,256,128]{1,2,0:T(8,128)S(1)} %fusion.8, f32[16,128,256]{2,1,0:T(8,128)S(1)} %fusion.33, f32[16,128,256]{2,1,0:T(8,128)S(1)} %fusion.32, f32[16,128,256]{2,1,0:T(8,128)S(1)} %fusion.31, ...), kind=kOutput, calls=%fused_computation.10 | convolution fusion | flops 139460608 | bytes 14158848 | tf_op jit(solution)/shard_map/cij,cjw->ciw/dot_general | solution.py:157
  (166 shorter events, 39.4 us)
Async XLA Ops:
  0.0 43.6 %copy-start = (bf16[384,1280]{1,0:T(8,128)(2,1)S(1)}, bf16[384,1280]{1,0:T(8,128)(2,1)}, u32[]{:S(2)}) copy-start(bf16[384,1280]{1,0:T(8,128)(2,1)} %param.14) | copy-start | bytes 2949124
  0.0 38.7 %copy-start.15 = (bf16[256,128]{1,0:T(8,128)(2,1)S(1)}, bf16[256,128]{1,0:T(8,128)(2,1)}, u32[]{:S(2)}) copy-start(bf16[256,128]{1,0:T(8,128)(2,1)} %param.13) | copy-start | bytes 196612
  1.4 42.2 %copy-start.31 = (f32[1280]{0:T(1024)S(1)}, f32[1280]{0:T(1024)}, u32[]{:S(2)}) copy-start(f32[1280]{0:T(1024)} %param.15) | copy-start | bytes 15364
  2.5 8.6 %collective-permute-start = (f32[4]{0:T(128)S(1)}, f32[4]{0:T(128)S(1)}, u32[]{:S(2)}, u32[]{:S(2)}) collective-permute-start(f32[4]{0:T(128)S(1)} %slice_bitcast_fusion.8), channel_id=1, source_target_pairs={{0,32},{32,64},{64,96},{96,128},{128,160},{160,192},{192,224},{224... | collective-permute-start | bytes 56 | tf_op jit(solution)/shard_map/ppermute | solution.py:18
  4.2 6.9 %collective-permute-start.1 = (f32[4]{0:T(128)S(1)}, f32[4]{0:T(128)S(1)}, u32[]{:S(2)}, u32[]{:S(2)}) collective-permute-start(f32[4]{0:T(128)S(1)} %slice_bitcast_fusion.8), channel_id=1, source_target_pairs={{0,64},{32,96},{64,128},{96,160},{128,192},{160,224},{192,256},{22... | collective-permute-start | bytes 56 | tf_op jit(solution)/shard_map/ppermute | solution.py:18
  10.3 27.8 %copy-start.12 = (s32[2051]{0:T(1024)}, s32[2051]{0:T(1024)S(1)}, u32[]{:S(2)}) copy-start(s32[2051]{0:T(1024)S(1)} %get-tuple-element.16) | copy-start | bytes 24616
  10.3 27.8 %copy-start.14 = (s32[2051]{0:T(1024)}, s32[2051]{0:T(1024)S(1)}, u32[]{:S(2)}) copy-start(s32[2051]{0:T(1024)S(1)} %get-tuple-element.17) | copy-start | bytes 24616
  10.3 31.9 %copy-start.10 = (s32[2051]{0:T(1024)}, s32[2051]{0:T(1024)S(1)}, u32[]{:S(2)}) copy-start(s32[2051]{0:T(1024)S(1)} %get-tuple-element.15) | copy-start | bytes 24616
  11.7 30.5 %copy-start.29 = (f32[4]{0:T(128)}, f32[4]{0:T(128)S(1)}, u32[]{:S(2)}) copy-start(f32[4]{0:T(128)S(1)} %get-tuple-element.11) | copy-start | bytes 52
  11.7 5.6 %collective-permute-start.2 = (f32[4]{0:T(128)S(1)}, f32[4]{0:T(128)S(1)}, u32[]{:S(2)}, u32[]{:S(2)}) collective-permute-start(f32[4]{0:T(128)S(1)} %get-tuple-element.11), channel_id=1, source_target_pairs={{0,64},{32,96},{64,128},{96,160},{128,192},{160,224},{192,256},{22... | collective-permute-start | bytes 56 | tf_op jit(solution)/shard_map/ppermute | solution.py:18
  17.2 21.5 %copy-start.32 = (f32[4]{0:T(128)}, f32[4]{0:T(128)S(1)}, u32[]{:S(2)}) copy-start(f32[4]{0:T(128)S(1)} %add.179) | copy-start | bytes 52
  17.3 8.6 %collective-permute-start.3 = (f32[4]{0:T(128)S(1)}, f32[4]{0:T(128)S(1)}, u32[]{:S(2)}, u32[]{:S(2)}) collective-permute-start(f32[4]{0:T(128)S(1)} %add.179), channel_id=1, source_target_pairs={{0,128},{32,160},{64,192},{96,224},{128,256},{160,288},{192,320},{... | collective-permute-start | bytes 56 | tf_op jit(solution)/shard_map/ppermute | solution.py:18
  25.8 12.3 %collective-permute-start.4 = (f32[4]{0:T(128)S(1)}, f32[4]{0:T(128)S(1)}, u32[]{:S(2)}, u32[]{:S(2)}) collective-permute-start(f32[4]{0:T(128)S(1)} %add.180), channel_id=1, source_target_pairs={{0,256},{32,288},{64,320},{96,352},{128,384},{160,416},{192,448},{... | collective-permute-start | bytes 56 | tf_op jit(solution)/shard_map/ppermute | solution.py:18
  38.7 4.8 %collective-permute-start.5 = (bf16[1,128]{1,0:T(2,128)(2,1)S(1)}, bf16[1,128]{1,0:T(2,128)(2,1)S(1)}, u32[]{:S(2)}, u32[]{:S(2)}) collective-permute-start(bf16[1,128]{1,0:T(2,128)(2,1)S(1)} %slice.94), channel_id=1, source_target_pairs={{0,4},{4,8},{8,12},{12,16},{16,20},{20,24},{24,28},{28,32},{32,36}... | collective-permute-start | bytes 776 | tf_op jit(solution)/shard_map/ppermute | solution.py:18
  49.6 24.8 %all-to-all-start = ((bf16[128,8,256]{2,0,1:T(8,128)(2,1)}), bf16[128,8,256]{2,0,1:T(8,128)(2,1)}, u32[]{:S(2)}, u32[]{:S(2)}) async-start(bf16[128,8,256]{2,0,1:T(8,128)(2,1)} %fusion.14), calls=%async_computation | async-start | bytes 1048576 | tf_op jit(solution)/shard_map/all_to_all | solution.py:106
  75.4 15.4 %collective-permute-start.6 = (bf16[262,256]{1,0:T(8,128)(2,1)S(1)}, bf16[262,256]{1,0:T(8,128)(2,1)S(1)}, u32[]{:S(2)}, u32[]{:S(2)}) collective-permute-start(bf16[262,256]{1,0:T(8,128)(2,1)S(1)} %pad_maximum_fusion), channel_id=1, source_target_pairs={{0,32},{32,64},{64,96},{96,128},{128,160},{160,192},{192,224},{224... | collective-permute-start | bytes 402440 | tf_op jit(solution)/shard_map/ppermute | solution.py:18
  78.2 12.6 %collective-permute-start.7 = (bf16[256,256]{1,0:T(8,128)(2,1)}, bf16[256,256]{1,0:T(8,128)(2,1)S(1)}, u32[]{:S(2)}, u32[]{:S(2)}) collective-permute-start(bf16[256,256]{1,0:T(8,128)(2,1)} %bitcast.12), channel_id=1, source_target_pairs={{32,0},{64,32},{96,64},{128,96},{160,128},{192,160},{224,192},{256... | collective-permute-start | bytes 393224 | tf_op jit(solution)/shard_map/ppermute | solution.py:18
  108.2 30.1 %copy-start.1 = (bf16[16,128,128,4]{2,1,0,3:T(8,128)(2,1)S(1)}, bf16[16,128,128,4]{2,1,0,3:T(8,128)(2,1)}, u32[]{:S(2)}) copy-start(bf16[16,128,128,4]{2,1,0,3:T(8,128)(2,1)} %multiply_convert_fusion) | copy-start | bytes 6291460
  111.3 9.9 %collective-permute-start.9 = (bf16[4,64,128]{2,1,0:T(8,128)(2,1)S(1)}, bf16[4,64,128]{2,1,0:T(8,128)(2,1)S(1)}, u32[]{:S(2)}, u32[]{:S(2)}) collective-permute-start(bf16[4,64,128]{2,1,0:T(8,128)(2,1)S(1)} %bitcast.101), channel_id=1, source_target_pairs={{0,64},{32,96},{64,128},{96,160},{128,192},{160,224},{192,256},{22... | collective-permute-start | bytes 196616 | tf_op jit(solution)/shard_map/ppermute | solution.py:18
  118.8 3.2 %collective-permute-start.8 = (bf16[4,64,128]{2,1,0:T(8,128)(2,1)S(1)}, bf16[4,64,128]{2,1,0:T(8,128)(2,1)S(1)}, u32[]{:S(2)}, u32[]{:S(2)}) collective-permute-start(bf16[4,64,128]{2,1,0:T(8,128)(2,1)S(1)} %bitcast.102), channel_id=1, source_target_pairs={{0,32},{32,64},{64,96},{96,128},{128,160},{160,192},{192,224},{224... | collective-permute-start | bytes 196616 | tf_op jit(solution)/shard_map/ppermute | solution.py:18
  122.1 8.5 %collective-permute-start.10 = (bf16[4,64,128]{2,1,0:T(8,128)(2,1)S(1)}, bf16[4,64,128]{2,1,0:T(8,128)(2,1)S(1)}, u32[]{:S(2)}, u32[]{:S(2)}) collective-permute-start(bf16[4,64,128]{2,1,0:T(8,128)(2,1)S(1)} %fusion.66), channel_id=1, source_target_pairs={{0,64},{32,96},{64,128},{96,160},{128,192},{160,224},{192,256},{22... | collective-permute-start | bytes 196616 | tf_op jit(solution)/shard_map/ppermute | solution.py:18
  130.7 9.4 %collective-permute-start.11 = (bf16[4,64,128]{2,1,0:T(8,128)(2,1)S(1)}, bf16[4,64,128]{2,1,0:T(8,128)(2,1)S(1)}, u32[]{:S(2)}, u32[]{:S(2)}) collective-permute-start(bf16[4,64,128]{2,1,0:T(8,128)(2,1)S(1)} %fusion.109), channel_id=1, source_target_pairs={{0,128},{32,160},{64,192},{96,224},{128,256},{160,288},{192,320},{... | collective-permute-start | bytes 196616 | tf_op jit(solution)/shard_map/ppermute | solution.py:18
  140.3 11.9 %collective-permute-start.12 = (bf16[4,64,128]{2,1,0:T(8,128)(2,1)S(1)}, bf16[4,64,128]{2,1,0:T(8,128)(2,1)S(1)}, u32[]{:S(2)}, u32[]{:S(2)}) collective-permute-start(bf16[4,64,128]{2,1,0:T(8,128)(2,1)S(1)} %fusion.73), channel_id=1, source_target_pairs={{0,256},{32,288},{64,320},{96,352},{128,384},{160,416},{192,448},{... | collective-permute-start | bytes 196616 | tf_op jit(solution)/shard_map/ppermute | solution.py:18
  152.3 16.7 %collective-permute-start.13 = (bf16[4,64,128]{2,1,0:T(8,128)(2,1)S(1)}, bf16[4,64,128]{2,1,0:T(8,128)(2,1)S(1)}, u32[]{:S(2)}, u32[]{:S(2)}) collective-permute-start(bf16[4,64,128]{2,1,0:T(8,128)(2,1)S(1)} %fusion.108), channel_id=1, source_target_pairs={{0,512},{32,544},{64,576},{96,608},{128,640},{160,672},{192,704},{... | collective-permute-start | bytes 196616 | tf_op jit(solution)/shard_map/ppermute | solution.py:18
  (28 other events, 232.5 us)
